TPU v7x, 512 devices: a whole 4x8x8 slice. The times are simulated.
512 devices in a mesh: island: 64 (over z, x, y_hi), fsdp: 8 (over y_lo, core).
Axes of the slice: x: 4, y: 8 (y_hi: 2, y_lo: 4; y = y_hi * 4 + y_lo), z: 8, core: 2. Of those that a mesh axis runs over, the one named last changes fastest.
Arguments:
- hidden: bfloat16 [64, 1024, 8192], P('island', 'fsdp'), may hold values from -6 to 6
- gain: bfloat16 [8192], P('fsdp'), may hold values from 0.5 to 1.5
- doc_ids: int32 [64, 1024], P('island', 'fsdp'), may hold values from 0 to 7, never falling along the last dimension, each value on 1 to 256 neighbouring positions
- cotangent: bfloat16 [64, 1024, 512], P('island', 'fsdp'), may hold values from -0.1796875 to 0.1796875
- pseudo_grad: bfloat16 [64, 8192, 512], P('island', 'fsdp'), may hold values from -0.75 to 0.75
- outer_weight: float32 [8192, 512], P(('fsdp', 'island')), may hold values from -0.0625 to 0.0625
- momentum: float32 [8192, 512], P(('fsdp', 'island')), may hold values from -0.0625 to 0.0625
Outputs:
- keys: bfloat16 [64, 1024, 512], P('island', 'fsdp')
- grad_weight: bfloat16 [64, 8192, 512], P('island', 'fsdp')
- grad_gain: float32 [64, 8192], P('island', 'fsdp')
- new_outer: float32 [8192, 512], P(('fsdp', 'island'))
- new_momentum: float32 [8192, 512], P(('fsdp', 'island'))
Inputs may be any that keep to these rules, and one draw needn't show every extreme that they name: `doc_ids`: document numbers never fall along a replica's sequence; every document holds 1 to 256 tokens, and one holds exactly 256.
All inputs are finite; a program needn't handle non-finite values.
Results may differ from a plain program's by a relative error of at most 0.014.
Values may be sent and summed in bfloat16 or wider, within the bound.
No kernel may reach another device: no remote copies, remote signals or barrier semaphores. Data moves between devices by JAX's collectives and lax.ppermute only.
A program may use at most 128 MiB of HBM per device.

v0:
```python
import math

import jax
import jax.numpy as jnp
from jax import lax
from jax.sharding import PartitionSpec as P

HEAD = 128
DOCS = 8


learn_rate = 0.7
momentum_rate = 0.9
norm_eps = 1e-05
rope_base = 500000.0
far_index = 1 << 30


def angles_for(positions, head_width):
    half_width = head_width // 2
    frequency = jnp.exp(
        jnp.arange(half_width, dtype=jnp.float32) * (-2.0 * math.log(rope_base) / head_width)
    )
    phases = positions[:, None] * frequency[None, :]
    return (jnp.cos(phases), jnp.sin(phases))


def rotate(values, cosine, sine_part, sign):
    rows = values.shape[0]
    half_width = cosine.shape[1]
    shaped = values.reshape(rows, -1, 2 * half_width)
    leading = shaped[:, :, :half_width]
    second = shaped[:, :, half_width:]
    cos_b = cosine[:, None, :]
    sin_b = sine_part[:, None, :] * sign
    joined = jnp.concatenate(
        [leading * cos_b - second * sin_b, second * cos_b + leading * sin_b], axis=2
    )
    return joined.reshape(rows, -1)


def body(hidden, gain, doc_ids, cotangent, pseudo_grad, outer_weight, momentum):
    islands = lax.axis_size("island")
    fsdp_ways = lax.axis_size("fsdp")
    summed = lax.psum_scatter(
        pseudo_grad[0].astype(jnp.float32), "island", scatter_dimension=0, tiled=True
    )
    mean_delta = summed / islands
    new_momentum = momentum_rate * momentum + mean_delta
    new_outer = outer_weight - learn_rate * (mean_delta + momentum_rate * new_momentum)
    fresh_rows = new_outer.astype(jnp.bfloat16)
    weight_shard = lax.all_gather(fresh_rows, "island", axis=0, tiled=True)
    tok_rows = hidden.shape[1]
    indices = lax.axis_index("fsdp") * tok_rows + jnp.arange(tok_rows, dtype=jnp.int32)
    documents = jnp.arange(DOCS, dtype=jnp.int32)
    in_document = doc_ids[0][:, None] == documents[None, :]
    local_first = jnp.min(jnp.where(in_document, indices[:, None], far_index), axis=0)
    starts = lax.pmin(local_first, "fsdp")
    doc_start = jnp.sum(jnp.where(in_document, starts[None, :], 0), axis=1)
    positions = (indices - doc_start).astype(jnp.float32)
    cosine, sine_part = angles_for(positions, HEAD)
    hidden_f = hidden[0].astype(jnp.float32)
    row_scale = lax.rsqrt(jnp.mean(hidden_f * hidden_f, axis=1, keepdims=True) + norm_eps)
    back_grad = rotate(cotangent[0].astype(jnp.float32), cosine, sine_part, -1.0).astype(
        jnp.bfloat16
    )
    columns = lax.all_to_all(hidden[0], "fsdp", split_axis=1, concat_axis=0, tiled=True)
    all_scales = lax.all_gather(row_scale, "fsdp", axis=0, tiled=True)
    normed_cols = columns.astype(jnp.float32) * all_scales
    act_cols = (normed_cols * gain.astype(jnp.float32)[None, :]).astype(jnp.bfloat16)
    weight_full, gain_full = (
        lax.all_gather(weight_shard, "fsdp", axis=0, tiled=True),
        lax.all_gather(gain, "fsdp", axis=0, tiled=True),
    )
    activations = (hidden_f * row_scale * gain_full.astype(jnp.float32)[None, :]).astype(
        jnp.bfloat16
    )
    projected = jnp.dot(activations, weight_full, preferred_element_type=jnp.float32)
    all_back = lax.all_gather(back_grad, "fsdp", axis=0, tiled=True)
    hidden_grad = lax.dot_general(
        all_back, weight_shard, (((1,), (1,)), ((), ())), preferred_element_type=jnp.float32
    )
    grad_gain = jnp.sum(hidden_grad * normed_cols, axis=0)
    grad_weight = jnp.zeros((act_cols.shape[1], all_back.shape[1]), jnp.float32)
    for block in range(fsdp_ways):
        act_block = act_cols[block * tok_rows : (block + 1) * tok_rows]
        back_block = all_back[block * tok_rows : (block + 1) * tok_rows]
        part = lax.dot_general(
            act_block, back_block, (((0,), (0,)), ((), ())), preferred_element_type=jnp.float32
        )
        grad_weight = grad_weight + part.astype(jnp.bfloat16).astype(jnp.float32)
    rotated = rotate(projected, cosine, sine_part, 1.0).astype(jnp.bfloat16)
    return (
        rotated[None],
        grad_weight.astype(jnp.bfloat16)[None],
        grad_gain[None],
        new_outer,
        new_momentum,
    )


def solution(mesh):
    placed = (
        P("island", "fsdp", None),
        P("fsdp"),
        P("island", "fsdp"),
        P("island", "fsdp", None),
        P("island", "fsdp", None),
        P(("fsdp", "island"), None),
        P(("fsdp", "island"), None),
    )
    return jax.shard_map(
        body,
        mesh=mesh,
        in_specs=placed,
        out_specs=(
            P("island", "fsdp", None),
            P("island", "fsdp", None),
            P("island", "fsdp"),
            P(("fsdp", "island"), None),
            P(("fsdp", "island"), None),
        ),
        check_vma=False,
    )
```

profile of v0, /device:TPU:6, one launch (start us, length us, event | category | flops | bytes accessed | tf_op | source)
XLA Modules:
  0.0 793.6 jit_solution(5089084613000666658)
XLA Ops:
  7.2 2.9 bitcast_convert_fusion
  10.2 444.6 %reduce-scatter.2.cloned.1.call-done = f32[16,512]{1,0:T(8,128)} async-done(((f32[1024,512]{1,0:T(8,128)}), f32[16,512]{1,0:T(8,128)}) %reduce-scatter.2.cloned.1.call-update) | async-done | bytes 32784 | tf_op jit(solution)/shard_map/reduce_scatter | solution.py:45
  454.7 1.4 fusion.26
  456.2 136.4 %all-gather.6.cloned.1.call-done = bf16[1024,512]{1,0:T(8,128)(2,1)} async-done(((bf16[16,512]{1,0:T(8,128)(2,1)}), bf16[1024,512]{1,0:T(8,128)(2,1)}) %all-gather.6.cloned.1.call-update) | async-done | bytes 1048592 | tf_op jit(solution)/shard_map/all_gather | solution.py:52
  592.6 1.4 copy.24
  594.1 2.5 copy.21
  596.5 4.5 all-to-all-start
  601.2 82.5 %pmin.7 = s32[8]{0:T(128)S(1)} all-reduce(s32[8]{0:T(128)S(1)} %select_reduce_fusion.1), channel_id=1, replica_groups=mesh['island'=64,'fsdp'=8] {'fsdp'}, use_global_device_ids=true, to_apply=%region_3.4 | all-reduce | flops 8 | bytes 64 | tf_op jit(solution)/shard_map/pmin | solution.py:58
  683.7 13.1 %all_gather.15 = bf16[8192]{0:T(1024)(128)(2,1)S(1)} all-gather(bf16[1024]{0:T(1024)(128)(2,1)S(1)} %copy-done.6), channel_id=1, replica_groups=mesh['island'=64,'fsdp'=8] {'fsdp'}, dimensions={0}, use_global_device_ids=true | all-gather | bytes 18432 | tf_op jit(solution)/shard_map/all_gather | solution.py:73
  697.0 0.5 fusion
  697.7 20.5 %all-gather.8.cloned.1.call-done = bf16[8192,512]{1,0:T(8,128)(2,1)} async-done(((bf16[1024,512]{1,0:T(8,128)(2,1)}), bf16[8192,512]{1,0:T(8,128)(2,1)}) %all-gather.8.cloned.1.call-update) | async-done | bytes 8388624 | tf_op jit(solution)/shard_map/all_gather | solution.py:72
  718.2 11.3 %copy.20 = bf16[512,8192]{1,0:T(8,128)(2,1)} copy(bf16[512,8192]{0,1:T(8,128)(2,1)} %bitcast.33) | data formatting | bytes 16777216 | tf_op jit(solution)/shard_map/dot_general | solution.py:78
  729.5 5.8 fusion.4
  735.4 0.7 pad_maximum_fusion.1
  736.1 18.0 %all-gather.1 = f32[8,1,128]{2,1,0:T(1,128)S(1)} all-gather(f32[1,1,128]{2,1,0:T(1,128)S(1)} %get-tuple-element.32), channel_id=2, replica_groups=mesh['island'=64,'fsdp'=8] {'fsdp'}, dimensions={0}, use_global_device_ids=true | all-gather | bytes 4608 | tf_op jit(solution)/shard_map/all_gather | solution.py:68
  754.1 2.1 multiply_convert_fusion
  756.3 0.8 copy.23
  757.0 18.7 %all-gather.10.cloned.1.call-done = bf16[1024,512]{0,1:T(8,128)(2,1)} async-done(((bf16[128,512]{0,1:T(8,128)(2,1)}), bf16[1024,512]{0,1:T(8,128)(2,1)}) %all-gather.10.cloned.1.call-update) | async-done | bytes 1048592 | tf_op jit(solution)/shard_map/all_gather | solution.py:79
  775.7 1.4 convolution_convert_fusion.6
  777.2 1.4 convolution_convert_fusion.5
  779.0 0.5 convolution_convert_fusion.3
  779.5 0.5 convolution_convert_fusion.2
  780.9 3.9 multiply_reduce_fusion
  784.9 2.2 fusion.8
  (40 shorter events, 2.3 us)
Async XLA Ops:
  7.2 447.6 %copy-start.4 = (f32[16,512]{1,0:T(8,128)S(1)}, f32[16,512]{1,0:T(8,128)}, u32[]{:S(2)}) copy-start(f32[16,512]{1,0:T(8,128)} %param.12) | copy-start | bytes 98308
  7.2 447.6 %copy-start.5 = (f32[16,512]{1,0:T(8,128)S(1)}, f32[16,512]{1,0:T(8,128)}, u32[]{:S(2)}) copy-start(f32[16,512]{1,0:T(8,128)} %param.13) | copy-start | bytes 98308
  7.2 447.5 %reduce-scatter.2.cloned.1.call-start = ((), (), s32[]{:S(2)}) async-start(), calls=%async_computation.2 | async-start | bytes 2129920 | tf_op jit(solution)/shard_map/reduce_scatter | solution.py:45
  10.1 582.5 %copy-start = (bf16[1,128,8192]{2,1,0:T(8,128)(2,1)S(1)}, bf16[1,128,8192]{2,1,0:T(8,128)(2,1)}, u32[]{:S(2)}) copy-start(bf16[1,128,8192]{2,1,0:T(8,128)(2,1)} %param.7) | copy-start | bytes 6291460
  10.1 582.5 %all-gather.6.cloned.1.call-start = ((), (), s32[]{:S(2)}) async-start(), calls=%async_computation.3 | async-start | bytes 1064960 | tf_op jit(solution)/shard_map/all_gather | solution.py:52
  456.1 262.0 %all-gather.8.cloned.1.call-start = ((), (), s32[]{:S(2)}) async-start(), calls=%async_computation.4 | async-start | bytes 9437184 | tf_op jit(solution)/shard_map/all_gather | solution.py:72
  596.5 4.6 copy-start.7
  596.5 87.1 %copy-start.6 = (bf16[1024]{0:T(1024)(128)(2,1)S(1)}, bf16[1024]{0:T(1024)(128)(2,1)}, u32[]{:S(2)}) copy-start(bf16[1024]{0:T(1024)(128)(2,1)} %param.8) | copy-start | bytes 6148
  596.5 100.3 %copy-start.3 = (bf16[1,128,512]{2,1,0:T(8,128)(2,1)S(1)}, bf16[1,128,512]{2,1,0:T(8,128)(2,1)}, u32[]{:S(2)}) copy-start(bf16[1,128,512]{2,1,0:T(8,128)(2,1)} %param.10) | copy-start | bytes 393220
  596.5 157.6 %all-to-all-start = ((bf16[128,8,1024]{2,0,1:T(8,128)(2,1)}), bf16[128,8,1024]{2,0,1:T(8,128)(2,1)}, u32[]{:S(2)}, u32[]{:S(2)}) async-start(bf16[128,8,1024]{2,0,1:T(8,128)(2,1)} %copy.21), calls=%async_computation.1 | async-start | bytes 4194304 | tf_op jit(solution)/shard_map/all_to_all | solution.py:67
  601.0 174.7 %all-gather.10.cloned.1.call-start = ((), (), s32[]{:S(2)}) async-start(), calls=%async_computation.5 | async-start | bytes 1179648 | tf_op jit(solution)/shard_map/all_gather | solution.py:79
  775.7 2.8 copy-start.2
  779.5 1.4 copy-start.1
Sparse Core Ops, SparseCore 0:
  10.8 443.8 reduce-scatter.1
  459.8 132.7 all-gather.5
  594.7 123.4 all-gather.7
  736.2 39.5 all-gather.9
where the time goes:
time: 796 us; the launch traced here: 794 us
  waiting for transfers between devices  620 us (78%)
  blocking collectives  114 us (14%)
  matrix products  17 us (2%)
  local copies, waits for them, and re-layouts  16.1 us (2%)
  between operations  14 us (2%)
  other arithmetic  8.09 us (1%)
    reduce_scatter x1, waiting for transfers between devices, body(): lax.psum_scatter(pseudo_grad[0].astype(jnp.float32), 'island', scatter_di...  445 us
    all_gather x1, waiting for transfers between devices, body(): weight_shard = lax.all_gather(fresh_rows, 'island', axis=0, tiled=True)  136 us
    pmin x1, blocking collectives, body(): starts = lax.pmin(local_first, 'fsdp')  82.5 us
    all_gather x1, waiting for transfers between devices, body(): lax.all_gather(weight_shard, 'fsdp', axis=0, tiled=True)  20.5 us
    all_gather x1, waiting for transfers between devices, body(): all_back = lax.all_gather(back_grad, 'fsdp', axis=0, tiled=True)  18.7 us
    all_gather x1, blocking collectives, body(): all_scales = lax.all_gather(row_scale, 'fsdp', axis=0, tiled=True)  18 us
  transfers between devices with their start and end apart: 5, of which 4 were waited for; matrix products, arithmetic and copies ran while one was open for 3% of the time, Pallas kernels for 0%

commit v1 on v0

v1 whole, which is shorter than its diff:
```python
import math

import jax
import jax.numpy as jnp
import numpy as np
from jax import lax
from jax.sharding import Mesh
from jax.sharding import PartitionSpec as P

HEAD = 128
DOCS = 8


learn_rate = 0.7
momentum_rate = 0.9
norm_eps = 1e-05
rope_base = 500000.0
far_index = 1 << 30

ISLAND_FACTORS = None


def angles_for(positions, head_width):
    half_width = head_width // 2
    frequency = jnp.exp(
        jnp.arange(half_width, dtype=jnp.float32) * (-2.0 * math.log(rope_base) / head_width)
    )
    phases = positions[:, None] * frequency[None, :]
    return (jnp.cos(phases), jnp.sin(phases))


def rotate(values, cosine, sine_part, sign):
    rows = values.shape[0]
    half_width = cosine.shape[1]
    shaped = values.reshape(rows, -1, 2 * half_width)
    leading = shaped[:, :, :half_width]
    second = shaped[:, :, half_width:]
    cos_b = cosine[:, None, :]
    sin_b = sine_part[:, None, :] * sign
    joined = jnp.concatenate(
        [leading * cos_b - second * sin_b, second * cos_b + leading * sin_b], axis=2
    )
    return joined.reshape(rows, -1)


def body(island_axes, hidden, gain, doc_ids, cotangent, pseudo_grad, outer_weight, momentum):
    islands = 1
    for ax in island_axes:
        islands *= lax.axis_size(ax)
    fsdp_ways = lax.axis_size("fsdp")

    summed = pseudo_grad[0].astype(jnp.float32)
    for ax in island_axes:
        summed = lax.psum_scatter(summed, ax, scatter_dimension=0, tiled=True)
    mean_delta = summed / islands
    new_momentum = momentum_rate * momentum + mean_delta
    new_outer = outer_weight - learn_rate * (mean_delta + momentum_rate * new_momentum)
    weight_shard = new_outer.astype(jnp.bfloat16)
    for ax in reversed(island_axes):
        weight_shard = lax.all_gather(weight_shard, ax, axis=0, tiled=True)

    tok_rows = hidden.shape[1]
    seq = tok_rows * fsdp_ways
    me = lax.axis_index("fsdp")
    all_docs = lax.all_gather(doc_ids[0], "fsdp", axis=0, tiled=True)
    indices = jnp.arange(seq, dtype=jnp.int32)
    documents = jnp.arange(DOCS, dtype=jnp.int32)
    in_document = all_docs[:, None] == documents[None, :]
    starts = jnp.min(jnp.where(in_document, indices[:, None], far_index), axis=0)
    doc_start = jnp.sum(jnp.where(in_document, starts[None, :], 0), axis=1)
    positions = (indices - doc_start).astype(jnp.float32)
    cosine, sine_part = angles_for(positions, HEAD)
    all_cot = lax.all_gather(cotangent[0], "fsdp", axis=0, tiled=True)
    all_back = rotate(all_cot.astype(jnp.float32), cosine, sine_part, -1.0).astype(jnp.bfloat16)

    hidden_f = hidden[0].astype(jnp.float32)
    row_scale = lax.rsqrt(jnp.mean(hidden_f * hidden_f, axis=1, keepdims=True) + norm_eps)
    all_scales = lax.all_gather(row_scale, "fsdp", axis=0, tiled=True)
    columns = lax.all_to_all(hidden[0], "fsdp", split_axis=1, concat_axis=0, tiled=True)
    normed_cols = columns.astype(jnp.float32) * all_scales
    act_cols = (normed_cols * gain.astype(jnp.float32)[None, :]).astype(jnp.bfloat16)

    grad_weight = jnp.zeros((act_cols.shape[1], all_back.shape[1]), jnp.float32)
    for block in range(fsdp_ways):
        act_block = act_cols[block * tok_rows : (block + 1) * tok_rows]
        back_block = all_back[block * tok_rows : (block + 1) * tok_rows]
        part = lax.dot_general(
            act_block, back_block, (((0,), (0,)), ((), ())), preferred_element_type=jnp.float32
        )
        grad_weight = grad_weight + part.astype(jnp.bfloat16).astype(jnp.float32)

    hidden_grad = lax.dot_general(
        all_back, weight_shard, (((1,), (1,)), ((), ())), preferred_element_type=jnp.float32
    )
    grad_gain = jnp.sum(hidden_grad * normed_cols, axis=0)

    partial_keys = jnp.dot(act_cols, weight_shard, preferred_element_type=jnp.float32)
    projected = lax.psum_scatter(partial_keys, "fsdp", scatter_dimension=0, tiled=True)
    my_cos = lax.dynamic_slice_in_dim(cosine, me * tok_rows, tok_rows, axis=0)
    my_sin = lax.dynamic_slice_in_dim(sine_part, me * tok_rows, tok_rows, axis=0)
    rotated = rotate(projected, my_cos, my_sin, 1.0).astype(jnp.bfloat16)
    return (
        rotated[None],
        grad_weight.astype(jnp.bfloat16)[None],
        grad_gain[None],
        new_outer,
        new_momentum,
    )


def _island_factors(n):
    if ISLAND_FACTORS is not None:
        return tuple(ISLAND_FACTORS)
    if n == 64:
        return (8, 4, 2)
    return (n,)


def solution(mesh):
    factors = _island_factors(mesh.shape["island"])
    island_axes = tuple(f"island{k}" for k in range(len(factors)))
    devices = np.asarray(mesh.devices).reshape(factors + (mesh.shape["fsdp"],))
    fine = Mesh(devices, island_axes + ("fsdp",))
    isl = island_axes
    placed = (
        P(isl, "fsdp", None),
        P("fsdp"),
        P(isl, "fsdp"),
        P(isl, "fsdp", None),
        P(isl, "fsdp", None),
        P(("fsdp",) + isl, None),
        P(("fsdp",) + isl, None),
    )
    return jax.shard_map(
        lambda *a: body(island_axes, *a),
        mesh=fine,
        in_specs=placed,
        out_specs=(
            P(isl, "fsdp", None),
            P(isl, "fsdp", None),
            P(isl, "fsdp"),
            P(("fsdp",) + isl, None),
            P(("fsdp",) + isl, None),
        ),
        check_vma=False,
    )
```

time: 796 us -> 269 us (0.34)
  waiting for transfers between devices: 620 us -> 173 us
  blocking collectives: 114 us -> 41.9 us
  local copies, waits for them, and re-layouts: 16.1 us -> 7.56 us
    reduce_scatter x1 -> x4, waiting for transfers between devices: 445 us -> 124 us  [the longest x3 93.9 us: body(): summed = lax.psum_scatter(summed, ax, scatter_dimension=0, tiled=True)]
    all_gather x3 -> x2, waiting for transfers between devices: 176 us -> 48.5 us  [the longest x1 33.9 us: body(): all_cot = lax.all_gather(cotangent[0], 'fsdp', axis=0, tiled=True)]
    pmin x1 -> x0, blocking collectives: 82.5 us -> none  [body(): starts = lax.pmin(local_first, 'fsdp')]
    all_gather x1 -> x3, blocking collectives: 13.1 us -> 29.9 us  [the longest x2 21.2 us: body(): weight_shard = lax.all_gather(weight_shard, ax, axis=0, tiled=True)]
    dot_general x1 -> x0, local copies, waits for them, and re-layouts: 11.3 us -> none  [body(): jnp.dot(activations, weight_full, preferred_element_type=jnp.float32)]
  transfers between devices with their start and end apart: 5 -> 7, of which waited for: 4 -> 6; matrix products, arithmetic and copies ran while one was open for 3% -> 11% of each run, Pallas kernels for 0% -> 0%
where the time goes in v1:
time: 269 us
  waiting for transfers between devices  173 us (64%)
  blocking collectives  41.9 us (16%)
  between operations  14.3 us (5%)
  other arithmetic  14.1 us (5%)
  matrix products  12.6 us (5%)
  local copies, waits for them, and re-layouts  7.56 us (3%)
  starting transfers between devices  5 us (2%)
    reduce_scatter x3, waiting for transfers between devices, body(): summed = lax.psum_scatter(summed, ax, scatter_dimension=0, tiled=True)  93.9 us
    all_gather x1, waiting for transfers between devices, body(): all_cot = lax.all_gather(cotangent[0], 'fsdp', axis=0, tiled=True)  33.9 us
    reduce_scatter x1, waiting for transfers between devices, body(): lax.psum_scatter(partial_keys, 'fsdp', scatter_dimension=0, tiled=True)  30.3 us
    all_gather x2, blocking collectives, body(): weight_shard = lax.all_gather(weight_shard, ax, axis=0, tiled=True)  21.2 us
    all_gather x1, waiting for transfers between devices, body(): weight_shard = lax.all_gather(weight_shard, ax, axis=0, tiled=True)  14.7 us
    all_gather x1, blocking collectives, body(): all_scales = lax.all_gather(row_scale, 'fsdp', axis=0, tiled=True)  12 us
    all_gather x1, blocking collectives, body(): all_docs = lax.all_gather(doc_ids[0], 'fsdp', axis=0, tiled=True)  8.72 us
  transfers between devices with their start and end apart: 7, of which 6 were waited for; matrix products, arithmetic and copies ran while one was open for 11% of the time, Pallas kernels for 0%

profile of v1, /device:TPU:6, one launch (start us, length us, event | category | flops | bytes accessed | tf_op | source)
XLA Modules:
  0.0 268.8 jit_solution(17551781969576260683)
XLA Ops:
  7.2 3.0 %bitcast_convert_fusion = f32[1024,512]{1,0:T(8,128)} fusion(bf16[1,1024,512]{2,1,0:T(8,128)(2,1)} %param.11), kind=kLoop, calls=%fused_computation.18 | loop fusion | flops 524288 | bytes 3145728 | tf_op jit(solution)/shard_map/convert_element_type | solution.py:52
  10.3 51.1 %reduce-scatter.5.cloned.1.call-done = f32[128,512]{1,0:T(8,128)} async-done(((f32[1024,512]{1,0:T(8,128)}), f32[128,512]{1,0:T(8,128)}) %reduce-scatter.5.cloned.1.call-update) | async-done | bytes 262160 | tf_op jit(solution)/shard_map/reduce_scatter | solution.py:54
  61.4 1.4 copy.15
  62.8 2.5 copy.14
  65.3 4.8 %all-to-all-start = ((bf16[128,8,1024]{2,0,1:T(8,128)(2,1)}), bf16[128,8,1024]{2,0,1:T(8,128)(2,1)}, u32[]{:S(2)}, u32[]{:S(2)}) async-start(bf16[128,8,1024]{2,0,1:T(8,128)(2,1)} %copy.14), calls=%async_computation | async-start | bytes 4194304 | tf_op jit(solution)/shard_map/all_to_all | solution.py:79
  70.1 17.2 %reduce-scatter.7.cloned.1.call-done = f32[32,512]{1,0:T(8,128)} async-done(((f32[128,512]{1,0:T(8,128)}), f32[32,512]{1,0:T(8,128)}) %reduce-scatter.7.cloned.1.call-update) | async-done | bytes 65552 | tf_op jit(solution)/shard_map/reduce_scatter | solution.py:54
  87.4 25.5 %reduce-scatter.9.cloned.1.call-done = f32[16,512]{1,0:T(8,128)} async-done(((f32[32,512]{1,0:T(8,128)}), f32[16,512]{1,0:T(8,128)}) %reduce-scatter.9.cloned.1.call-update) | async-done | bytes 32784 | tf_op jit(solution)/shard_map/reduce_scatter | solution.py:54
  113.0 1.4 fusion.27
  114.3 8.5 %all_gather.19 = bf16[32,512]{1,0:T(8,128)(2,1)S(1)} all-gather(bf16[16,512]{1,0:T(8,128)(2,1)S(1)} %get-tuple-element.5), channel_id=1, replica_groups=mesh['island0'=8,'island1'=4,'island2'=2,'fsdp'=8] {'island2'}, dimensions={0}, use_global_device_ids=true | all-gather | bytes 49152 | tf_op jit(solution)/shard_map/all_gather | solution.py:60
  122.8 12.7 %all_gather.20 = bf16[128,512]{1,0:T(8,128)(2,1)} all-gather(bf16[32,512]{1,0:T(8,128)(2,1)S(1)} %all_gather.19), channel_id=1, replica_groups=mesh['island0'=8,'island1'=4,'island2'=2,'fsdp'=8] {'island1'}, dimensions={0}, use_global_device_ids=true | all-gather | bytes 163840 | tf_op jit(solution)/shard_map/all_gather | solution.py:60
  136.7 12.0 %all-gather.3 = f32[8,1,128]{2,1,0:T(1,128)S(1)} all-gather(f32[1,1,128]{2,1,0:T(1,128)S(1)} %rsqrt_bitcast_fusion), channel_id=2, replica_groups=mesh['island0'=8,'island1'=4,'island2'=2,'fsdp'=8] {'fsdp'}, dimensions={0}, use_global_device_ids=true | all-gather | bytes 4608 | tf_op jit(solution)/shard_map/all_gather | solution.py:78
  148.7 8.7 %all-gather.1 = s32[1,1024]{1,0:T(1,128)S(1)} all-gather(s32[1,128]{1,0:T(1,128)S(1)} %copy-done.6), channel_id=3, replica_groups=mesh['island0'=8,'island1'=4,'island2'=2,'fsdp'=8] {'fsdp'}, dimensions={1}, use_global_device_ids=true | all-gather | bytes 4608 | tf_op jit(solution)/shard_map/all_gather | solution.py:65
  157.6 2.1 multiply_convert_fusion
  159.8 14.7 %all-gather.7.cloned.1.call-done = bf16[1024,512]{1,0:T(8,128)(2,1)} async-done(((bf16[128,512]{1,0:T(8,128)(2,1)}), bf16[1024,512]{1,0:T(8,128)(2,1)}) %all-gather.7.cloned.1.call-update) | async-done | bytes 1048592 | tf_op jit(solution)/shard_map/all_gather | solution.py:60
  174.5 3.8 %fusion.28 = f32[1024,512]{1,0:T(8,128)} fusion(bf16[1024,1024]{1,0:T(8,128)(2,1)S(1)} %multiply_convert_fusion, bf16[1024,512]{1,0:T(8,128)(2,1)} %all-gather.7.cloned.1.call-done), kind=kOutput, calls=%fused_computation.69 | convolution fusion | flops 1073741824 | bytes 5242880 | tf_op jit(solution)/shard_map/dot_general | solution.py:97
  178.3 1.9 broadcast_multiply_fusion
  180.3 33.9 %all-gather.9.cloned.1.call-done = bf16[1,1024,512]{2,1,0:T(8,128)(2,1)} async-done(((bf16[1,128,512]{2,1,0:T(8,128)(2,1)}), bf16[1,1024,512]{2,1,0:T(8,128)(2,1)}) %all-gather.9.cloned.1.call-update) | async-done | bytes 1048592 | tf_op jit(solution)/shard_map/all_gather | solution.py:73
  214.1 1.7 reshape.144
  215.9 1.6 subtract_convert_fusion
  218.9 1.4 pad_maximum_fusion.1
  223.7 2.2 fusion
  225.9 3.5 %multiply_reduce_fusion = f32[1024]{0:T(1024)} fusion(bf16[128,8,1024]{2,0,1:T(8,128)(2,1)} %all-to-all-done, bf16[1024,512]{1,0:T(8,128)(2,1)S(1)} %copy-done.7, f32[1024]{0:T(1024)S(1)} %bitcast.74, bf16[128,8,4,128]{3,2,1,0:T(4,128)(2,1)S(1)} %bitcast.62), kind=kOutput, calls=%fused_computation.1 | convolution fusion | flops 1077935104 | bytes 4202496 | tf_op jit(solution)/shard_map/dot_general | solution.py:92
  229.4 30.3 %reduce-scatter.11.cloned.1.call-done = f32[128,512]{1,0:T(8,128)} async-done(((f32[1024,512]{1,0:T(8,128)}), f32[128,512]{1,0:T(8,128)}) %reduce-scatter.11.cloned.1.call-update) | async-done | bytes 262160 | tf_op jit(solution)/shard_map/reduce_scatter | solution.py:98
  259.7 1.0 reshape.138
  (49 shorter events, 7.5 us)
Async XLA Ops:
  7.2 54.2 %copy-start.2 = (bf16[1,128,8192]{2,1,0:T(8,128)(2,1)S(1)}, bf16[1,128,8192]{2,1,0:T(8,128)(2,1)}, u32[]{:S(2)}) copy-start(bf16[1,128,8192]{2,1,0:T(8,128)(2,1)} %param.7) | copy-start | bytes 6291460
  7.2 54.2 %reduce-scatter.5.cloned.1.call-start = ((), (), s32[]{:S(2)}) async-start(), calls=%async_computation.5 | async-start | bytes 2359296 | tf_op jit(solution)/shard_map/reduce_scatter | solution.py:54
  10.2 77.1 %reduce-scatter.7.cloned.1.call-start = ((), (), s32[]{:S(2)}) async-start(), calls=%async_computation.6 | async-start | bytes 327680 | tf_op jit(solution)/shard_map/reduce_scatter | solution.py:54
  65.3 47.6 %copy-start.3 = (f32[16,512]{1,0:T(8,128)S(1)}, f32[16,512]{1,0:T(8,128)}, u32[]{:S(2)}) copy-start(f32[16,512]{1,0:T(8,128)} %param.12) | copy-start | bytes 98308
  65.3 47.6 %copy-start.4 = (f32[16,512]{1,0:T(8,128)S(1)}, f32[16,512]{1,0:T(8,128)}, u32[]{:S(2)}) copy-start(f32[16,512]{1,0:T(8,128)} %param.13) | copy-start | bytes 98308
  65.3 70.9 %copy-start.5 = (bf16[1024]{0:T(1024)(128)(2,1)S(1)}, bf16[1024]{0:T(1024)(128)(2,1)}, u32[]{:S(2)}) copy-start(bf16[1024]{0:T(1024)(128)(2,1)} %param.8) | copy-start | bytes 6148
  65.3 92.3 %all-to-all-start = ((bf16[128,8,1024]{2,0,1:T(8,128)(2,1)}), bf16[128,8,1024]{2,0,1:T(8,128)(2,1)}, u32[]{:S(2)}, u32[]{:S(2)}) async-start(bf16[128,8,1024]{2,0,1:T(8,128)(2,1)} %copy.14), calls=%async_computation | async-start | bytes 4194304 | tf_op jit(solution)/shard_map/all_to_all | solution.py:79
  70.1 78.6 %copy-start.6 = (s32[1,128]{1,0:T(1,128)S(1)}, s32[1,128]{1,0:T(1,128)}, u32[]{:S(2)}) copy-start(s32[1,128]{1,0:T(1,128)} %param.9) | copy-start | bytes 1540
  70.1 42.9 %reduce-scatter.9.cloned.1.call-start = ((), (), s32[]{:S(2)}) async-start(), calls=%async_computation.7 | async-start | bytes 98304 | tf_op jit(solution)/shard_map/reduce_scatter | solution.py:54
  87.4 87.1 %all-gather.7.cloned.1.call-start = ((), (), s32[]{:S(2)}) async-start(), calls=%async_computation.8 | async-start | bytes 1179648 | tf_op jit(solution)/shard_map/all_gather | solution.py:60
  135.5 78.6 %all-gather.9.cloned.1.call-start = ((), (), s32[]{:S(2)}) async-start(), calls=%async_computation.10 | async-start | bytes 1179648 | tf_op jit(solution)/shard_map/all_gather | solution.py:73
  136.1 123.6 %reduce-scatter.11.cloned.1.call-start = ((), (), s32[]{:S(2)}) async-start(), calls=%async_computation.9 | async-start | bytes 2359296 | tf_op jit(solution)/shard_map/reduce_scatter | solution.py:98
  159.8 18.5 %copy-start = (bf16[1024,1024]{1,0:T(8,128)(2,1)}, bf16[1024,1024]{1,0:T(8,128)(2,1)S(1)}, u32[]{:S(2)}) copy-start(bf16[1024,1024]{1,0:T(8,128)(2,1)S(1)} %multiply_convert_fusion) | copy-start | bytes 6291460
  218.9 1.6 copy-start.1
  223.7 2.2 copy-start.7
Sparse Core Ops, SparseCore 0:
  10.8 50.5 reduce-scatter.4
  64.2 23.1 reduce-scatter.6
  90.1 22.8 reduce-scatter.8
  135.7 38.7 all-gather.6
  176.4 37.6 all-gather.8
  216.8 42.8 reduce-scatter.10

commit v2 on v1

--- a/solution.py
+++ b/solution.py
@@ -49,15 +49,16 @@
         islands *= lax.axis_size(ax)
     fsdp_ways = lax.axis_size("fsdp")
 
+    stages = (island_axes[:1], island_axes[1:]) if len(island_axes) > 1 else (island_axes,)
     summed = pseudo_grad[0].astype(jnp.float32)
-    for ax in island_axes:
-        summed = lax.psum_scatter(summed, ax, scatter_dimension=0, tiled=True)
+    for axes in stages:
+        summed = lax.psum_scatter(summed, axes, scatter_dimension=0, tiled=True)
     mean_delta = summed / islands
     new_momentum = momentum_rate * momentum + mean_delta
     new_outer = outer_weight - learn_rate * (mean_delta + momentum_rate * new_momentum)
     weight_shard = new_outer.astype(jnp.bfloat16)
-    for ax in reversed(island_axes):
-        weight_shard = lax.all_gather(weight_shard, ax, axis=0, tiled=True)
+    for axes in reversed(stages):
+        weight_shard = lax.all_gather(weight_shard, axes, axis=0, tiled=True)
 
     tok_rows = hidden.shape[1]
     seq = tok_rows * fsdp_ways
@@ -70,13 +71,23 @@
     doc_start = jnp.sum(jnp.where(in_document, starts[None, :], 0), axis=1)
     positions = (indices - doc_start).astype(jnp.float32)
     cosine, sine_part = angles_for(positions, HEAD)
-    all_cot = lax.all_gather(cotangent[0], "fsdp", axis=0, tiled=True)
+    width = hidden.shape[2] // fsdp_ways
+    cols_out = cotangent.shape[2]
+    outgoing = jnp.concatenate(
+        [
+            hidden[0].reshape(tok_rows, fsdp_ways, width).transpose(1, 0, 2),
+            jnp.broadcast_to(cotangent[0][None], (fsdp_ways, tok_rows, cols_out)),
+        ],
+        axis=2,
+    )
+    incoming = lax.all_to_all(outgoing, "fsdp", split_axis=0, concat_axis=0, tiled=True)
+    columns = incoming[:, :, :width].reshape(seq, width)
+    all_cot = incoming[:, :, width:].reshape(seq, cols_out)
     all_back = rotate(all_cot.astype(jnp.float32), cosine, sine_part, -1.0).astype(jnp.bfloat16)
 
     hidden_f = hidden[0].astype(jnp.float32)
     row_scale = lax.rsqrt(jnp.mean(hidden_f * hidden_f, axis=1, keepdims=True) + norm_eps)
     all_scales = lax.all_gather(row_scale, "fsdp", axis=0, tiled=True)
-    columns = lax.all_to_all(hidden[0], "fsdp", split_axis=1, concat_axis=0, tiled=True)
     normed_cols = columns.astype(jnp.float32) * all_scales
     act_cols = (normed_cols * gain.astype(jnp.float32)[None, :]).astype(jnp.bfloat16)
 

time: 269 us -> 295 us (1.097)
  blocking collectives: 41.9 us -> 63.2 us
  other arithmetic: 14.1 us -> 20 us
    reduce_scatter x3 -> x2, waiting for transfers between devices: 93.9 us -> 133 us  [body(): summed = lax.psum_scatter(summed, axes, scatter_dimension=0, tiled=True)]
    all_gather x2 -> x1, waiting for transfers between devices: 48.5 us -> 15.5 us  [body(): weight_shard = lax.all_gather(weight_shard, axes, axis=0, tiled=True)]
    all_gather x2 -> x1, blocking collectives: 21.2 us -> 44.3 us  [body(): weight_shard = lax.all_gather(weight_shard, axes, axis=0, tiled=True)]
    reduce_scatter x1, waiting for transfers between devices: 30.3 us -> 22.8 us  [body(): lax.psum_scatter(partial_keys, 'fsdp', scatter_dimension=0, tiled=True)]
  transfers between devices with their start and end apart: 7 -> 5, of which waited for: 6 -> 4; matrix products, arithmetic and copies ran while one was open for 11% -> 10% of each run, Pallas kernels for 0% -> 0%
where the time goes in v2:
time: 295 us; the launch traced here: 294 us
  waiting for transfers between devices  171 us (58%)
  blocking collectives  63.2 us (21%)
  other arithmetic  20 us (7%)
  between operations  14 us (5%)
  matrix products  11.6 us (4%)
  local copies, waits for them, and re-layouts  9 us (3%)
  starting transfers between devices  5.17 us (2%)
    reduce_scatter x2, waiting for transfers between devices, body(): summed = lax.psum_scatter(summed, axes, scatter_dimension=0, tiled=True)  133 us
    all_gather x1, blocking collectives, body(): weight_shard = lax.all_gather(weight_shard, axes, axis=0, tiled=True)  44.3 us
    reduce_scatter x1, waiting for transfers between devices, body(): lax.psum_scatter(partial_keys, 'fsdp', scatter_dimension=0, tiled=True)  22.8 us
    all_gather x1, waiting for transfers between devices, body(): weight_shard = lax.all_gather(weight_shard, axes, axis=0, tiled=True)  15.5 us
    all_gather x1, blocking collectives, body(): all_docs = lax.all_gather(doc_ids[0], 'fsdp', axis=0, tiled=True)  9.69 us
    all_gather x1, blocking collectives, body(): all_scales = lax.all_gather(row_scale, 'fsdp', axis=0, tiled=True)  9.28 us
  transfers between devices with their start and end apart: 5, of which 4 were waited for; matrix products, arithmetic and copies ran while one was open for 10% of the time, Pallas kernels for 0%

profile of v2, /device:TPU:6, one launch (start us, length us, event | category | flops | bytes accessed | tf_op | source)
XLA Modules:
  0.0 294.2 jit_solution(8046850983464915095)
XLA Ops:
  7.2 3.0 %bitcast_convert_fusion = f32[1024,512]{1,0:T(8,128)} fusion(bf16[1,1024,512]{2,1,0:T(8,128)(2,1)} %param.11), kind=kLoop, calls=%fused_computation.23 | loop fusion | flops 524288 | bytes 3145728 | tf_op jit(solution)/shard_map/convert_element_type | solution.py:53
  10.3 1.4 copy.15
  11.7 1.2 copy.62
  13.0 1.9 pad_maximum_fusion
  14.8 5.0 %all-to-all-start = ((bf16[8,128,1536]{2,1,0:T(8,128)(2,1)}), bf16[8,128,1536]{2,1,0:T(8,128)(2,1)S(1)}, u32[]{:S(2)}, u32[]{:S(2)}) async-start(bf16[8,128,1536]{2,1,0:T(8,128)(2,1)} %pad_maximum_fusion), calls=%async_computation | async-start | bytes 6291456 | tf_op jit(solution)/shard_map/all_to_all | solution.py:83
  19.9 41.5 %reduce-scatter.4.cloned.1.call-done = f32[128,512]{1,0:T(8,128)} async-done(((f32[1024,512]{1,0:T(8,128)}), f32[128,512]{1,0:T(8,128)}) %reduce-scatter.4.cloned.1.call-update) | async-done | bytes 262160 | tf_op jit(solution)/shard_map/reduce_scatter | solution.py:55
  61.5 91.3 %reduce-scatter.6.cloned.1.call-done = f32[16,512]{1,0:T(8,128)} async-done(((f32[128,512]{1,0:T(8,128)}), f32[16,512]{1,0:T(8,128)}) %reduce-scatter.6.cloned.1.call-update) | async-done | bytes 32784 | tf_op jit(solution)/shard_map/reduce_scatter | solution.py:55
  152.8 1.4 fusion.31
  154.2 44.3 %all_gather.13 = bf16[128,512]{1,0:T(8,128)(2,1)} all-gather(bf16[16,512]{1,0:T(8,128)(2,1)S(1)} %get-tuple-element.5), channel_id=1, replica_groups=mesh['island0'=8,'island1'=4,'island2'=2,'fsdp'=8] {'island1','island2'}, dimensions={0}, use_global_device_ids=true | all-gather | bytes 147456 | tf_op jit(solution)/shard_map/all_gather | solution.py:61
  198.5 2.1 multiply_reduce_fusion
  200.6 9.3 %all-gather.2 = f32[8,1,128]{2,1,0:T(1,128)S(1)} all-gather(f32[1,1,128]{2,1,0:T(1,128)S(1)} %rsqrt_bitcast_fusion), channel_id=2, replica_groups=mesh['island0'=8,'island1'=4,'island2'=2,'fsdp'=8] {'fsdp'}, dimensions={0}, use_global_device_ids=true | all-gather | bytes 4608 | tf_op jit(solution)/shard_map/all_gather | solution.py:90
  209.9 9.7 %all-gather.1 = s32[1,1024]{1,0:T(1,128)S(1)} all-gather(s32[1,128]{1,0:T(1,128)S(1)} %copy-done.11), channel_id=3, replica_groups=mesh['island0'=8,'island1'=4,'island2'=2,'fsdp'=8] {'fsdp'}, dimensions={1}, use_global_device_ids=true | all-gather | bytes 4608 | tf_op jit(solution)/shard_map/all_gather | solution.py:66
  220.1 1.3 copy-done.2
  221.4 1.9 fusion.2
  223.3 15.5 %all-gather.5.cloned.1.call-done = bf16[1024,512]{1,0:T(8,128)(2,1)} async-done(((bf16[128,512]{1,0:T(8,128)(2,1)}), bf16[1024,512]{1,0:T(8,128)(2,1)}) %all-gather.5.cloned.1.call-update) | async-done | bytes 1048592 | tf_op jit(solution)/shard_map/all_gather | solution.py:61
  238.8 4.4 %fusion.32 = f32[1024,512]{1,0:T(8,128)} fusion(bf16[1024,1024]{1,0:T(8,128)(2,1)} %fusion.2, bf16[1024,512]{1,0:T(8,128)(2,1)} %all-gather.5.cloned.1.call-done), kind=kOutput, calls=%fused_computation.74 | convolution fusion | flops 1073741824 | bytes 5242880 | tf_op jit(solution)/shard_map/dot_general | solution.py:108
  243.2 3.0 %broadcast_multiply_fusion = (f32[1024,64]{1,0:T(8,128)}, f32[1024,64]{1,0:T(8,128)S(1)}, f32[1024,64]{1,0:T(8,128)S(1)}) fusion(f32[64]{0:T(128)S(1)} %multiply_exponential_fusion, f32[1024]{0:T(1024)S(1)} %subtract_convert_fusion.2), kind=kLoop, calls=%fused_computation.34 | loop fusion | flops 131072 | bytes 790784 | tf_op jit(solution)/shard_map/mul | solution.py:39
  247.0 1.6 slice_convert_fusion
  248.6 2.0 reshape.137
  250.7 1.6 subtract_convert_fusion
  253.8 1.4 pad_maximum_fusion.2
  258.6 2.2 fusion.4
  260.7 1.9 fusion.3
  262.6 22.8 %reduce-scatter.8.cloned.1.call-done = f32[128,512]{1,0:T(8,128)} async-done(((f32[1024,512]{1,0:T(8,128)}), f32[128,512]{1,0:T(8,128)}) %reduce-scatter.8.cloned.1.call-update) | async-done | bytes 262160 | tf_op jit(solution)/shard_map/reduce_scatter | solution.py:109
  (56 shorter events, 8.6 us)
Async XLA Ops:
  7.2 3.1 %copy-start.1 = (bf16[1,128,8192]{2,1,0:T(8,128)(2,1)S(1)}, bf16[1,128,8192]{2,1,0:T(8,128)(2,1)}, u32[]{:S(2)}) copy-start(bf16[1,128,8192]{2,1,0:T(8,128)(2,1)} %param.7) | copy-start | bytes 6291460
  7.2 54.2 %reduce-scatter.4.cloned.1.call-start = ((), (), s32[]{:S(2)}) async-start(), calls=%async_computation.4 | async-start | bytes 2359296 | tf_op jit(solution)/shard_map/reduce_scatter | solution.py:55
  11.7 1.2 copy-start.7
  14.8 137.9 %copy-start.8 = (f32[16,512]{1,0:T(8,128)S(1)}, f32[16,512]{1,0:T(8,128)}, u32[]{:S(2)}) copy-start(f32[16,512]{1,0:T(8,128)} %param.12) | copy-start | bytes 98308
  14.8 137.9 %copy-start.9 = (f32[16,512]{1,0:T(8,128)S(1)}, f32[16,512]{1,0:T(8,128)}, u32[]{:S(2)}) copy-start(f32[16,512]{1,0:T(8,128)} %param.13) | copy-start | bytes 98308
  14.8 183.7 %copy-start.10 = (bf16[1024]{0:T(1024)(128)(2,1)S(1)}, bf16[1024]{0:T(1024)(128)(2,1)}, u32[]{:S(2)}) copy-start(bf16[1024]{0:T(1024)(128)(2,1)} %param.8) | copy-start | bytes 6148
  14.8 205.0 %all-to-all-start = ((bf16[8,128,1536]{2,1,0:T(8,128)(2,1)}), bf16[8,128,1536]{2,1,0:T(8,128)(2,1)S(1)}, u32[]{:S(2)}, u32[]{:S(2)}) async-start(bf16[8,128,1536]{2,1,0:T(8,128)(2,1)} %pad_maximum_fusion), calls=%async_computation | async-start | bytes 6291456 | tf_op jit(solution)/shard_map/all_to_all | solution.py:83
  19.9 190.1 %copy-start.11 = (s32[1,128]{1,0:T(1,128)S(1)}, s32[1,128]{1,0:T(1,128)}, u32[]{:S(2)}) copy-start(s32[1,128]{1,0:T(1,128)} %param.9) | copy-start | bytes 1540
  19.9 132.9 %reduce-scatter.6.cloned.1.call-start = ((), (), s32[]{:S(2)}) async-start(), calls=%async_computation.5 | async-start | bytes 294912 | tf_op jit(solution)/shard_map/reduce_scatter | solution.py:55
  61.4 177.4 %all-gather.5.cloned.1.call-start = ((), (), s32[]{:S(2)}) async-start(), calls=%async_computation.6 | async-start | bytes 1179648 | tf_op jit(solution)/shard_map/all_gather | solution.py:61
  198.5 87.0 %reduce-scatter.8.cloned.1.call-start = ((), (), s32[]{:S(2)}) async-start(), calls=%async_computation.7 | async-start | bytes 2359296 | tf_op jit(solution)/shard_map/reduce_scatter | solution.py:109
  220.1 1.3 copy-start.2
  246.2 0.8 copy-start.4
  248.6 2.0 copy-start.5
  248.6 2.0 copy-start.6
  253.8 1.6 copy-start
  258.5 2.2 copy-start.3
  258.6 2.2 copy-start.12
Sparse Core Ops, SparseCore 0:
  10.8 50.5 reduce-scatter.3
  65.8 86.9 reduce-scatter.5
  198.6 40.1 all-gather.4
  243.3 42.0 reduce-scatter.7

commit v3 on v2

--- a/solution.py
+++ b/solution.py
@@ -43,22 +43,54 @@
     return joined.reshape(rows, -1)
 
 
+def halving_scatter(values, axis):
+    n = lax.axis_size(axis)
+    me = lax.axis_index(axis)
+    step = n // 2
+    while step >= 1:
+        rows = values.shape[0] // 2
+        upper = (me // step) % 2
+        keep = lax.dynamic_slice_in_dim(values, upper * rows, rows, axis=0)
+        send = lax.dynamic_slice_in_dim(values, (1 - upper) * rows, rows, axis=0)
+        got = lax.ppermute(send, axis, [(j, j ^ step) for j in range(n)])
+        values = keep + got
+        step //= 2
+    return values
+
+
+def doubling_gather(values, axis):
+    n = lax.axis_size(axis)
+    me = lax.axis_index(axis)
+    step = 1
+    while step < n:
+        got = lax.ppermute(values, axis, [(j, j ^ step) for j in range(n)])
+        upper = (me // step) % 2
+        values = jnp.where(
+            upper == 1,
+            jnp.concatenate([got, values], axis=0),
+            jnp.concatenate([values, got], axis=0),
+        )
+        step *= 2
+    return values
+
+
 def body(island_axes, hidden, gain, doc_ids, cotangent, pseudo_grad, outer_weight, momentum):
     islands = 1
     for ax in island_axes:
         islands *= lax.axis_size(ax)
     fsdp_ways = lax.axis_size("fsdp")
 
-    stages = (island_axes[:1], island_axes[1:]) if len(island_axes) > 1 else (island_axes,)
     summed = pseudo_grad[0].astype(jnp.float32)
-    for axes in stages:
-        summed = lax.psum_scatter(summed, axes, scatter_dimension=0, tiled=True)
+    summed = lax.psum_scatter(summed, island_axes[0], scatter_dimension=0, tiled=True)
+    for ax in island_axes[1:]:
+        summed = halving_scatter(summed, ax)
     mean_delta = summed / islands
     new_momentum = momentum_rate * momentum + mean_delta
     new_outer = outer_weight - learn_rate * (mean_delta + momentum_rate * new_momentum)
     weight_shard = new_outer.astype(jnp.bfloat16)
-    for axes in reversed(stages):
-        weight_shard = lax.all_gather(weight_shard, axes, axis=0, tiled=True)
+    for ax in reversed(island_axes[1:]):
+        weight_shard = doubling_gather(weight_shard, ax)
+    weight_shard = lax.all_gather(weight_shard, island_axes[0], axis=0, tiled=True)
 
     tok_rows = hidden.shape[1]
     seq = tok_rows * fsdp_ways

time: 295 us -> 213 us (0.72)
  waiting for transfers between devices: 171 us -> 95.1 us
  blocking collectives: 63.2 us -> 27.3 us
  starting transfers between devices: 5.17 us -> 32.2 us
    reduce_scatter x2 -> x1, waiting for transfers between devices: 133 us -> 41.4 us  [body(): lax.psum_scatter(summed, island_axes[0], scatter_dimension=0, tiled=True)]
    all_gather x1 -> x0, blocking collectives: 44.3 us -> none  [body(): weight_shard = lax.all_gather(weight_shard, axes, axis=0, tiled=True)]
    ppermute x0 -> x6, starting transfers between devices: none -> 27.1 us  [the longest x3 13.6 us: doubling_gather(): got = lax.ppermute(values, axis, [(j, j ^ step) for j in range(n)])]
    ppermute x0 -> x6, waiting for transfers between devices: none -> 20.1 us  [the longest x3 10.8 us: halving_scatter(): got = lax.ppermute(send, axis, [(j, j ^ step) for j in range(n)])]
    all_gather x1, blocking collectives: 9.28 us -> 18.4 us  [body(): all_scales = lax.all_gather(row_scale, 'fsdp', axis=0, tiled=True)]
    all_gather x1, waiting for transfers between devices: 15.5 us -> 12.2 us  [body(): lax.all_gather(weight_shard, island_axes[0], axis=0, tiled=True)]
  transfers between devices with their start and end apart: 5 -> 10, of which waited for: 4 -> 9; matrix products, arithmetic and copies ran while one was open for 10% -> 15% of each run, Pallas kernels for 0% -> 0%
where the time goes in v3:
time: 213 us
  waiting for transfers between devices  95.1 us (45%)
  starting transfers between devices  32.2 us (15%)
  blocking collectives  27.3 us (13%)
  other arithmetic  22 us (10%)
  between operations  14.2 us (7%)
  matrix products  11.7 us (5%)
  local copies, waits for them, and re-layouts  10 us (5%)
    reduce_scatter x1, waiting for transfers between devices, body(): lax.psum_scatter(summed, island_axes[0], scatter_dimension=0, tiled=True)  41.4 us
    reduce_scatter x1, waiting for transfers between devices, body(): lax.psum_scatter(partial_keys, 'fsdp', scatter_dimension=0, tiled=True)  21.4 us
    all_gather x1, blocking collectives, body(): all_scales = lax.all_gather(row_scale, 'fsdp', axis=0, tiled=True)  18.4 us
    ppermute x3, starting transfers between devices, doubling_gather(): got = lax.ppermute(values, axis, [(j, j ^ step) for j in range(n)])  13.6 us
    ppermute x3, starting transfers between devices, halving_scatter(): got = lax.ppermute(send, axis, [(j, j ^ step) for j in range(n)])  13.5 us
    all_gather x1, waiting for transfers between devices, body(): lax.all_gather(weight_shard, island_axes[0], axis=0, tiled=True)  12.2 us
    ppermute x3, waiting for transfers between devices, halving_scatter(): got = lax.ppermute(send, axis, [(j, j ^ step) for j in range(n)])  10.8 us
    ppermute x3, waiting for transfers between devices, doubling_gather(): got = lax.ppermute(values, axis, [(j, j ^ step) for j in range(n)])  9.36 us
  transfers between devices with their start and end apart: 10, of which 9 were waited for; matrix products, arithmetic and copies ran while one was open for 15% of the time, Pallas kernels for 0%

profile of v3, /device:TPU:6, one launch (start us, length us, event | category | flops | bytes accessed | tf_op | source)
XLA Modules:
  0.0 212.6 jit_solution(1480349684459717179)
XLA Ops:
  7.2 3.0 %bitcast_convert_fusion = f32[1024,512]{1,0:T(8,128)} fusion(bf16[1,1024,512]{2,1,0:T(8,128)(2,1)} %param.11), kind=kLoop, calls=%fused_computation.23 | loop fusion | flops 524288 | bytes 3145728 | tf_op jit(solution)/shard_map/convert_element_type | solution.py:83
  14.9 5.0 %all-to-all-start = ((bf16[8,128,1536]{2,1,0:T(8,128)(2,1)}), bf16[8,128,1536]{2,1,0:T(8,128)(2,1)S(1)}, u32[]{:S(2)}, u32[]{:S(2)}) async-start(bf16[8,128,1536]{2,1,0:T(8,128)(2,1)} %pad_maximum_fusion), calls=%async_computation | async-start | bytes 6291456 | tf_op jit(solution)/shard_map/all_to_all | solution.py:115
  20.0 41.4 %reduce-scatter.3.cloned.1.call-done = f32[128,512]{1,0:T(8,128)} async-done(((f32[1024,512]{1,0:T(8,128)}), f32[128,512]{1,0:T(8,128)}) %reduce-scatter.3.cloned.1.call-update) | async-done | bytes 262160 | tf_op jit(solution)/shard_map/reduce_scatter | solution.py:84
  62.3 3.4 %collective-permute-start = (f32[64,512]{1,0:T(8,128)S(1)}, f32[64,512]{1,0:T(8,128)S(1)}, u32[]{:S(2)}, u32[]{:S(2)}) collective-permute-start(f32[64,512]{1,0:T(8,128)S(1)} %constant_dynamic-slice_fusion.4), channel_id=1, source_target_pairs={{0,32},{16,48},{32,0},{48,16},{1,33},{17,49},{33,1},{49,17},{2,34}... | collective-permute-start | bytes 393224 | tf_op jit(solution)/shard_map/ppermute | solution.py:55
  65.7 5.0 %collective-permute-done = f32[64,512]{1,0:T(8,128)S(1)} collective-permute-done((f32[64,512]{1,0:T(8,128)S(1)}, f32[64,512]{1,0:T(8,128)S(1)}, u32[]{:S(2)}, u32[]{:S(2)}) %collective-permute-start) | collective-permute-done | bytes 131104 | tf_op jit(solution)/shard_map/ppermute | solution.py:55
  71.6 2.8 %collective-permute-start.1 = (f32[32,512]{1,0:T(8,128)S(1)}, f32[32,512]{1,0:T(8,128)S(1)}, u32[]{:S(2)}, u32[]{:S(2)}) collective-permute-start(f32[32,512]{1,0:T(8,128)S(1)} %constant_dynamic-slice_fusion.3), channel_id=1, source_target_pairs={{0,16},{16,0},{32,48},{48,32},{1,17},{17,1},{33,49},{49,33},{2,18}... | collective-permute-start | bytes 196616 | tf_op jit(solution)/shard_map/ppermute | solution.py:55
  74.4 3.4 %collective-permute-done.1 = f32[32,512]{1,0:T(8,128)S(1)} collective-permute-done((f32[32,512]{1,0:T(8,128)S(1)}, f32[32,512]{1,0:T(8,128)S(1)}, u32[]{:S(2)}, u32[]{:S(2)}) %collective-permute-start.1) | collective-permute-done | bytes 65568 | tf_op jit(solution)/shard_map/ppermute | solution.py:55
  77.8 7.4 %collective-permute-start.2 = (f32[16,512]{1,0:T(8,128)S(1)}, f32[16,512]{1,0:T(8,128)S(1)}, u32[]{:S(2)}, u32[]{:S(2)}) collective-permute-start(f32[16,512]{1,0:T(8,128)S(1)} %constant_dynamic-slice_fusion.2), channel_id=1, source_target_pairs={{0,8},{8,0},{1,9},{9,1},{2,10},{10,2},{3,11},{11,3},{4,12},{12,4},... | collective-permute-start | bytes 98312 | tf_op jit(solution)/shard_map/ppermute | solution.py:55
  85.2 2.4 %collective-permute-done.2 = f32[16,512]{1,0:T(8,128)S(1)} collective-permute-done((f32[16,512]{1,0:T(8,128)S(1)}, f32[16,512]{1,0:T(8,128)S(1)}, u32[]{:S(2)}, u32[]{:S(2)}) %collective-permute-start.2) | collective-permute-done | bytes 32800 | tf_op jit(solution)/shard_map/ppermute | solution.py:55
  88.3 7.4 %collective-permute-start.3 = (bf16[16,512]{1,0:T(8,128)(2,1)S(1)}, bf16[16,512]{1,0:T(8,128)(2,1)S(1)}, u32[]{:S(2)}, u32[]{:S(2)}) collective-permute-start(bf16[16,512]{1,0:T(8,128)(2,1)S(1)} %get-tuple-element.5), channel_id=1, source_target_pairs={{0,8},{8,0},{1,9},{9,1},{2,10},{10,2},{3,11},{11,3},{4,12},{12,4},... | collective-permute-start | bytes 49160 | tf_op jit(solution)/shard_map/ppermute | solution.py:66
  95.7 2.1 collective-permute-done.3
  97.8 2.8 %collective-permute-start.4 = (bf16[32,512]{1,0:T(8,128)(2,1)S(1)}, bf16[32,512]{1,0:T(8,128)(2,1)S(1)}, u32[]{:S(2)}, u32[]{:S(2)}) collective-permute-start(bf16[32,512]{1,0:T(8,128)(2,1)S(1)} %maximum_select_fusion.2), channel_id=1, source_target_pairs={{0,16},{16,0},{32,48},{48,32},{1,17},{17,1},{33,49},{49,33},{2,18}... | collective-permute-start | bytes 98312 | tf_op jit(solution)/shard_map/ppermute | solution.py:66
  100.6 3.0 %collective-permute-done.4 = bf16[32,512]{1,0:T(8,128)(2,1)S(1)} collective-permute-done((bf16[32,512]{1,0:T(8,128)(2,1)S(1)}, bf16[32,512]{1,0:T(8,128)(2,1)S(1)}, u32[]{:S(2)}, u32[]{:S(2)}) %collective-permute-start.4) | collective-permute-done | bytes 32800 | tf_op jit(solution)/shard_map/ppermute | solution.py:66
  103.6 3.4 %collective-permute-start.5 = (bf16[64,512]{1,0:T(8,128)(2,1)S(1)}, bf16[64,512]{1,0:T(8,128)(2,1)S(1)}, u32[]{:S(2)}, u32[]{:S(2)}) collective-permute-start(bf16[64,512]{1,0:T(8,128)(2,1)S(1)} %maximum_select_fusion.1), channel_id=1, source_target_pairs={{0,32},{16,48},{32,0},{48,16},{1,33},{17,49},{33,1},{49,17},{2,34}... | collective-permute-start | bytes 196616 | tf_op jit(solution)/shard_map/ppermute | solution.py:66
  107.1 4.2 %collective-permute-done.5 = bf16[64,512]{1,0:T(8,128)(2,1)S(1)} collective-permute-done((bf16[64,512]{1,0:T(8,128)(2,1)S(1)}, bf16[64,512]{1,0:T(8,128)(2,1)S(1)}, u32[]{:S(2)}, u32[]{:S(2)}) %collective-permute-start.5) | collective-permute-done | bytes 65568 | tf_op jit(solution)/shard_map/ppermute | solution.py:66
  112.1 2.1 multiply_reduce_fusion
  114.2 18.4 %all-gather.2 = f32[8,1,128]{2,1,0:T(1,128)S(1)} all-gather(f32[1,1,128]{2,1,0:T(1,128)S(1)} %rsqrt_bitcast_fusion), channel_id=2, replica_groups=mesh['island0'=8,'island1'=4,'island2'=2,'fsdp'=8] {'fsdp'}, dimensions={0}, use_global_device_ids=true | all-gather | bytes 4608 | tf_op jit(solution)/shard_map/all_gather | solution.py:122
  132.6 8.9 %all-gather.1 = s32[1,1024]{1,0:T(1,128)S(1)} all-gather(s32[1,128]{1,0:T(1,128)S(1)} %copy-done.9), channel_id=3, replica_groups=mesh['island0'=8,'island1'=4,'island2'=2,'fsdp'=8] {'fsdp'}, dimensions={1}, use_global_device_ids=true | all-gather | bytes 4608 | tf_op jit(solution)/shard_map/all_gather | solution.py:98
  145.3 12.2 %all-gather.5.cloned.1.call-done = bf16[1024,512]{1,0:T(8,128)(2,1)} async-done(((bf16[128,512]{1,0:T(8,128)(2,1)}), bf16[1024,512]{1,0:T(8,128)(2,1)}) %all-gather.5.cloned.1.call-update) | async-done | bytes 1048592 | tf_op jit(solution)/shard_map/all_gather | solution.py:93
  157.4 4.4 %fusion.32 = f32[1024,512]{1,0:T(8,128)} fusion(bf16[1024,1024]{1,0:T(8,128)(2,1)} %fusion.2, bf16[1024,512]{1,0:T(8,128)(2,1)} %all-gather.5.cloned.1.call-done), kind=kOutput, calls=%fused_computation.83 | convolution fusion | flops 1073741824 | bytes 5242880 | tf_op jit(solution)/shard_map/dot_general | solution.py:140
  161.9 3.0 %broadcast_multiply_fusion = (f32[1024,64]{1,0:T(8,128)}, f32[1024,64]{1,0:T(8,128)S(1)}, f32[1024,64]{1,0:T(8,128)S(1)}) fusion(f32[64]{0:T(128)S(1)} %multiply_exponential_fusion, f32[1024]{0:T(1024)S(1)} %subtract_convert_fusion.2), kind=kLoop, calls=%fused_computation.34 | loop fusion | flops 131072 | bytes 790784 | tf_op jit(solution)/shard_map/mul | solution.py:39
  169.3 2.6 %subtract_convert_fusion = (bf16[1024,4,64]{2,1,0:T(4,128)(2,1)S(1)}, bf16[1024,4,64]{2,1,0:T(4,128)(2,1)S(1)}) fusion(f32[1024,4,128]{2,1,0:T(4,128)S(1)} %reshape.137, f32[1024,64]{1,0:T(8,128)} %get-tuple-element.20, f32[1024,64]{1,0:T(8,128)} %copy-done.4), kind=kLoop, calls=%fused_computation.10 | loop fusion | flops 2097152 | bytes 3670016 | tf_op jit(solution)/shard_map/convert.3
  178.4 2.2 %fusion.4 = bf16[1,1024,512]{2,1,0:T(8,128)(2,1)} fusion(bf16[1024,512]{1,0:T(8,128)(2,1)S(1)} %convolution_convert_fusion, bf16[1024,512]{1,0:T(8,128)(2,1)S(1)} %convolution_convert_fusion.1, bf16[1024,512]{1,0:T(8,128)(2,1)S(1)} %convolution_convert_fusion.2, bf16[1024,512]{1,0:T(8,128)(2,1)S(1)} %convolution_convert_fusion.3, ...), kind=kOutput, calls=%fused_computation.19 | convolution fusion | flops 143130624 | bytes 8781824 | tf_op jit(solution)/shard_map/dot_general | solution.py:130
  182.5 21.4 %reduce-scatter.5.cloned.1.call-done = f32[128,512]{1,0:T(8,128)} async-done(((f32[1024,512]{1,0:T(8,128)}), f32[128,512]{1,0:T(8,128)}) %reduce-scatter.5.cloned.1.call-update) | async-done | bytes 262160 | tf_op jit(solution)/shard_map/reduce_scatter | solution.py:141
  (68 shorter events, 26.6 us)
Async XLA Ops:
  7.2 3.1 %copy-start.1 = (bf16[1,128,8192]{2,1,0:T(8,128)(2,1)S(1)}, bf16[1,128,8192]{2,1,0:T(8,128)(2,1)}, u32[]{:S(2)}) copy-start(bf16[1,128,8192]{2,1,0:T(8,128)(2,1)} %param.7) | copy-start | bytes 6291460
  7.2 54.2 %reduce-scatter.3.cloned.1.call-start = ((), (), s32[]{:S(2)}) async-start(), calls=%async_computation.3 | async-start | bytes 2359296 | tf_op jit(solution)/shard_map/reduce_scatter | solution.py:84
  11.7 1.2 copy-start.5
  14.9 72.8 %copy-start.6 = (f32[16,512]{1,0:T(8,128)S(1)}, f32[16,512]{1,0:T(8,128)}, u32[]{:S(2)}) copy-start(f32[16,512]{1,0:T(8,128)} %param.12) | copy-start | bytes 98308
  14.9 72.8 %copy-start.7 = (f32[16,512]{1,0:T(8,128)S(1)}, f32[16,512]{1,0:T(8,128)}, u32[]{:S(2)}) copy-start(f32[16,512]{1,0:T(8,128)} %param.13) | copy-start | bytes 98308
  14.9 97.2 %copy-start.8 = (bf16[1024]{0:T(1024)(128)(2,1)S(1)}, bf16[1024]{0:T(1024)(128)(2,1)}, u32[]{:S(2)}) copy-start(bf16[1024]{0:T(1024)(128)(2,1)} %param.8) | copy-start | bytes 6148
  14.9 126.9 %all-to-all-start = ((bf16[8,128,1536]{2,1,0:T(8,128)(2,1)}), bf16[8,128,1536]{2,1,0:T(8,128)(2,1)S(1)}, u32[]{:S(2)}, u32[]{:S(2)}) async-start(bf16[8,128,1536]{2,1,0:T(8,128)(2,1)} %pad_maximum_fusion), calls=%async_computation | async-start | bytes 6291456 | tf_op jit(solution)/shard_map/all_to_all | solution.py:115
  19.9 112.7 %copy-start.9 = (s32[1,128]{1,0:T(1,128)S(1)}, s32[1,128]{1,0:T(1,128)}, u32[]{:S(2)}) copy-start(s32[1,128]{1,0:T(1,128)} %param.9) | copy-start | bytes 1540
  19.9 137.5 %all-gather.5.cloned.1.call-start = ((), (), s32[]{:S(2)}) async-start(), calls=%async_computation.4 | async-start | bytes 1179648 | tf_op jit(solution)/shard_map/all_gather | solution.py:93
  62.3 8.4 %collective-permute-start = (f32[64,512]{1,0:T(8,128)S(1)}, f32[64,512]{1,0:T(8,128)S(1)}, u32[]{:S(2)}, u32[]{:S(2)}) collective-permute-start(f32[64,512]{1,0:T(8,128)S(1)} %constant_dynamic-slice_fusion.4), channel_id=1, source_target_pairs={{0,32},{16,48},{32,0},{48,16},{1,33},{17,49},{33,1},{49,17},{2,34}... | collective-permute-start | bytes 393224 | tf_op jit(solution)/shard_map/ppermute | solution.py:55
  71.6 6.2 %collective-permute-start.1 = (f32[32,512]{1,0:T(8,128)S(1)}, f32[32,512]{1,0:T(8,128)S(1)}, u32[]{:S(2)}, u32[]{:S(2)}) collective-permute-start(f32[32,512]{1,0:T(8,128)S(1)} %constant_dynamic-slice_fusion.3), channel_id=1, source_target_pairs={{0,16},{16,0},{32,48},{48,32},{1,17},{17,1},{33,49},{49,33},{2,18}... | collective-permute-start | bytes 196616 | tf_op jit(solution)/shard_map/ppermute | solution.py:55
  77.8 9.8 %collective-permute-start.2 = (f32[16,512]{1,0:T(8,128)S(1)}, f32[16,512]{1,0:T(8,128)S(1)}, u32[]{:S(2)}, u32[]{:S(2)}) collective-permute-start(f32[16,512]{1,0:T(8,128)S(1)} %constant_dynamic-slice_fusion.2), channel_id=1, source_target_pairs={{0,8},{8,0},{1,9},{9,1},{2,10},{10,2},{3,11},{11,3},{4,12},{12,4},... | collective-permute-start | bytes 98312 | tf_op jit(solution)/shard_map/ppermute | solution.py:55
  88.3 9.5 %collective-permute-start.3 = (bf16[16,512]{1,0:T(8,128)(2,1)S(1)}, bf16[16,512]{1,0:T(8,128)(2,1)S(1)}, u32[]{:S(2)}, u32[]{:S(2)}) collective-permute-start(bf16[16,512]{1,0:T(8,128)(2,1)S(1)} %get-tuple-element.5), channel_id=1, source_target_pairs={{0,8},{8,0},{1,9},{9,1},{2,10},{10,2},{3,11},{11,3},{4,12},{12,4},... | collective-permute-start | bytes 49160 | tf_op jit(solution)/shard_map/ppermute | solution.py:66
  97.8 5.8 %collective-permute-start.4 = (bf16[32,512]{1,0:T(8,128)(2,1)S(1)}, bf16[32,512]{1,0:T(8,128)(2,1)S(1)}, u32[]{:S(2)}, u32[]{:S(2)}) collective-permute-start(bf16[32,512]{1,0:T(8,128)(2,1)S(1)} %maximum_select_fusion.2), channel_id=1, source_target_pairs={{0,16},{16,0},{32,48},{48,32},{1,17},{17,1},{33,49},{49,33},{2,18}... | collective-permute-start | bytes 98312 | tf_op jit(solution)/shard_map/ppermute | solution.py:66
  103.6 7.7 %collective-permute-start.5 = (bf16[64,512]{1,0:T(8,128)(2,1)S(1)}, bf16[64,512]{1,0:T(8,128)(2,1)S(1)}, u32[]{:S(2)}, u32[]{:S(2)}) collective-permute-start(bf16[64,512]{1,0:T(8,128)(2,1)S(1)} %maximum_select_fusion.1), channel_id=1, source_target_pairs={{0,32},{16,48},{32,0},{48,16},{1,33},{17,49},{33,1},{49,17},{2,34}... | collective-permute-start | bytes 196616 | tf_op jit(solution)/shard_map/ppermute | solution.py:66
  112.0 91.8 %reduce-scatter.5.cloned.1.call-start = ((), (), s32[]{:S(2)}) async-start(), calls=%async_computation.5 | async-start | bytes 2359296 | tf_op jit(solution)/shard_map/reduce_scatter | solution.py:141
  142.0 1.3 copy-start.2
  164.9 0.8 copy-start.4
  173.4 1.8 copy-start
  178.4 2.2 %copy-start.3 = (bf16[8,128,1024]{2,1,0:T(8,128)(2,1)S(1)}, bf16[8,128,1024]{2,1,0:T(8,128)(2,1)}, u32[]{:S(2)}) copy-start(bf16[8,128,1024]{2,1,0:T(8,128)(2,1)} %copy-done.2) | copy-start | bytes 6291460
  178.4 2.2 %copy-start.10 = (bf16[1024,512]{1,0:T(8,128)(2,1)S(1)}, bf16[1024,512]{1,0:T(8,128)(2,1)}, u32[]{:S(2)}) copy-start(bf16[1024,512]{1,0:T(8,128)(2,1)} %all-gather.5.cloned.1.call-done) | copy-start | bytes 3145732
Sparse Core Ops, SparseCore 0:
  10.8 50.5 reduce-scatter.2
  112.1 45.2 all-gather.4
  162.0 41.7 reduce-scatter.4

commit v4 on v3

--- a/solution.py
+++ b/solution.py
@@ -74,6 +74,13 @@
     return values
 
 
+def gather_by_all_to_all(values, axis):
+    n = lax.axis_size(axis)
+    repeated = jnp.broadcast_to(values[None], (n,) + values.shape)
+    arrived = lax.all_to_all(repeated, axis, split_axis=0, concat_axis=0, tiled=True)
+    return arrived.reshape((n * values.shape[0],) + values.shape[1:])
+
+
 def body(island_axes, hidden, gain, doc_ids, cotangent, pseudo_grad, outer_weight, momentum):
     islands = 1
     for ax in island_axes:
@@ -90,36 +97,45 @@
     weight_shard = new_outer.astype(jnp.bfloat16)
     for ax in reversed(island_axes[1:]):
         weight_shard = doubling_gather(weight_shard, ax)
-    weight_shard = lax.all_gather(weight_shard, island_axes[0], axis=0, tiled=True)
+    weight_shard = gather_by_all_to_all(weight_shard, island_axes[0])
 
     tok_rows = hidden.shape[1]
     seq = tok_rows * fsdp_ways
     me = lax.axis_index("fsdp")
-    all_docs = lax.all_gather(doc_ids[0], "fsdp", axis=0, tiled=True)
     indices = jnp.arange(seq, dtype=jnp.int32)
     documents = jnp.arange(DOCS, dtype=jnp.int32)
+    hidden_f = hidden[0].astype(jnp.float32)
+    row_scale = lax.rsqrt(jnp.mean(hidden_f * hidden_f, axis=1, keepdims=True) + norm_eps)
+    width = hidden.shape[2] // fsdp_ways
+    cols_out = cotangent.shape[2]
+    scale_high = lax.reduce_precision(row_scale, exponent_bits=8, mantissa_bits=7)
+    scale_mid = lax.reduce_precision(row_scale - scale_high, exponent_bits=8, mantissa_bits=7)
+    scale_low = row_scale - scale_high - scale_mid
+    extras = jnp.concatenate(
+        [doc_ids[0][:, None].astype(jnp.float32), scale_high, scale_mid, scale_low], axis=1
+    ).astype(jnp.bfloat16)
+    extras = jnp.pad(extras, ((0, 0), (0, 128 - extras.shape[1])))
+    outgoing = jnp.concatenate(
+        [
+            hidden[0].reshape(tok_rows, fsdp_ways, width).transpose(1, 0, 2),
+            jnp.broadcast_to(cotangent[0][None], (fsdp_ways, tok_rows, cols_out)),
+            jnp.broadcast_to(extras[None], (fsdp_ways,) + extras.shape),
+        ],
+        axis=2,
+    )
+    incoming = lax.all_to_all(outgoing, "fsdp", split_axis=0, concat_axis=0, tiled=True)
+    columns = incoming[:, :, :width].reshape(seq, width)
+    all_cot = incoming[:, :, width : width + cols_out].reshape(seq, cols_out)
+    all_extras = incoming[:, :, width + cols_out :].reshape(seq, -1).astype(jnp.float32)
+    all_docs = all_extras[:, 0].astype(jnp.int32)
+    all_scales = (all_extras[:, 1:2] + all_extras[:, 2:3]) + all_extras[:, 3:4]
     in_document = all_docs[:, None] == documents[None, :]
     starts = jnp.min(jnp.where(in_document, indices[:, None], far_index), axis=0)
     doc_start = jnp.sum(jnp.where(in_document, starts[None, :], 0), axis=1)
     positions = (indices - doc_start).astype(jnp.float32)
     cosine, sine_part = angles_for(positions, HEAD)
-    width = hidden.shape[2] // fsdp_ways
-    cols_out = cotangent.shape[2]
-    outgoing = jnp.concatenate(
-        [
-            hidden[0].reshape(tok_rows, fsdp_ways, width).transpose(1, 0, 2),
-            jnp.broadcast_to(cotangent[0][None], (fsdp_ways, tok_rows, cols_out)),
-        ],
-        axis=2,
-    )
-    incoming = lax.all_to_all(outgoing, "fsdp", split_axis=0, concat_axis=0, tiled=True)
-    columns = incoming[:, :, :width].reshape(seq, width)
-    all_cot = incoming[:, :, width:].reshape(seq, cols_out)
     all_back = rotate(all_cot.astype(jnp.float32), cosine, sine_part, -1.0).astype(jnp.bfloat16)
 
-    hidden_f = hidden[0].astype(jnp.float32)
-    row_scale = lax.rsqrt(jnp.mean(hidden_f * hidden_f, axis=1, keepdims=True) + norm_eps)
-    all_scales = lax.all_gather(row_scale, "fsdp", axis=0, tiled=True)
     normed_cols = columns.astype(jnp.float32) * all_scales
     act_cols = (normed_cols * gain.astype(jnp.float32)[None, :]).astype(jnp.bfloat16)
 
@@ -138,7 +154,9 @@
     grad_gain = jnp.sum(hidden_grad * normed_cols, axis=0)
 
     partial_keys = jnp.dot(act_cols, weight_shard, preferred_element_type=jnp.float32)
-    projected = lax.psum_scatter(partial_keys, "fsdp", scatter_dimension=0, tiled=True)
+    projected = lax.psum_scatter(
+        partial_keys.astype(jnp.bfloat16), "fsdp", scatter_dimension=0, tiled=True
+    ).astype(jnp.float32)
     my_cos = lax.dynamic_slice_in_dim(cosine, me * tok_rows, tok_rows, axis=0)
     my_sin = lax.dynamic_slice_in_dim(sine_part, me * tok_rows, tok_rows, axis=0)
     rotated = rotate(projected, my_cos, my_sin, 1.0).astype(jnp.bfloat16)

time: 213 us -> 219 us (1.028)
  blocking collectives: 27.3 us -> 0 us
  waiting for transfers between devices: 95.1 us -> 104 us
  local copies, waits for them, and re-layouts: 10 us -> 18.7 us
  other arithmetic: 22 us -> 28.2 us
  starting transfers between devices: 32.2 us -> 36.5 us
  matrix products: 11.7 us -> 15.8 us
    all_gather x2 -> x0, blocking collectives: 27.3 us -> none  [the longest x1 18.4 us: body(): all_scales = lax.all_gather(row_scale, 'fsdp', axis=0, tiled=True)]
    all_gather x1 -> x0, waiting for transfers between devices: 12.2 us -> none  [body(): lax.all_gather(weight_shard, island_axes[0], axis=0, tiled=True)]
    reduce_scatter x1, waiting for transfers between devices: 21.4 us -> 32.9 us  [body(): lax.psum_scatter(partial_keys.astype(jnp.bfloat16), 'fsdp', scatter_dimen...]
    reduce_scatter x1, waiting for transfers between devices: 41.4 us -> 50.5 us  [body(): lax.psum_scatter(summed, island_axes[0], scatter_dimension=0, tiled=True)]
    convert_element_type x0 -> x4, other arithmetic: none -> 5.63 us  [the longest x1 2.97 us: body(): rotate(all_cot.astype(jnp.float32), cosine, sine_part, -1.0)]
    sub x0 -> x1, other arithmetic: none -> 4.8 us  [rotate(): leading * cos_b - second * sin_b]
    all_to_all x0 -> x1, starting transfers between devices: none -> 4.41 us  [gather_by_all_to_all(): lax.all_to_all(repeated, axis, split_axis=0, concat_axis=0, tiled=True)]
    unnamed x23 -> x38, local copies, waits for them, and re-layouts: 3.89 us -> 7.85 us
  transfers between devices with their start and end apart: 10 -> 10, of which waited for: 9 -> 8; matrix products, arithmetic and copies ran while one was open for 15% -> 21% of each run, Pallas kernels for 0% -> 0%
where the time goes in v4:
time: 219 us; the launch traced here: 218 us
  waiting for transfers between devices  104 us (47%)
  starting transfers between devices  36.5 us (17%)
  other arithmetic  28.2 us (13%)
  local copies, waits for them, and re-layouts  18.7 us (9%)
  matrix products  15.8 us (7%)
  between operations  14.6 us (7%)
    reduce_scatter x1, waiting for transfers between devices, body(): lax.psum_scatter(summed, island_axes[0], scatter_dimension=0, tiled=True)  50.5 us
    reduce_scatter x1, waiting for transfers between devices, body(): lax.psum_scatter(partial_keys.astype(jnp.bfloat16), 'fsdp', scatter_dimen...  32.9 us
    ppermute x3, starting transfers between devices, doubling_gather(): got = lax.ppermute(values, axis, [(j, j ^ step) for j in range(n)])  13.6 us
    ppermute x3, starting transfers between devices, halving_scatter(): got = lax.ppermute(send, axis, [(j, j ^ step) for j in range(n)])  13.5 us
    ppermute x3, waiting for transfers between devices, halving_scatter(): got = lax.ppermute(send, axis, [(j, j ^ step) for j in range(n)])  11.1 us
    ppermute x3, waiting for transfers between devices, doubling_gather(): got = lax.ppermute(values, axis, [(j, j ^ step) for j in range(n)])  9.3 us
    dot_general x8, matrix products, body(): lax.dot_general(act_block, back_block, (((0,), (0,)), ((), ())), preferre...  8.53 us
    unnamed x38, local copies, waits for them, and re-layouts  7.85 us
  transfers between devices with their start and end apart: 10, of which 8 were waited for; matrix products, arithmetic and copies ran while one was open for 21% of the time, Pallas kernels for 0%

profile of v4, /device:TPU:6, one launch (start us, length us, event | category | flops | bytes accessed | tf_op | source)
XLA Modules:
  0.0 217.6 jit_solution(14501565857006387728)
XLA Ops:
  14.8 4.9 %all-to-all-start = ((bf16[8,128,1664]{2,1,0:T(8,128)(2,1)}), bf16[8,128,1664]{2,1,0:T(8,128)(2,1)S(1)}, u32[]{:S(2)}, u32[]{:S(2)}) async-start(bf16[8,128,1664]{2,1,0:T(8,128)(2,1)} %pad_maximum_fusion), calls=%async_computation | async-start | bytes 6815744 | tf_op jit(solution)/shard_map/all_to_all | solution.py:126
  19.8 2.8 %bitcast_convert_fusion = f32[1024,512]{1,0:T(8,128)} fusion(bf16[1,1024,512]{2,1,0:T(8,128)(2,1)} %param.11), kind=kLoop, calls=%fused_computation.24 | loop fusion | flops 524288 | bytes 3145728 | tf_op jit(solution)/shard_map/convert_element_type | solution.py:90
  22.7 50.5 %reduce-scatter.3.cloned.1.call-done = f32[128,512]{1,0:T(8,128)} async-done(((f32[1024,512]{1,0:T(8,128)}), f32[128,512]{1,0:T(8,128)}) %reduce-scatter.3.cloned.1.call-update) | async-done | bytes 262160 | tf_op jit(solution)/shard_map/reduce_scatter | solution.py:91
  74.1 3.4 %collective-permute-start = (f32[64,512]{1,0:T(8,128)S(1)}, f32[64,512]{1,0:T(8,128)}, u32[]{:S(2)}, u32[]{:S(2)}) collective-permute-start(f32[64,512]{1,0:T(8,128)S(1)} %constant_dynamic-slice_fusion.4), channel_id=1, source_target_pairs={{0,32},{16,48},{32,0},{48,16},{1,33},{17,49},{33,1},{49,17},{2,34}... | collective-permute-start | bytes 393224 | tf_op jit(solution)/shard_map/ppermute | solution.py:55
  77.5 5.1 %collective-permute-done = f32[64,512]{1,0:T(8,128)} collective-permute-done((f32[64,512]{1,0:T(8,128)S(1)}, f32[64,512]{1,0:T(8,128)}, u32[]{:S(2)}, u32[]{:S(2)}) %collective-permute-start) | collective-permute-done | bytes 131104 | tf_op jit(solution)/shard_map/ppermute | solution.py:55
  84.2 2.8 %collective-permute-start.1 = (f32[32,512]{1,0:T(8,128)}, f32[32,512]{1,0:T(8,128)}, u32[]{:S(2)}, u32[]{:S(2)}) collective-permute-start(f32[32,512]{1,0:T(8,128)} %constant_dynamic-slice_fusion.3), channel_id=1, source_target_pairs={{0,16},{16,0},{32,48},{48,32},{1,17},{17,1},{33,49},{49,33},{2,18}... | collective-permute-start | bytes 196616 | tf_op jit(solution)/shard_map/ppermute | solution.py:55
  87.0 3.7 %collective-permute-done.1 = f32[32,512]{1,0:T(8,128)} collective-permute-done((f32[32,512]{1,0:T(8,128)}, f32[32,512]{1,0:T(8,128)}, u32[]{:S(2)}, u32[]{:S(2)}) %collective-permute-start.1) | collective-permute-done | bytes 65568 | tf_op jit(solution)/shard_map/ppermute | solution.py:55
  92.2 7.4 %collective-permute-start.2 = (f32[16,512]{1,0:T(8,128)S(1)}, f32[16,512]{1,0:T(8,128)S(1)}, u32[]{:S(2)}, u32[]{:S(2)}) collective-permute-start(f32[16,512]{1,0:T(8,128)S(1)} %constant_dynamic-slice_fusion.2), channel_id=1, source_target_pairs={{0,8},{8,0},{1,9},{9,1},{2,10},{10,2},{3,11},{11,3},{4,12},{12,4},... | collective-permute-start | bytes 98312 | tf_op jit(solution)/shard_map/ppermute | solution.py:55
  99.6 2.4 %collective-permute-done.2 = f32[16,512]{1,0:T(8,128)S(1)} collective-permute-done((f32[16,512]{1,0:T(8,128)S(1)}, f32[16,512]{1,0:T(8,128)S(1)}, u32[]{:S(2)}, u32[]{:S(2)}) %collective-permute-start.2) | collective-permute-done | bytes 32800 | tf_op jit(solution)/shard_map/ppermute | solution.py:55
  103.3 7.4 %collective-permute-start.3 = (bf16[16,512]{1,0:T(8,128)(2,1)S(1)}, bf16[16,512]{1,0:T(8,128)(2,1)S(1)}, u32[]{:S(2)}, u32[]{:S(2)}) collective-permute-start(bf16[16,512]{1,0:T(8,128)(2,1)S(1)} %get-tuple-element.5), channel_id=1, source_target_pairs={{0,8},{8,0},{1,9},{9,1},{2,10},{10,2},{3,11},{11,3},{4,12},{12,4},... | collective-permute-start | bytes 49160 | tf_op jit(solution)/shard_map/ppermute | solution.py:66
  110.7 2.1 collective-permute-done.3
  112.9 2.8 %collective-permute-start.4 = (bf16[32,512]{1,0:T(8,128)(2,1)S(1)}, bf16[32,512]{1,0:T(8,128)(2,1)S(1)}, u32[]{:S(2)}, u32[]{:S(2)}) collective-permute-start(bf16[32,512]{1,0:T(8,128)(2,1)S(1)} %maximum_select_fusion.2), channel_id=1, source_target_pairs={{0,16},{16,0},{32,48},{48,32},{1,17},{17,1},{33,49},{49,33},{2,18}... | collective-permute-start | bytes 98312 | tf_op jit(solution)/shard_map/ppermute | solution.py:66
  115.7 3.0 %collective-permute-done.4 = bf16[32,512]{1,0:T(8,128)(2,1)S(1)} collective-permute-done((bf16[32,512]{1,0:T(8,128)(2,1)S(1)}, bf16[32,512]{1,0:T(8,128)(2,1)S(1)}, u32[]{:S(2)}, u32[]{:S(2)}) %collective-permute-start.4) | collective-permute-done | bytes 32800 | tf_op jit(solution)/shard_map/ppermute | solution.py:66
  118.7 3.5 %collective-permute-start.5 = (bf16[64,512]{1,0:T(8,128)(2,1)S(1)}, bf16[64,512]{1,0:T(8,128)(2,1)S(1)}, u32[]{:S(2)}, u32[]{:S(2)}) collective-permute-start(bf16[64,512]{1,0:T(8,128)(2,1)S(1)} %maximum_select_fusion.1), channel_id=1, source_target_pairs={{0,32},{16,48},{32,0},{48,16},{1,33},{17,49},{33,1},{49,17},{2,34}... | collective-permute-start | bytes 196616 | tf_op jit(solution)/shard_map/ppermute | solution.py:66
  122.2 4.1 %collective-permute-done.5 = bf16[64,512]{1,0:T(8,128)(2,1)S(1)} collective-permute-done((bf16[64,512]{1,0:T(8,128)(2,1)S(1)}, bf16[64,512]{1,0:T(8,128)(2,1)S(1)}, u32[]{:S(2)}, u32[]{:S(2)}) %collective-permute-start.5) | collective-permute-done | bytes 65568 | tf_op jit(solution)/shard_map/ppermute | solution.py:66
  127.6 4.4 %all-to-all-start.1 = ((bf16[8,128,512]{2,1,0:T(8,128)(2,1)}), bf16[8,128,512]{2,1,0:T(8,128)(2,1)}, u32[]{:S(2)}, u32[]{:S(2)}) async-start(bf16[8,128,512]{2,1,0:T(8,128)(2,1)} %broadcast_in_dim.39), calls=%async_computation.2 | async-start | bytes 2097152 | tf_op jit(solution)/shard_map/all_to_all | solution.py:80
  137.0 2.9 %reshape.252 = f32[1024,4,128]{2,1,0:T(4,128)} reshape(f32[8,128,512]{2,1,0:T(8,128)} %slice_convert_fusion) | data formatting | bytes 4194304 | tf_op jit(solution)/shard_map/convert_element_type | solution.py:137
  139.9 3.0 %broadcast_multiply_fusion = (f32[1024,64]{1,0:T(8,128)S(1)}, f32[1024,64]{1,0:T(8,128)}, f32[1024,64]{1,0:T(8,128)S(1)}) fusion(f32[64]{0:T(128)S(1)} %multiply_exponential_fusion, f32[1024]{0:T(1024)S(1)} %subtract_convert_fusion.1), kind=kLoop, calls=%fused_computation.37 | loop fusion | flops 131072 | bytes 790784 | tf_op jit(solution)/shard_map/mul | solution.py:39
  142.9 4.8 %multiply_subtract_fusion = (bf16[1024,4,64]{2,1,0:T(4,128)(2,1)}, bf16[1024,4,64]{2,1,0:T(4,128)(2,1)}) fusion(f32[1024,4,128]{2,1,0:T(4,128)} %reshape.252, f32[1024,64]{1,0:T(8,128)S(1)} %get-tuple-element.24, f32[1024,64]{1,0:T(8,128)S(1)} %get-tuple-element.26), kind=kLoop, calls=%fused_computation.10 | loop fusion | flops 2097152 | bytes 3670016 | tf_op jit(solution)/shard_map/sub | solution.py:41
  151.4 3.0 %maximum_convert_fusion = bf16[1024,4,128]{2,1,0:T(4,128)(2,1)S(1)} fusion(bf16[1024,4,64]{2,1,0:T(4,128)(2,1)} %get-tuple-element.9, bf16[1024,4,64]{2,1,0:T(4,128)(2,1)} %get-tuple-element.8), kind=kLoop, calls=%fused_computation.6 | loop fusion | flops 2097152 | bytes 2097152 | tf_op jit(solution)/shard_map/convert_element_type | solution.py:137
  161.0 4.1 %convolution_convert_fusion.8 = bf16[1024,512]{1,0:T(8,128)(2,1)} fusion(bf16[1024,1024]{1,0:T(8,128)(2,1)} %bitcast.79, bf16[1024,512]{1,0:T(8,128)(2,1)} %bitcast.9), kind=kOutput, calls=%fused_computation.19 | convolution fusion | flops 1074266112 | bytes 4194304 | tf_op jit(solution)/shard_map/dot_general | solution.py:156
  170.3 2.2 fusion
  172.5 3.1 %multiply_reduce_fusion = f32[1024]{0:T(1024)} fusion(bf16[8,128,1024]{2,1,0:T(8,128)(2,1)S(1)} %slice-done, bf16[1024,512]{1,0:T(8,128)(2,1)} %bitcast.9, f32[1024]{0:T(1024)S(1)} %bitcast.93, bf16[128,8,4,128]{3,2,1,0:T(4,128)(2,1)S(1)} %bitcast.78), kind=kOutput, calls=%fused_computation.1 | convolution fusion | flops 1077935104 | bytes 4202496 | tf_op jit(solution)/shard_map/dot_general | solution.py:151
  175.6 32.9 %reduce-scatter.5.cloned.1.call-done = bf16[128,512]{1,0:T(8,128)(2,1)} async-done(((bf16[1024,512]{1,0:T(8,128)(2,1)}), bf16[128,512]{1,0:T(8,128)(2,1)}) %reduce-scatter.5.cloned.1.call-update) | async-done | bytes 131088 | tf_op jit(solution)/shard_map/reduce_scatter | solution.py:157
  (90 shorter events, 36.9 us)
Async XLA Ops:
  7.2 3.1 %copy-start.3 = (bf16[1,128,8192]{2,1,0:T(8,128)(2,1)S(1)}, bf16[1,128,8192]{2,1,0:T(8,128)(2,1)}, u32[]{:S(2)}) copy-start(bf16[1,128,8192]{2,1,0:T(8,128)(2,1)} %param.7) | copy-start | bytes 6291460
  14.8 111.6 %all-to-all-start = ((bf16[8,128,1664]{2,1,0:T(8,128)(2,1)}), bf16[8,128,1664]{2,1,0:T(8,128)(2,1)S(1)}, u32[]{:S(2)}, u32[]{:S(2)}) async-start(bf16[8,128,1664]{2,1,0:T(8,128)(2,1)} %pad_maximum_fusion), calls=%async_computation | async-start | bytes 6815744 | tf_op jit(solution)/shard_map/all_to_all | solution.py:126
  19.7 53.5 %reduce-scatter.3.cloned.1.call-start = ((), (), s32[]{:S(2)}) async-start(), calls=%async_computation.4 | async-start | bytes 2359296 | tf_op jit(solution)/shard_map/reduce_scatter | solution.py:91
  22.6 93.1 %copy-start.15 = (bf16[1024]{0:T(1024)(128)(2,1)S(1)}, bf16[1024]{0:T(1024)(128)(2,1)}, u32[]{:S(2)}) copy-start(bf16[1024]{0:T(1024)(128)(2,1)} %param.8) | copy-start | bytes 6148
  74.1 8.5 %collective-permute-start = (f32[64,512]{1,0:T(8,128)S(1)}, f32[64,512]{1,0:T(8,128)}, u32[]{:S(2)}, u32[]{:S(2)}) collective-permute-start(f32[64,512]{1,0:T(8,128)S(1)} %constant_dynamic-slice_fusion.4), channel_id=1, source_target_pairs={{0,32},{16,48},{32,0},{48,16},{1,33},{17,49},{33,1},{49,17},{2,34}... | collective-permute-start | bytes 393224 | tf_op jit(solution)/shard_map/ppermute | solution.py:55
  84.2 6.5 %collective-permute-start.1 = (f32[32,512]{1,0:T(8,128)}, f32[32,512]{1,0:T(8,128)}, u32[]{:S(2)}, u32[]{:S(2)}) collective-permute-start(f32[32,512]{1,0:T(8,128)} %constant_dynamic-slice_fusion.3), channel_id=1, source_target_pairs={{0,16},{16,0},{32,48},{48,32},{1,17},{17,1},{33,49},{49,33},{2,18}... | collective-permute-start | bytes 196616 | tf_op jit(solution)/shard_map/ppermute | solution.py:55
  92.2 9.7 %collective-permute-start.2 = (f32[16,512]{1,0:T(8,128)S(1)}, f32[16,512]{1,0:T(8,128)S(1)}, u32[]{:S(2)}, u32[]{:S(2)}) collective-permute-start(f32[16,512]{1,0:T(8,128)S(1)} %constant_dynamic-slice_fusion.2), channel_id=1, source_target_pairs={{0,8},{8,0},{1,9},{9,1},{2,10},{10,2},{3,11},{11,3},{4,12},{12,4},... | collective-permute-start | bytes 98312 | tf_op jit(solution)/shard_map/ppermute | solution.py:55
  103.3 9.5 %collective-permute-start.3 = (bf16[16,512]{1,0:T(8,128)(2,1)S(1)}, bf16[16,512]{1,0:T(8,128)(2,1)S(1)}, u32[]{:S(2)}, u32[]{:S(2)}) collective-permute-start(bf16[16,512]{1,0:T(8,128)(2,1)S(1)} %get-tuple-element.5), channel_id=1, source_target_pairs={{0,8},{8,0},{1,9},{9,1},{2,10},{10,2},{3,11},{11,3},{4,12},{12,4},... | collective-permute-start | bytes 49160 | tf_op jit(solution)/shard_map/ppermute | solution.py:66
  112.9 5.8 %collective-permute-start.4 = (bf16[32,512]{1,0:T(8,128)(2,1)S(1)}, bf16[32,512]{1,0:T(8,128)(2,1)S(1)}, u32[]{:S(2)}, u32[]{:S(2)}) collective-permute-start(bf16[32,512]{1,0:T(8,128)(2,1)S(1)} %maximum_select_fusion.2), channel_id=1, source_target_pairs={{0,16},{16,0},{32,48},{48,32},{1,17},{17,1},{33,49},{49,33},{2,18}... | collective-permute-start | bytes 98312 | tf_op jit(solution)/shard_map/ppermute | solution.py:66
  118.7 7.7 %collective-permute-start.5 = (bf16[64,512]{1,0:T(8,128)(2,1)S(1)}, bf16[64,512]{1,0:T(8,128)(2,1)S(1)}, u32[]{:S(2)}, u32[]{:S(2)}) collective-permute-start(bf16[64,512]{1,0:T(8,128)(2,1)S(1)} %maximum_select_fusion.1), channel_id=1, source_target_pairs={{0,32},{16,48},{32,0},{48,16},{1,33},{17,49},{33,1},{49,17},{2,34}... | collective-permute-start | bytes 196616 | tf_op jit(solution)/shard_map/ppermute | solution.py:66
  126.4 40.2 %copy-start = (bf16[8,128,1664]{2,1,0:T(8,128)(2,1)}, bf16[8,128,1664]{2,1,0:T(8,128)(2,1)S(1)}, u32[]{:S(2)}) copy-start(bf16[8,128,1664]{2,1,0:T(8,128)(2,1)S(1)} %all-to-all-done) | copy-start | bytes 10223620
  127.6 33.5 %all-to-all-start.1 = ((bf16[8,128,512]{2,1,0:T(8,128)(2,1)}), bf16[8,128,512]{2,1,0:T(8,128)(2,1)}, u32[]{:S(2)}, u32[]{:S(2)}) async-start(bf16[8,128,512]{2,1,0:T(8,128)(2,1)} %broadcast_in_dim.39), calls=%async_computation.2 | async-start | bytes 2097152 | tf_op jit(solution)/shard_map/all_to_all | solution.py:80
  132.0 76.6 %reduce-scatter.5.cloned.1.call-start = ((), (), s32[]{:S(2)}) async-start(), calls=%async_computation.5 | async-start | bytes 1179648 | tf_op jit(solution)/shard_map/reduce_scatter | solution.py:157
  142.9 4.8 %copy-start.8 = (f32[1024,64]{1,0:T(8,128)}, f32[1024,64]{1,0:T(8,128)S(1)}, u32[]{:S(2)}) copy-start(f32[1024,64]{1,0:T(8,128)S(1)} %get-tuple-element.26) | copy-start | bytes 786436
  156.1 1.7 copy-start.1
  166.6 1.7 copy-start.2
  166.6 1.6 copy-start.12
  166.6 2.1 copy-start.11
  166.7 2.6 %copy-start.10 = (bf16[128,4,128]{2,1,0:T(4,128)(2,1)S(1)}, bf16[128,4,128]{2,1,0:T(4,128)(2,1)}, u32[]{:S(2)}) copy-start(bf16[128,4,128]{2,1,0:T(4,128)(2,1)} %get-tuple-element.16) | copy-start | bytes 393220
  168.3 1.4 copy-start.9
  168.8 1.4 copy-start.6
  168.8 1.5 copy-start.7
  170.3 2.2 slice-start
  170.3 2.2 copy-start.5
  (3 other events, 3.0 us)
Sparse Core Ops, SparseCore 0:
  23.4 49.7 reduce-scatter.2
  165.3 43.1 reduce-scatter.4

commit v5 on v4

--- a/solution.py
+++ b/solution.py
@@ -74,11 +74,11 @@
     return values
 
 
-def gather_by_all_to_all(values, axis):
+def scatter_by_all_to_all(values, axis):
     n = lax.axis_size(axis)
-    repeated = jnp.broadcast_to(values[None], (n,) + values.shape)
-    arrived = lax.all_to_all(repeated, axis, split_axis=0, concat_axis=0, tiled=True)
-    return arrived.reshape((n * values.shape[0],) + values.shape[1:])
+    blocks = values.reshape((n, values.shape[0] // n) + values.shape[1:])
+    arrived = lax.all_to_all(blocks, axis, split_axis=0, concat_axis=0, tiled=True)
+    return jnp.sum(arrived.astype(jnp.float32), axis=0)
 
 
 def body(island_axes, hidden, gain, doc_ids, cotangent, pseudo_grad, outer_weight, momentum):
@@ -87,8 +87,8 @@
         islands *= lax.axis_size(ax)
     fsdp_ways = lax.axis_size("fsdp")
 
-    summed = pseudo_grad[0].astype(jnp.float32)
-    summed = lax.psum_scatter(summed, island_axes[0], scatter_dimension=0, tiled=True)
+    first_stage = scatter_by_all_to_all(pseudo_grad[0], island_axes[0])
+    summed = first_stage
     for ax in island_axes[1:]:
         summed = halving_scatter(summed, ax)
     mean_delta = summed / islands
@@ -97,7 +97,7 @@
     weight_shard = new_outer.astype(jnp.bfloat16)
     for ax in reversed(island_axes[1:]):
         weight_shard = doubling_gather(weight_shard, ax)
-    weight_shard = gather_by_all_to_all(weight_shard, island_axes[0])
+    weight_shard = lax.all_gather(weight_shard, island_axes[0], axis=0, tiled=True)
 
     tok_rows = hidden.shape[1]
     seq = tok_rows * fsdp_ways
@@ -123,6 +123,7 @@
         ],
         axis=2,
     )
+    _, outgoing = lax.optimization_barrier((first_stage, outgoing))
     incoming = lax.all_to_all(outgoing, "fsdp", split_axis=0, concat_axis=0, tiled=True)
     columns = incoming[:, :, :width].reshape(seq, width)
     all_cot = incoming[:, :, width : width + cols_out].reshape(seq, cols_out)
@@ -154,9 +155,7 @@
     grad_gain = jnp.sum(hidden_grad * normed_cols, axis=0)
 
     partial_keys = jnp.dot(act_cols, weight_shard, preferred_element_type=jnp.float32)
-    projected = lax.psum_scatter(
-        partial_keys.astype(jnp.bfloat16), "fsdp", scatter_dimension=0, tiled=True
-    ).astype(jnp.float32)
+    projected = lax.psum_scatter(partial_keys, "fsdp", scatter_dimension=0, tiled=True)
     my_cos = lax.dynamic_slice_in_dim(cosine, me * tok_rows, tok_rows, axis=0)
     my_sin = lax.dynamic_slice_in_dim(sine_part, me * tok_rows, tok_rows, axis=0)
     rotated = rotate(projected, my_cos, my_sin, 1.0).astype(jnp.bfloat16)

time: 219 us -> 233 us (1.064)
  waiting for transfers between devices: 104 us -> 132 us
  other arithmetic: 28.2 us -> 19.8 us
  matrix products: 15.8 us -> 11.7 us
  local copies, waits for them, and re-layouts: 18.7 us -> 16 us
    reduce_scatter x2 -> x1, waiting for transfers between devices: 83.4 us -> 23.6 us  [body(): lax.psum_scatter(partial_keys, 'fsdp', scatter_dimension=0, tiled=True)]
    ppermute x3, waiting for transfers between devices: 11.1 us -> 46 us  [halving_scatter(): got = lax.ppermute(send, axis, [(j, j ^ step) for j in range(n)])]
    all_gather x0 -> x1, waiting for transfers between devices: none -> 25.3 us  [body(): lax.all_gather(weight_shard, island_axes[0], axis=0, tiled=True)]
    all_to_all x1, waiting for transfers between devices: 0.01 us -> 23.4 us  [scatter_by_all_to_all(): lax.all_to_all(blocks, axis, split_axis=0, concat_axis=0, tiled=True)]
    all_to_all x1, starting transfers between devices: 4.41 us -> 10.5 us  [scatter_by_all_to_all(): lax.all_to_all(blocks, axis, split_axis=0, concat_axis=0, tiled=True)]
    convert_element_type x2 -> x0, other arithmetic: 5.81 us -> none  [the longest x1 2.97 us: body(): rotate(all_cot.astype(jnp.float32), cosine, sine_part, -1.0)]
    sub x1 -> x0, other arithmetic: 4.8 us -> none  [rotate(): leading * cos_b - second * sin_b]
    ppermute x3, waiting for transfers between devices: 9.3 us -> 13.9 us  [doubling_gather(): got = lax.ppermute(values, axis, [(j, j ^ step) for j in range(n)])]
  transfers between devices with their start and end apart: 10 -> 10, of which waited for: 8 -> 9; matrix products, arithmetic and copies ran while one was open for 21% -> 16% of each run, Pallas kernels for 0% -> 0%
where the time goes in v5:
time: 233 us; the launch traced here: 231 us
  waiting for transfers between devices  132 us (57%)
  starting transfers between devices  37.2 us (16%)
  other arithmetic  19.8 us (8%)
  local copies, waits for them, and re-layouts  16 us (7%)
  between operations  14.5 us (6%)
  matrix products  11.7 us (5%)
    ppermute x3, waiting for transfers between devices, halving_scatter(): got = lax.ppermute(send, axis, [(j, j ^ step) for j in range(n)])  46 us
    all_gather x1, waiting for transfers between devices, body(): lax.all_gather(weight_shard, island_axes[0], axis=0, tiled=True)  25.3 us
    reduce_scatter x1, waiting for transfers between devices, body(): lax.psum_scatter(partial_keys, 'fsdp', scatter_dimension=0, tiled=True)  23.6 us
    all_to_all x1, waiting for transfers between devices, scatter_by_all_to_all(): lax.all_to_all(blocks, axis, split_axis=0, concat_axis=0, tiled=True)  23.4 us
    ppermute x3, waiting for transfers between devices, doubling_gather(): got = lax.ppermute(values, axis, [(j, j ^ step) for j in range(n)])  13.9 us
    ppermute x3, starting transfers between devices, halving_scatter(): got = lax.ppermute(send, axis, [(j, j ^ step) for j in range(n)])  12.5 us
    all_to_all x1, starting transfers between devices, scatter_by_all_to_all(): lax.all_to_all(blocks, axis, split_axis=0, concat_axis=0, tiled=True)  10.5 us
    ppermute x3, starting transfers between devices, doubling_gather(): got = lax.ppermute(values, axis, [(j, j ^ step) for j in range(n)])  9.19 us
  transfers between devices with their start and end apart: 10, of which 9 were waited for; matrix products, arithmetic and copies ran while one was open for 16% of the time, Pallas kernels for 0%

profile of v5, /device:TPU:6, one launch (start us, length us, event | category | flops | bytes accessed | tf_op | source)
XLA Modules:
  0.0 231.5 jit_solution(15694277476031675574)
XLA Ops:
  7.2 10.5 %all-to-all-start = ((bf16[8,128,512]{2,1,0:T(8,128)(2,1)}), bf16[8,128,512]{2,1,0:T(8,128)(2,1)S(1)}, u32[]{:S(2)}, u32[]{:S(2)}) async-start(bf16[8,128,512]{2,1,0:T(8,128)(2,1)} %bitcast.72), calls=%async_computation | async-start | bytes 2097152 | tf_op jit(solution)/shard_map/all_to_all | solution.py:80
  21.1 1.9 pad_maximum_fusion
  22.9 23.4 %all-to-all-done = bf16[8,128,512]{2,1,0:T(8,128)(2,1)S(1)} async-done(((bf16[8,128,512]{2,1,0:T(8,128)(2,1)}), bf16[8,128,512]{2,1,0:T(8,128)(2,1)S(1)}, u32[]{:S(2)}, u32[]{:S(2)}) %all-to-all-start) | async-done | bytes 1048608 | tf_op jit(solution)/shard_map/all_to_all | solution.py:80
  47.2 5.0 %all-to-all-start.1 = ((bf16[8,128,1664]{2,1,0:T(8,128)(2,1)}), bf16[8,128,1664]{2,1,0:T(8,128)(2,1)S(1)}, u32[]{:S(2)}, u32[]{:S(2)}) async-start(bf16[8,128,1664]{2,1,0:T(8,128)(2,1)} %pad_maximum_fusion), calls=%async_computation.1 | async-start | bytes 6815744 | tf_op jit(solution)/shard_map/all_to_all | solution.py:127
  53.2 3.3 %collective-permute-start = (f32[64,512]{1,0:T(8,128)S(1)}, f32[64,512]{1,0:T(8,128)}, u32[]{:S(2)}, u32[]{:S(2)}) collective-permute-start(f32[64,512]{1,0:T(8,128)S(1)} %constant_dynamic-slice_fusion.4), channel_id=1, source_target_pairs={{0,32},{16,48},{32,0},{48,16},{1,33},{17,49},{33,1},{49,17},{2,34}... | collective-permute-start | bytes 393224 | tf_op jit(solution)/shard_map/ppermute | solution.py:55
  56.6 6.0 %collective-permute-done = f32[64,512]{1,0:T(8,128)} collective-permute-done((f32[64,512]{1,0:T(8,128)S(1)}, f32[64,512]{1,0:T(8,128)}, u32[]{:S(2)}, u32[]{:S(2)}) %collective-permute-start) | collective-permute-done | bytes 131104 | tf_op jit(solution)/shard_map/ppermute | solution.py:55
  64.2 2.7 %collective-permute-start.1 = (f32[32,512]{1,0:T(8,128)}, f32[32,512]{1,0:T(8,128)}, u32[]{:S(2)}, u32[]{:S(2)}) collective-permute-start(f32[32,512]{1,0:T(8,128)} %constant_dynamic-slice_fusion.3), channel_id=1, source_target_pairs={{0,16},{16,0},{32,48},{48,32},{1,17},{17,1},{33,49},{49,33},{2,18}... | collective-permute-start | bytes 196616 | tf_op jit(solution)/shard_map/ppermute | solution.py:55
  67.0 3.7 %collective-permute-done.1 = f32[32,512]{1,0:T(8,128)} collective-permute-done((f32[32,512]{1,0:T(8,128)}, f32[32,512]{1,0:T(8,128)}, u32[]{:S(2)}, u32[]{:S(2)}) %collective-permute-start.1) | collective-permute-done | bytes 65568 | tf_op jit(solution)/shard_map/ppermute | solution.py:55
  72.2 6.4 %collective-permute-start.2 = (f32[16,512]{1,0:T(8,128)S(1)}, f32[16,512]{1,0:T(8,128)S(1)}, u32[]{:S(2)}, u32[]{:S(2)}) collective-permute-start(f32[16,512]{1,0:T(8,128)S(1)} %constant_dynamic-slice_fusion.2), channel_id=1, source_target_pairs={{0,8},{8,0},{1,9},{9,1},{2,10},{10,2},{3,11},{11,3},{4,12},{12,4},... | collective-permute-start | bytes 98312 | tf_op jit(solution)/shard_map/ppermute | solution.py:55
  78.6 36.3 %collective-permute-done.2 = f32[16,512]{1,0:T(8,128)S(1)} collective-permute-done((f32[16,512]{1,0:T(8,128)S(1)}, f32[16,512]{1,0:T(8,128)S(1)}, u32[]{:S(2)}, u32[]{:S(2)}) %collective-permute-start.2) | collective-permute-done | bytes 32800 | tf_op jit(solution)/shard_map/ppermute | solution.py:55
  116.3 3.1 %collective-permute-start.3 = (bf16[16,512]{1,0:T(8,128)(2,1)S(1)}, bf16[16,512]{1,0:T(8,128)(2,1)S(1)}, u32[]{:S(2)}, u32[]{:S(2)}) collective-permute-start(bf16[16,512]{1,0:T(8,128)(2,1)S(1)} %get-tuple-element.7), channel_id=1, source_target_pairs={{0,8},{8,0},{1,9},{9,1},{2,10},{10,2},{3,11},{11,3},{4,12},{12,4},... | collective-permute-start | bytes 49160 | tf_op jit(solution)/shard_map/ppermute | solution.py:66
  119.5 6.5 %collective-permute-done.3 = bf16[16,512]{1,0:T(8,128)(2,1)S(1)} collective-permute-done((bf16[16,512]{1,0:T(8,128)(2,1)S(1)}, bf16[16,512]{1,0:T(8,128)(2,1)S(1)}, u32[]{:S(2)}, u32[]{:S(2)}) %collective-permute-start.3) | collective-permute-done | bytes 16416 | tf_op jit(solution)/shard_map/ppermute | solution.py:66
  125.9 2.7 %collective-permute-start.4 = (bf16[32,512]{1,0:T(8,128)(2,1)S(1)}, bf16[32,512]{1,0:T(8,128)(2,1)S(1)}, u32[]{:S(2)}, u32[]{:S(2)}) collective-permute-start(bf16[32,512]{1,0:T(8,128)(2,1)S(1)} %maximum_select_fusion.2), channel_id=1, source_target_pairs={{0,16},{16,0},{32,48},{48,32},{1,17},{17,1},{33,49},{49,33},{2,18}... | collective-permute-start | bytes 98312 | tf_op jit(solution)/shard_map/ppermute | solution.py:66
  128.7 3.1 %collective-permute-done.4 = bf16[32,512]{1,0:T(8,128)(2,1)S(1)} collective-permute-done((bf16[32,512]{1,0:T(8,128)(2,1)S(1)}, bf16[32,512]{1,0:T(8,128)(2,1)S(1)}, u32[]{:S(2)}, u32[]{:S(2)}) %collective-permute-start.4) | collective-permute-done | bytes 32800 | tf_op jit(solution)/shard_map/ppermute | solution.py:66
  131.8 3.3 %collective-permute-start.5 = (bf16[64,512]{1,0:T(8,128)(2,1)S(1)}, bf16[64,512]{1,0:T(8,128)(2,1)S(1)}, u32[]{:S(2)}, u32[]{:S(2)}) collective-permute-start(bf16[64,512]{1,0:T(8,128)(2,1)S(1)} %maximum_select_fusion.1), channel_id=1, source_target_pairs={{0,32},{16,48},{32,0},{48,16},{1,33},{17,49},{33,1},{49,17},{2,34}... | collective-permute-start | bytes 196616 | tf_op jit(solution)/shard_map/ppermute | solution.py:66
  135.1 4.3 %collective-permute-done.5 = bf16[64,512]{1,0:T(8,128)(2,1)S(1)} collective-permute-done((bf16[64,512]{1,0:T(8,128)(2,1)S(1)}, bf16[64,512]{1,0:T(8,128)(2,1)S(1)}, u32[]{:S(2)}, u32[]{:S(2)}) %collective-permute-start.5) | collective-permute-done | bytes 65568 | tf_op jit(solution)/shard_map/ppermute | solution.py:66
  148.7 1.9 fusion.2
  150.6 25.3 %all-gather.2.cloned.1.call-done = bf16[1024,512]{1,0:T(8,128)(2,1)} async-done(((bf16[128,512]{1,0:T(8,128)(2,1)}), bf16[1024,512]{1,0:T(8,128)(2,1)}) %all-gather.2.cloned.1.call-update) | async-done | bytes 1048592 | tf_op jit(solution)/shard_map/all_gather | solution.py:100
  176.0 4.4 %fusion.33 = f32[1024,512]{1,0:T(8,128)} fusion(bf16[1024,1024]{1,0:T(8,128)(2,1)} %fusion.2, bf16[1024,512]{1,0:T(8,128)(2,1)} %all-gather.2.cloned.1.call-done), kind=kOutput, calls=%fused_computation.93 | convolution fusion | flops 1073741824 | bytes 5242880 | tf_op jit(solution)/shard_map/dot_general | solution.py:157
  182.1 2.1 reshape.176
  184.3 1.9 broadcast_multiply_fusion
  194.7 1.9 fusion.3
  196.6 2.2 fusion.4
  198.8 23.6 %reduce-scatter.2.cloned.1.call-done = f32[128,512]{1,0:T(8,128)} async-done(((f32[1024,512]{1,0:T(8,128)}), f32[128,512]{1,0:T(8,128)}) %reduce-scatter.2.cloned.1.call-update) | async-done | bytes 262160 | tf_op jit(solution)/shard_map/reduce_scatter | solution.py:158
  (74 shorter events, 31.3 us)
Async XLA Ops:
  7.2 10.5 %copy-start.8 = (s32[1,128]{1,0:T(1,128)S(1)}, s32[1,128]{1,0:T(1,128)}, u32[]{:S(2)}) copy-start(s32[1,128]{1,0:T(1,128)} %param.9) | copy-start | bytes 1540
  7.2 10.5 %copy-start.1 = (bf16[1,128,8192]{2,1,0:T(8,128)(2,1)S(1)}, bf16[1,128,8192]{2,1,0:T(8,128)(2,1)}, u32[]{:S(2)}) copy-start(bf16[1,128,8192]{2,1,0:T(8,128)(2,1)} %param.7) | copy-start | bytes 6291460
  7.2 39.2 %all-to-all-start = ((bf16[8,128,512]{2,1,0:T(8,128)(2,1)}), bf16[8,128,512]{2,1,0:T(8,128)(2,1)S(1)}, u32[]{:S(2)}, u32[]{:S(2)}) async-start(bf16[8,128,512]{2,1,0:T(8,128)(2,1)} %bitcast.72), calls=%async_computation | async-start | bytes 2097152 | tf_op jit(solution)/shard_map/all_to_all | solution.py:80
  19.7 1.2 copy-start.5
  47.2 93.0 %copy-start.6 = (bf16[1024]{0:T(1024)(128)(2,1)S(1)}, bf16[1024]{0:T(1024)(128)(2,1)}, u32[]{:S(2)}) copy-start(bf16[1024]{0:T(1024)(128)(2,1)} %param.8) | copy-start | bytes 6148
  47.2 93.0 %all-to-all-start.1 = ((bf16[8,128,1664]{2,1,0:T(8,128)(2,1)}), bf16[8,128,1664]{2,1,0:T(8,128)(2,1)S(1)}, u32[]{:S(2)}, u32[]{:S(2)}) async-start(bf16[8,128,1664]{2,1,0:T(8,128)(2,1)} %pad_maximum_fusion), calls=%async_computation.1 | async-start | bytes 6815744 | tf_op jit(solution)/shard_map/all_to_all | solution.py:127
  52.2 123.7 %all-gather.2.cloned.1.call-start = ((), (), s32[]{:S(2)}) async-start(), calls=%async_computation.3 | async-start | bytes 1179648 | tf_op jit(solution)/shard_map/all_gather | solution.py:100
  53.2 9.3 %collective-permute-start = (f32[64,512]{1,0:T(8,128)S(1)}, f32[64,512]{1,0:T(8,128)}, u32[]{:S(2)}, u32[]{:S(2)}) collective-permute-start(f32[64,512]{1,0:T(8,128)S(1)} %constant_dynamic-slice_fusion.4), channel_id=1, source_target_pairs={{0,32},{16,48},{32,0},{48,16},{1,33},{17,49},{33,1},{49,17},{2,34}... | collective-permute-start | bytes 393224 | tf_op jit(solution)/shard_map/ppermute | solution.py:55
  64.2 6.5 %collective-permute-start.1 = (f32[32,512]{1,0:T(8,128)}, f32[32,512]{1,0:T(8,128)}, u32[]{:S(2)}, u32[]{:S(2)}) collective-permute-start(f32[32,512]{1,0:T(8,128)} %constant_dynamic-slice_fusion.3), channel_id=1, source_target_pairs={{0,16},{16,0},{32,48},{48,32},{1,17},{17,1},{33,49},{49,33},{2,18}... | collective-permute-start | bytes 196616 | tf_op jit(solution)/shard_map/ppermute | solution.py:55
  71.5 0.6 copy-start.4
  72.2 42.7 %collective-permute-start.2 = (f32[16,512]{1,0:T(8,128)S(1)}, f32[16,512]{1,0:T(8,128)S(1)}, u32[]{:S(2)}, u32[]{:S(2)}) collective-permute-start(f32[16,512]{1,0:T(8,128)S(1)} %constant_dynamic-slice_fusion.2), channel_id=1, source_target_pairs={{0,8},{8,0},{1,9},{9,1},{2,10},{10,2},{3,11},{11,3},{4,12},{12,4},... | collective-permute-start | bytes 98312 | tf_op jit(solution)/shard_map/ppermute | solution.py:55
  116.3 9.6 %collective-permute-start.3 = (bf16[16,512]{1,0:T(8,128)(2,1)S(1)}, bf16[16,512]{1,0:T(8,128)(2,1)S(1)}, u32[]{:S(2)}, u32[]{:S(2)}) collective-permute-start(bf16[16,512]{1,0:T(8,128)(2,1)S(1)} %get-tuple-element.7), channel_id=1, source_target_pairs={{0,8},{8,0},{1,9},{9,1},{2,10},{10,2},{3,11},{11,3},{4,12},{12,4},... | collective-permute-start | bytes 49160 | tf_op jit(solution)/shard_map/ppermute | solution.py:66
  125.9 5.8 %collective-permute-start.4 = (bf16[32,512]{1,0:T(8,128)(2,1)S(1)}, bf16[32,512]{1,0:T(8,128)(2,1)S(1)}, u32[]{:S(2)}, u32[]{:S(2)}) collective-permute-start(bf16[32,512]{1,0:T(8,128)(2,1)S(1)} %maximum_select_fusion.2), channel_id=1, source_target_pairs={{0,16},{16,0},{32,48},{48,32},{1,17},{17,1},{33,49},{49,33},{2,18}... | collective-permute-start | bytes 98312 | tf_op jit(solution)/shard_map/ppermute | solution.py:66
  131.8 7.7 %collective-permute-start.5 = (bf16[64,512]{1,0:T(8,128)(2,1)S(1)}, bf16[64,512]{1,0:T(8,128)(2,1)S(1)}, u32[]{:S(2)}, u32[]{:S(2)}) collective-permute-start(bf16[64,512]{1,0:T(8,128)(2,1)S(1)} %maximum_select_fusion.1), channel_id=1, source_target_pairs={{0,32},{16,48},{32,0},{48,16},{1,33},{17,49},{33,1},{49,17},{2,34}... | collective-permute-start | bytes 196616 | tf_op jit(solution)/shard_map/ppermute | solution.py:66
  140.1 82.3 %reduce-scatter.2.cloned.1.call-start = ((), (), s32[]{:S(2)}) async-start(), calls=%async_computation.4 | async-start | bytes 2359296 | tf_op jit(solution)/shard_map/reduce_scatter | solution.py:158
  147.4 1.3 copy-start.2
  189.4 1.6 copy-start
  192.9 1.6 copy-start.3
  192.9 1.9 copy-start.7
Sparse Core Ops, SparseCore 0:
  140.3 35.6 all-gather.1
  180.5 41.8 reduce-scatter.1

commit v6 on v3

--- a/solution.py
+++ b/solution.py
@@ -74,6 +74,15 @@
     return values
 
 
+def doubling_sum(values, axis):
+    n = lax.axis_size(axis)
+    step = 1 << (n.bit_length() - 2) if n > 1 else 0
+    while step >= 1:
+        values = values + lax.ppermute(values, axis, [(j, j ^ step) for j in range(n)])
+        step //= 2
+    return values
+
+
 def body(island_axes, hidden, gain, doc_ids, cotangent, pseudo_grad, outer_weight, momentum):
     islands = 1
     for ax in island_axes:
@@ -82,15 +91,25 @@
 
     summed = pseudo_grad[0].astype(jnp.float32)
     summed = lax.psum_scatter(summed, island_axes[0], scatter_dimension=0, tiled=True)
-    for ax in island_axes[1:]:
-        summed = halving_scatter(summed, ax)
+    rest = island_axes[1:]
+    state = jnp.concatenate([outer_weight, momentum], axis=1)
+    for ax in reversed(rest):
+        state = lax.all_gather(state, ax, axis=0, tiled=True)
+    for ax in rest:
+        summed = doubling_sum(summed, ax)
+    cols = outer_weight.shape[1]
+    group_outer, group_momentum = state[:, :cols], state[:, cols:]
     mean_delta = summed / islands
-    new_momentum = momentum_rate * momentum + mean_delta
-    new_outer = outer_weight - learn_rate * (mean_delta + momentum_rate * new_momentum)
-    weight_shard = new_outer.astype(jnp.bfloat16)
-    for ax in reversed(island_axes[1:]):
-        weight_shard = doubling_gather(weight_shard, ax)
+    group_new_momentum = momentum_rate * group_momentum + mean_delta
+    group_new_outer = group_outer - learn_rate * (mean_delta + momentum_rate * group_new_momentum)
+    weight_shard = group_new_outer.astype(jnp.bfloat16)
     weight_shard = lax.all_gather(weight_shard, island_axes[0], axis=0, tiled=True)
+    mine = 0
+    for ax in rest:
+        mine = mine * lax.axis_size(ax) + lax.axis_index(ax)
+    own_rows = outer_weight.shape[0]
+    new_outer = lax.dynamic_slice_in_dim(group_new_outer, mine * own_rows, own_rows, axis=0)
+    new_momentum = lax.dynamic_slice_in_dim(group_new_momentum, mine * own_rows, own_rows, axis=0)
 
     tok_rows = hidden.shape[1]
     seq = tok_rows * fsdp_ways

time: 213 us -> 212 us (level)
  blocking collectives: 27.3 us -> 50.6 us
  starting transfers between devices: 32.2 us -> 18.6 us
  waiting for transfers between devices: 95.1 us -> 84.8 us
    all_gather x0 -> x2, blocking collectives: none -> 22.4 us  [body(): state = lax.all_gather(state, ax, axis=0, tiled=True)]
    ppermute x6 -> x3, starting transfers between devices: 27.1 us -> 13.5 us  [doubling_sum(): lax.ppermute(values, axis, [(j, j ^ step) for j in range(n)])]
    ppermute x6 -> x3, waiting for transfers between devices: 20.1 us -> 12.1 us  [doubling_sum(): lax.ppermute(values, axis, [(j, j ^ step) for j in range(n)])]
  transfers between devices with their start and end apart: 10 -> 7, of which waited for: 9 -> 5; matrix products, arithmetic and copies ran while one was open for 15% -> 15% of each run, Pallas kernels for 0% -> 0%
where the time goes in v6:
time: 212 us; the launch traced here: 211 us
  waiting for transfers between devices  84.8 us (40%)
  blocking collectives  50.6 us (24%)
  other arithmetic  20.8 us (10%)
  starting transfers between devices  18.6 us (9%)
  between operations  14.1 us (7%)
  matrix products  11.6 us (5%)
  local copies, waits for them, and re-layouts  10.5 us (5%)
    reduce_scatter x1, waiting for transfers between devices, body(): lax.psum_scatter(summed, island_axes[0], scatter_dimension=0, tiled=True)  41.5 us
    all_gather x2, blocking collectives, body(): state = lax.all_gather(state, ax, axis=0, tiled=True)  22.4 us
    reduce_scatter x1, waiting for transfers between devices, body(): lax.psum_scatter(partial_keys, 'fsdp', scatter_dimension=0, tiled=True)  21.1 us
    all_gather x1, blocking collectives, body(): all_scales = lax.all_gather(row_scale, 'fsdp', axis=0, tiled=True)  19.4 us
    ppermute x3, starting transfers between devices, doubling_sum(): lax.ppermute(values, axis, [(j, j ^ step) for j in range(n)])  13.5 us
    ppermute x3, waiting for transfers between devices, doubling_sum(): lax.ppermute(values, axis, [(j, j ^ step) for j in range(n)])  12.1 us
    all_gather x1, waiting for transfers between devices, body(): lax.all_gather(weight_shard, island_axes[0], axis=0, tiled=True)  10.1 us
    all_gather x1, blocking collectives, body(): all_docs = lax.all_gather(doc_ids[0], 'fsdp', axis=0, tiled=True)  8.9 us
  transfers between devices with their start and end apart: 7, of which 5 were waited for; matrix products, arithmetic and copies ran while one was open for 15% of the time, Pallas kernels for 0%

profile of v6, /device:TPU:6, one launch (start us, length us, event | category | flops | bytes accessed | tf_op | source)
XLA Modules:
  0.0 211.0 jit_solution(6590753907570988543)
XLA Ops:
  7.2 3.0 %bitcast_convert_fusion = f32[1024,512]{1,0:T(8,128)} fusion(bf16[1,1024,512]{2,1,0:T(8,128)(2,1)} %param.11), kind=kLoop, calls=%fused_computation.23 | loop fusion | flops 524288 | bytes 3145728 | tf_op jit(solution)/shard_map/convert_element_type | solution.py:92
  13.0 1.9 pad_maximum_fusion
  14.9 5.0 %all-to-all-start = ((bf16[8,128,1536]{2,1,0:T(8,128)(2,1)}), bf16[8,128,1536]{2,1,0:T(8,128)(2,1)S(1)}, u32[]{:S(2)}, u32[]{:S(2)}) async-start(bf16[8,128,1536]{2,1,0:T(8,128)(2,1)} %pad_maximum_fusion), calls=%async_computation | async-start | bytes 6291456 | tf_op jit(solution)/shard_map/all_to_all | solution.py:134
  19.9 41.5 %reduce-scatter.3.cloned.1.call-done = f32[128,512]{1,0:T(8,128)} async-done(((f32[1024,512]{1,0:T(8,128)}), f32[128,512]{1,0:T(8,128)}) %reduce-scatter.3.cloned.1.call-update) | async-done | bytes 262160 | tf_op jit(solution)/shard_map/reduce_scatter | solution.py:93
  61.4 3.4 %collective-permute-start = (f32[128,512]{1,0:T(8,128)}, f32[128,512]{1,0:T(8,128)S(1)}, u32[]{:S(2)}, u32[]{:S(2)}) collective-permute-start(f32[128,512]{1,0:T(8,128)} %reduce-scatter.3.cloned.1.call-done), channel_id=1, source_target_pairs={{0,32},{16,48},{32,0},{48,16},{1,33},{17,49},{33,1},{49,17},{2,34}... | collective-permute-start | bytes 786440 | tf_op jit(solution)/shard_map/ppermute | solution.py:81
  64.8 6.6 %collective-permute-done = f32[128,512]{1,0:T(8,128)S(1)} collective-permute-done((f32[128,512]{1,0:T(8,128)}, f32[128,512]{1,0:T(8,128)S(1)}, u32[]{:S(2)}, u32[]{:S(2)}) %collective-permute-start) | collective-permute-done | bytes 262176 | tf_op jit(solution)/shard_map/ppermute | solution.py:81
  72.4 2.8 %collective-permute-start.1 = (f32[128,512]{1,0:T(8,128)S(1)}, f32[128,512]{1,0:T(8,128)S(1)}, u32[]{:S(2)}, u32[]{:S(2)}) collective-permute-start(f32[128,512]{1,0:T(8,128)S(1)} %add.74), channel_id=1, source_target_pairs={{0,16},{16,0},{32,48},{48,32},{1,17},{17,1},{33,49},{49,33},{2,18}... | collective-permute-start | bytes 786440 | tf_op jit(solution)/shard_map/ppermute | solution.py:81
  75.1 5.5 %collective-permute-done.1 = f32[128,512]{1,0:T(8,128)S(1)} collective-permute-done((f32[128,512]{1,0:T(8,128)S(1)}, f32[128,512]{1,0:T(8,128)S(1)}, u32[]{:S(2)}, u32[]{:S(2)}) %collective-permute-start.1) | collective-permute-done | bytes 262176 | tf_op jit(solution)/shard_map/ppermute | solution.py:81
  80.7 7.4 %collective-permute-start.2 = (f32[128,512]{1,0:T(8,128)S(1)}, f32[128,512]{1,0:T(8,128)S(1)}, u32[]{:S(2)}, u32[]{:S(2)}) collective-permute-start(f32[128,512]{1,0:T(8,128)S(1)} %add.75), channel_id=1, source_target_pairs={{0,8},{8,0},{1,9},{9,1},{2,10},{10,2},{3,11},{11,3},{4,12},{12,4},... | collective-permute-start | bytes 786440 | tf_op jit(solution)/shard_map/ppermute | solution.py:81
  88.1 9.6 %all_gather.16 = f32[32,1024]{1,0:T(8,128)S(1)} all-gather(f32[16,1024]{1,0:T(8,128)S(1)} %pad_maximum_fusion.2), channel_id=1, replica_groups=mesh['island0'=8,'island1'=4,'island2'=2,'fsdp'=8] {'island2'}, dimensions={0}, use_global_device_ids=true | all-gather | bytes 196608 | tf_op jit(solution)/shard_map/all_gather | solution.py:97
  97.7 12.8 %all_gather.17 = f32[128,1024]{1,0:T(8,128)S(1)} all-gather(f32[32,1024]{1,0:T(8,128)S(1)} %all_gather.16), channel_id=1, replica_groups=mesh['island0'=8,'island1'=4,'island2'=2,'fsdp'=8] {'island1'}, dimensions={0}, use_global_device_ids=true | all-gather | bytes 655360 | tf_op jit(solution)/shard_map/all_gather | solution.py:97
  111.4 2.1 multiply_reduce_fusion
  113.5 19.4 %all-gather.2 = f32[8,1,128]{2,1,0:T(1,128)S(1)} all-gather(f32[1,1,128]{2,1,0:T(1,128)S(1)} %rsqrt_bitcast_fusion), channel_id=2, replica_groups=mesh['island0'=8,'island1'=4,'island2'=2,'fsdp'=8] {'fsdp'}, dimensions={0}, use_global_device_ids=true | all-gather | bytes 4608 | tf_op jit(solution)/shard_map/all_gather | solution.py:141
  132.8 8.9 %all-gather.1 = s32[1,1024]{1,0:T(1,128)S(1)} all-gather(s32[1,128]{1,0:T(1,128)S(1)} %copy-done.10), channel_id=3, replica_groups=mesh['island0'=8,'island1'=4,'island2'=2,'fsdp'=8] {'fsdp'}, dimensions={1}, use_global_device_ids=true | all-gather | bytes 4608 | tf_op jit(solution)/shard_map/all_gather | solution.py:117
  143.6 1.9 fusion.2
  145.5 10.1 %all-gather.5.cloned.1.call-done = bf16[1024,512]{1,0:T(8,128)(2,1)} async-done(((bf16[128,512]{1,0:T(8,128)(2,1)}), bf16[1024,512]{1,0:T(8,128)(2,1)}) %all-gather.5.cloned.1.call-update) | async-done | bytes 1048592 | tf_op jit(solution)/shard_map/all_gather | solution.py:106
  155.6 4.4 %fusion.33 = f32[1024,512]{1,0:T(8,128)} fusion(bf16[1024,1024]{1,0:T(8,128)(2,1)} %fusion.2, bf16[1024,512]{1,0:T(8,128)(2,1)} %all-gather.5.cloned.1.call-done), kind=kOutput, calls=%fused_computation.79 | convolution fusion | flops 1073741824 | bytes 5242880 | tf_op jit(solution)/shard_map/dot_general | solution.py:159
  160.1 3.2 %broadcast_multiply_fusion = (f32[1024,64]{1,0:T(8,128)}, f32[1024,64]{1,0:T(8,128)}, f32[1024,64]{1,0:T(8,128)}) fusion(f32[64]{0:T(128)S(1)} %multiply_exponential_fusion, f32[1024]{0:T(1024)S(1)} %subtract_convert_fusion.2), kind=kLoop, calls=%fused_computation.37 | loop fusion | flops 131072 | bytes 790784 | tf_op jit(solution)/shard_map/mul | solution.py:39
  165.5 1.6 slice_convert_fusion
  167.2 2.0 reshape.137
  169.2 1.6 subtract_convert_fusion
  177.1 2.2 %fusion.4 = bf16[1,1024,512]{2,1,0:T(8,128)(2,1)} fusion(bf16[1024,512]{1,0:T(8,128)(2,1)S(1)} %convolution_convert_fusion, bf16[1024,512]{1,0:T(8,128)(2,1)S(1)} %convolution_convert_fusion.1, bf16[1024,512]{1,0:T(8,128)(2,1)S(1)} %convolution_convert_fusion.2, bf16[1024,512]{1,0:T(8,128)(2,1)S(1)} %convolution_convert_fusion.3, ...), kind=kOutput, calls=%fused_computation.19 | convolution fusion | flops 143130624 | bytes 8781824 | tf_op jit(solution)/shard_map/dot_general | solution.py:149
  179.3 1.9 fusion.3
  181.2 21.1 %reduce-scatter.5.cloned.1.call-done = f32[128,512]{1,0:T(8,128)} async-done(((f32[1024,512]{1,0:T(8,128)}), f32[128,512]{1,0:T(8,128)}) %reduce-scatter.5.cloned.1.call-update) | async-done | bytes 262160 | tf_op jit(solution)/shard_map/reduce_scatter | solution.py:160
  (62 shorter events, 17.2 us)
Async XLA Ops:
  7.2 3.1 %copy-start.1 = (bf16[1,128,8192]{2,1,0:T(8,128)(2,1)S(1)}, bf16[1,128,8192]{2,1,0:T(8,128)(2,1)}, u32[]{:S(2)}) copy-start(bf16[1,128,8192]{2,1,0:T(8,128)(2,1)} %param.7) | copy-start | bytes 6291460
  7.2 54.2 %reduce-scatter.3.cloned.1.call-start = ((), (), s32[]{:S(2)}) async-start(), calls=%async_computation.3 | async-start | bytes 2359296 | tf_op jit(solution)/shard_map/reduce_scatter | solution.py:93
  11.7 1.2 copy-start.6
  14.9 73.2 %copy-start.7 = (f32[16,512]{1,0:T(8,128)S(1)}, f32[16,512]{1,0:T(8,128)}, u32[]{:S(2)}) copy-start(f32[16,512]{1,0:T(8,128)} %param.13) | copy-start | bytes 98308
  14.9 73.2 %copy-start.8 = (f32[16,512]{1,0:T(8,128)S(1)}, f32[16,512]{1,0:T(8,128)}, u32[]{:S(2)}) copy-start(f32[16,512]{1,0:T(8,128)} %param.12) | copy-start | bytes 98308
  14.9 127.1 %all-to-all-start = ((bf16[8,128,1536]{2,1,0:T(8,128)(2,1)}), bf16[8,128,1536]{2,1,0:T(8,128)(2,1)S(1)}, u32[]{:S(2)}, u32[]{:S(2)}) async-start(bf16[8,128,1536]{2,1,0:T(8,128)(2,1)} %pad_maximum_fusion), calls=%async_computation | async-start | bytes 6291456 | tf_op jit(solution)/shard_map/all_to_all | solution.py:134
  19.9 91.5 %copy-start.9 = (bf16[1024]{0:T(1024)(128)(2,1)S(1)}, bf16[1024]{0:T(1024)(128)(2,1)}, u32[]{:S(2)}) copy-start(bf16[1024]{0:T(1024)(128)(2,1)} %param.8) | copy-start | bytes 6148
  19.9 135.7 %all-gather.5.cloned.1.call-start = ((), (), s32[]{:S(2)}) async-start(), calls=%async_computation.4 | async-start | bytes 1179648 | tf_op jit(solution)/shard_map/all_gather | solution.py:106
  61.4 10.0 %collective-permute-start = (f32[128,512]{1,0:T(8,128)}, f32[128,512]{1,0:T(8,128)S(1)}, u32[]{:S(2)}, u32[]{:S(2)}) collective-permute-start(f32[128,512]{1,0:T(8,128)} %reduce-scatter.3.cloned.1.call-done), channel_id=1, source_target_pairs={{0,32},{16,48},{32,0},{48,16},{1,33},{17,49},{33,1},{49,17},{2,34}... | collective-permute-start | bytes 786440 | tf_op jit(solution)/shard_map/ppermute | solution.py:81
  72.4 8.3 %collective-permute-start.1 = (f32[128,512]{1,0:T(8,128)S(1)}, f32[128,512]{1,0:T(8,128)S(1)}, u32[]{:S(2)}, u32[]{:S(2)}) collective-permute-start(f32[128,512]{1,0:T(8,128)S(1)} %add.74), channel_id=1, source_target_pairs={{0,16},{16,0},{32,48},{48,32},{1,17},{17,1},{33,49},{49,33},{2,18}... | collective-permute-start | bytes 786440 | tf_op jit(solution)/shard_map/ppermute | solution.py:81
  80.7 29.8 %collective-permute-start.2 = (f32[128,512]{1,0:T(8,128)S(1)}, f32[128,512]{1,0:T(8,128)S(1)}, u32[]{:S(2)}, u32[]{:S(2)}) collective-permute-start(f32[128,512]{1,0:T(8,128)S(1)} %add.75), channel_id=1, source_target_pairs={{0,8},{8,0},{1,9},{9,1},{2,10},{10,2},{3,11},{11,3},{4,12},{12,4},... | collective-permute-start | bytes 786440 | tf_op jit(solution)/shard_map/ppermute | solution.py:81
  110.4 22.4 %copy-start.10 = (s32[1,128]{1,0:T(1,128)S(1)}, s32[1,128]{1,0:T(1,128)}, u32[]{:S(2)}) copy-start(s32[1,128]{1,0:T(1,128)} %param.9) | copy-start | bytes 1540
  111.3 90.9 %reduce-scatter.5.cloned.1.call-start = ((), (), s32[]{:S(2)}) async-start(), calls=%async_computation.5 | async-start | bytes 2359296 | tf_op jit(solution)/shard_map/reduce_scatter | solution.py:160
  142.3 1.3 copy-start.2
  167.2 2.0 copy-start.4
  167.2 2.0 copy-start.5
  172.3 1.6 copy-start
  177.1 2.2 %copy-start.3 = (bf16[8,128,1024]{2,1,0:T(8,128)(2,1)S(1)}, bf16[8,128,1024]{2,1,0:T(8,128)(2,1)}, u32[]{:S(2)}) copy-start(bf16[8,128,1024]{2,1,0:T(8,128)(2,1)} %copy-done.2) | copy-start | bytes 6291460
  177.1 2.2 %copy-start.11 = (bf16[1024,512]{1,0:T(8,128)(2,1)S(1)}, bf16[1024,512]{1,0:T(8,128)(2,1)}, u32[]{:S(2)}) copy-start(bf16[1024,512]{1,0:T(8,128)(2,1)} %all-gather.5.cloned.1.call-done) | copy-start | bytes 3145732
Sparse Core Ops, SparseCore 0:
  10.8 50.5 reduce-scatter.2
  111.4 44.1 all-gather.4
  160.2 41.9 reduce-scatter.4

commit v7 on v6

--- a/solution.py
+++ b/solution.py
@@ -94,7 +94,7 @@
     rest = island_axes[1:]
     state = jnp.concatenate([outer_weight, momentum], axis=1)
     for ax in reversed(rest):
-        state = lax.all_gather(state, ax, axis=0, tiled=True)
+        state = doubling_gather(state, ax)
     for ax in rest:
         summed = doubling_sum(summed, ax)
     cols = outer_weight.shape[1]

time: 212 us -> 212 us (level)
  blocking collectives: 50.6 us -> 20.6 us
  waiting for transfers between devices: 84.8 us -> 99 us
  starting transfers between devices: 18.6 us -> 27.6 us
  other arithmetic: 20.8 us -> 27.5 us
    all_gather x2 -> x0, blocking collectives: 22.4 us -> none  [body(): state = lax.all_gather(state, ax, axis=0, tiled=True)]
    ppermute x0 -> x3, waiting for transfers between devices: none -> 14.9 us  [doubling_gather(): got = lax.ppermute(values, axis, [(j, j ^ step) for j in range(n)])]
    ppermute x0 -> x3, starting transfers between devices: none -> 12.6 us  [doubling_gather(): got = lax.ppermute(values, axis, [(j, j ^ step) for j in range(n)])]
    all_gather x1, waiting for transfers between devices: 10.1 us -> 18.7 us  [body(): lax.all_gather(weight_shard, island_axes[0], axis=0, tiled=True)]
    all_gather x1, blocking collectives: 19.4 us -> 11.7 us  [body(): all_scales = lax.all_gather(row_scale, 'fsdp', axis=0, tiled=True)]
    reduce_scatter x1, waiting for transfers between devices: 41.5 us -> 34.9 us  [body(): lax.psum_scatter(summed, island_axes[0], scatter_dimension=0, tiled=True)]
    ppermute x3, starting transfers between devices: 13.5 us -> 9.93 us  [doubling_sum(): lax.ppermute(values, axis, [(j, j ^ step) for j in range(n)])]
    select_n x0 -> x3, other arithmetic: none -> 2.97 us  [doubling_gather(): jnp.where(upper == 1, jnp.concatenate([got, values], axis=0), jnp.concate...]
  transfers between devices with their start and end apart: 7 -> 10, of which waited for: 5 -> 7; matrix products, arithmetic and copies ran while one was open for 15% -> 18% of each run, Pallas kernels for 0% -> 0%
where the time goes in v7:
time: 212 us; the launch traced here: 211 us
  waiting for transfers between devices  99 us (47%)
  starting transfers between devices  27.6 us (13%)
  other arithmetic  27.5 us (13%)
  blocking collectives  20.6 us (10%)
  between operations  14.2 us (7%)
  matrix products  11.7 us (6%)
  local copies, waits for them, and re-layouts  10.4 us (5%)
    reduce_scatter x1, waiting for transfers between devices, body(): lax.psum_scatter(summed, island_axes[0], scatter_dimension=0, tiled=True)  34.9 us
    reduce_scatter x1, waiting for transfers between devices, body(): lax.psum_scatter(partial_keys, 'fsdp', scatter_dimension=0, tiled=True)  20.1 us
    all_gather x1, waiting for transfers between devices, body(): lax.all_gather(weight_shard, island_axes[0], axis=0, tiled=True)  18.7 us
    ppermute x3, waiting for transfers between devices, doubling_gather(): got = lax.ppermute(values, axis, [(j, j ^ step) for j in range(n)])  14.9 us
    ppermute x3, starting transfers between devices, doubling_gather(): got = lax.ppermute(values, axis, [(j, j ^ step) for j in range(n)])  12.6 us
    all_gather x1, blocking collectives, body(): all_scales = lax.all_gather(row_scale, 'fsdp', axis=0, tiled=True)  11.7 us
    ppermute x3, waiting for transfers between devices, doubling_sum(): lax.ppermute(values, axis, [(j, j ^ step) for j in range(n)])  10.4 us
    ppermute x3, starting transfers between devices, doubling_sum(): lax.ppermute(values, axis, [(j, j ^ step) for j in range(n)])  9.93 us
  transfers between devices with their start and end apart: 10, of which 7 were waited for; matrix products, arithmetic and copies ran while one was open for 18% of the time, Pallas kernels for 0%

profile of v7, /device:TPU:6, one launch (start us, length us, event | category | flops | bytes accessed | tf_op | source)
XLA Modules:
  0.0 211.0 jit_solution(1625987378388351854)
XLA Ops:
  7.2 3.0 %bitcast_convert_fusion = f32[1024,512]{1,0:T(8,128)} fusion(bf16[1,1024,512]{2,1,0:T(8,128)(2,1)} %param.11), kind=kLoop, calls=%fused_computation.23 | loop fusion | flops 524288 | bytes 3145728 | tf_op jit(solution)/shard_map/convert_element_type | solution.py:92
  13.0 1.9 pad_maximum_fusion
  14.9 5.0 %all-to-all-start = ((bf16[8,128,1536]{2,1,0:T(8,128)(2,1)}), bf16[8,128,1536]{2,1,0:T(8,128)(2,1)S(1)}, u32[]{:S(2)}, u32[]{:S(2)}) async-start(bf16[8,128,1536]{2,1,0:T(8,128)(2,1)} %pad_maximum_fusion), calls=%async_computation | async-start | bytes 6291456 | tf_op jit(solution)/shard_map/all_to_all | solution.py:134
  20.0 6.5 %collective-permute-start = (f32[16,1024]{1,0:T(8,128)S(1)}, f32[16,1024]{1,0:T(8,128)S(1)}, u32[]{:S(2)}, u32[]{:S(2)}) collective-permute-start(f32[16,1024]{1,0:T(8,128)S(1)} %constant_dynamic-update-slice_fusion), channel_id=1, source_target_pairs={{0,8},{8,0},{1,9},{9,1},{2,10},{10,2},{3,11},{11,3},{4,12},{12,4},... | collective-permute-start | bytes 196616 | tf_op jit(solution)/shard_map/ppermute | solution.py:66
  26.5 34.9 %reduce-scatter.3.cloned.1.call-done = f32[128,512]{1,0:T(8,128)} async-done(((f32[1024,512]{1,0:T(8,128)}), f32[128,512]{1,0:T(8,128)}) %reduce-scatter.3.cloned.1.call-update) | async-done | bytes 262160 | tf_op jit(solution)/shard_map/reduce_scatter | solution.py:93
  61.4 3.4 %collective-permute-start.3 = (f32[128,512]{1,0:T(8,128)}, f32[128,512]{1,0:T(8,128)}, u32[]{:S(2)}, u32[]{:S(2)}) collective-permute-start(f32[128,512]{1,0:T(8,128)} %reduce-scatter.3.cloned.1.call-done), channel_id=1, source_target_pairs={{0,32},{16,48},{32,0},{48,16},{1,33},{17,49},{33,1},{49,17},{2,34}... | collective-permute-start | bytes 786440 | tf_op jit(solution)/shard_map/ppermute | solution.py:81
  64.8 14.6 %collective-permute-done = f32[16,1024]{1,0:T(8,128)S(1)} collective-permute-done((f32[16,1024]{1,0:T(8,128)S(1)}, f32[16,1024]{1,0:T(8,128)S(1)}, u32[]{:S(2)}, u32[]{:S(2)}) %collective-permute-start) | collective-permute-done | bytes 65568 | tf_op jit(solution)/shard_map/ppermute | solution.py:66
  79.4 2.7 %collective-permute-start.1 = (f32[32,1024]{1,0:T(8,128)S(1)}, f32[32,1024]{1,0:T(8,128)}, u32[]{:S(2)}, u32[]{:S(2)}) collective-permute-start(f32[32,1024]{1,0:T(8,128)S(1)} %maximum_select_fusion.2), channel_id=1, source_target_pairs={{0,16},{16,0},{32,48},{48,32},{1,17},{17,1},{33,49},{49,33},{2,18}... | collective-permute-start | bytes 393224 | tf_op jit(solution)/shard_map/ppermute | solution.py:66
  83.2 3.1 %collective-permute-start.4 = (f32[128,512]{1,0:T(8,128)S(1)}, f32[128,512]{1,0:T(8,128)}, u32[]{:S(2)}, u32[]{:S(2)}) collective-permute-start(f32[128,512]{1,0:T(8,128)S(1)} %add.90), channel_id=1, source_target_pairs={{0,16},{16,0},{32,48},{48,32},{1,17},{17,1},{33,49},{49,33},{2,18}... | collective-permute-start | bytes 786440 | tf_op jit(solution)/shard_map/ppermute | solution.py:81
  88.4 3.3 %collective-permute-start.2 = (f32[64,1024]{1,0:T(8,128)}, f32[64,1024]{1,0:T(8,128)}, u32[]{:S(2)}, u32[]{:S(2)}) collective-permute-start(f32[64,1024]{1,0:T(8,128)} %maximum_select_fusion.1), channel_id=1, source_target_pairs={{0,32},{16,48},{32,0},{48,16},{1,33},{17,49},{33,1},{49,17},{2,34}... | collective-permute-start | bytes 786440 | tf_op jit(solution)/shard_map/ppermute | solution.py:66
  91.7 2.7 %collective-permute-done.4 = f32[128,512]{1,0:T(8,128)} collective-permute-done((f32[128,512]{1,0:T(8,128)S(1)}, f32[128,512]{1,0:T(8,128)}, u32[]{:S(2)}, u32[]{:S(2)}) %collective-permute-start.4) | collective-permute-done | bytes 262176 | tf_op jit(solution)/shard_map/ppermute | solution.py:81
  96.1 3.5 %collective-permute-start.5 = (f32[128,512]{1,0:T(8,128)}, f32[128,512]{1,0:T(8,128)}, u32[]{:S(2)}, u32[]{:S(2)}) collective-permute-start(f32[128,512]{1,0:T(8,128)} %add.91), channel_id=1, source_target_pairs={{0,8},{8,0},{1,9},{9,1},{2,10},{10,2},{3,11},{11,3},{4,12},{12,4},... | collective-permute-start | bytes 786440 | tf_op jit(solution)/shard_map/ppermute | solution.py:81
  100.9 7.7 %collective-permute-done.5 = f32[128,512]{1,0:T(8,128)} collective-permute-done((f32[128,512]{1,0:T(8,128)}, f32[128,512]{1,0:T(8,128)}, u32[]{:S(2)}, u32[]{:S(2)}) %collective-permute-start.5) | collective-permute-done | bytes 262176 | tf_op jit(solution)/shard_map/ppermute | solution.py:81
  110.5 2.1 multiply_reduce_fusion
  112.6 11.7 %all-gather.2 = f32[8,1,128]{2,1,0:T(1,128)S(1)} all-gather(f32[1,1,128]{2,1,0:T(1,128)S(1)} %rsqrt_bitcast_fusion), channel_id=2, replica_groups=mesh['island0'=8,'island1'=4,'island2'=2,'fsdp'=8] {'fsdp'}, dimensions={0}, use_global_device_ids=true | all-gather | bytes 4608 | tf_op jit(solution)/shard_map/all_gather | solution.py:141
  124.3 8.9 %all-gather.1 = s32[1,1024]{1,0:T(1,128)S(1)} all-gather(s32[1,128]{1,0:T(1,128)S(1)} %copy-done.8), channel_id=3, replica_groups=mesh['island0'=8,'island1'=4,'island2'=2,'fsdp'=8] {'fsdp'}, dimensions={1}, use_global_device_ids=true | all-gather | bytes 4608 | tf_op jit(solution)/shard_map/all_gather | solution.py:117
  136.9 18.7 %all-gather.5.cloned.1.call-done = bf16[1024,512]{1,0:T(8,128)(2,1)} async-done(((bf16[128,512]{1,0:T(8,128)(2,1)}), bf16[1024,512]{1,0:T(8,128)(2,1)}) %all-gather.5.cloned.1.call-update) | async-done | bytes 1048592 | tf_op jit(solution)/shard_map/all_gather | solution.py:106
  155.6 4.4 %fusion.33 = f32[1024,512]{1,0:T(8,128)} fusion(bf16[1024,1024]{1,0:T(8,128)(2,1)} %fusion.2, bf16[1024,512]{1,0:T(8,128)(2,1)} %all-gather.5.cloned.1.call-done), kind=kOutput, calls=%fused_computation.83 | convolution fusion | flops 1073741824 | bytes 5242880 | tf_op jit(solution)/shard_map/dot_general | solution.py:159
  160.1 3.2 %broadcast_multiply_fusion = (f32[1024,64]{1,0:T(8,128)}, f32[1024,64]{1,0:T(8,128)}, f32[1024,64]{1,0:T(8,128)}) fusion(f32[64]{0:T(128)S(1)} %multiply_exponential_fusion, f32[1024]{0:T(1024)S(1)} %subtract_convert_fusion.2), kind=kLoop, calls=%fused_computation.39 | loop fusion | flops 131072 | bytes 790784 | tf_op jit(solution)/shard_map/mul | solution.py:39
  167.1 1.9 reshape.137
  169.1 2.6 %subtract_convert_fusion = (bf16[1024,4,64]{2,1,0:T(4,128)(2,1)S(1)}, bf16[1024,4,64]{2,1,0:T(4,128)(2,1)S(1)}) fusion(f32[1024,4,128]{2,1,0:T(4,128)S(1)} %reshape.137, f32[1024,64]{1,0:T(8,128)} %get-tuple-element.20, f32[1024,64]{1,0:T(8,128)} %get-tuple-element.22), kind=kLoop, calls=%fused_computation.10 | loop fusion | flops 2097152 | bytes 3670016 | tf_op jit(solution)/shard_map/convert.3
  178.0 2.2 %fusion.4 = bf16[1,1024,512]{2,1,0:T(8,128)(2,1)} fusion(bf16[1024,512]{1,0:T(8,128)(2,1)S(1)} %convolution_convert_fusion, bf16[1024,512]{1,0:T(8,128)(2,1)S(1)} %convolution_convert_fusion.1, bf16[1024,512]{1,0:T(8,128)(2,1)S(1)} %convolution_convert_fusion.2, bf16[1024,512]{1,0:T(8,128)(2,1)S(1)} %convolution_convert_fusion.3, ...), kind=kOutput, calls=%fused_computation.19 | convolution fusion | flops 143130624 | bytes 8781824 | tf_op jit(solution)/shard_map/dot_general | solution.py:149
  180.2 1.9 fusion.3
  182.1 20.1 %reduce-scatter.5.cloned.1.call-done = f32[128,512]{1,0:T(8,128)} async-done(((f32[1024,512]{1,0:T(8,128)}), f32[128,512]{1,0:T(8,128)}) %reduce-scatter.5.cloned.1.call-update) | async-done | bytes 262160 | tf_op jit(solution)/shard_map/reduce_scatter | solution.py:160
  (66 shorter events, 26.9 us)
Async XLA Ops:
  7.2 3.1 %copy-start.1 = (bf16[1,128,8192]{2,1,0:T(8,128)(2,1)S(1)}, bf16[1,128,8192]{2,1,0:T(8,128)(2,1)}, u32[]{:S(2)}) copy-start(bf16[1,128,8192]{2,1,0:T(8,128)(2,1)} %param.7) | copy-start | bytes 6291460
  7.2 54.2 %reduce-scatter.3.cloned.1.call-start = ((), (), s32[]{:S(2)}) async-start(), calls=%async_computation.3 | async-start | bytes 2359296 | tf_op jit(solution)/shard_map/reduce_scatter | solution.py:93
  11.7 1.2 copy-start.4
  14.9 5.1 %copy-start.5 = (f32[16,512]{1,0:T(8,128)S(1)}, f32[16,512]{1,0:T(8,128)}, u32[]{:S(2)}) copy-start(f32[16,512]{1,0:T(8,128)} %param.12) | copy-start | bytes 98308
  14.9 5.1 %copy-start.6 = (f32[16,512]{1,0:T(8,128)S(1)}, f32[16,512]{1,0:T(8,128)}, u32[]{:S(2)}) copy-start(f32[16,512]{1,0:T(8,128)} %param.13) | copy-start | bytes 98308
  14.9 118.6 %all-to-all-start = ((bf16[8,128,1536]{2,1,0:T(8,128)(2,1)}), bf16[8,128,1536]{2,1,0:T(8,128)(2,1)S(1)}, u32[]{:S(2)}, u32[]{:S(2)}) async-start(bf16[8,128,1536]{2,1,0:T(8,128)(2,1)} %pad_maximum_fusion), calls=%async_computation | async-start | bytes 6291456 | tf_op jit(solution)/shard_map/all_to_all | solution.py:134
  19.9 135.7 %all-gather.5.cloned.1.call-start = ((), (), s32[]{:S(2)}) async-start(), calls=%async_computation.4 | async-start | bytes 1179648 | tf_op jit(solution)/shard_map/all_gather | solution.py:106
  20.0 59.4 %collective-permute-start = (f32[16,1024]{1,0:T(8,128)S(1)}, f32[16,1024]{1,0:T(8,128)S(1)}, u32[]{:S(2)}, u32[]{:S(2)}) collective-permute-start(f32[16,1024]{1,0:T(8,128)S(1)} %constant_dynamic-update-slice_fusion), channel_id=1, source_target_pairs={{0,8},{8,0},{1,9},{9,1},{2,10},{10,2},{3,11},{11,3},{4,12},{12,4},... | collective-permute-start | bytes 196616 | tf_op jit(solution)/shard_map/ppermute | solution.py:66
  61.4 20.7 %collective-permute-start.3 = (f32[128,512]{1,0:T(8,128)}, f32[128,512]{1,0:T(8,128)}, u32[]{:S(2)}, u32[]{:S(2)}) collective-permute-start(f32[128,512]{1,0:T(8,128)} %reduce-scatter.3.cloned.1.call-done), channel_id=1, source_target_pairs={{0,32},{16,48},{32,0},{48,16},{1,33},{17,49},{33,1},{49,17},{2,34}... | collective-permute-start | bytes 786440 | tf_op jit(solution)/shard_map/ppermute | solution.py:81
  79.4 7.3 %collective-permute-start.1 = (f32[32,1024]{1,0:T(8,128)S(1)}, f32[32,1024]{1,0:T(8,128)}, u32[]{:S(2)}, u32[]{:S(2)}) collective-permute-start(f32[32,1024]{1,0:T(8,128)S(1)} %maximum_select_fusion.2), channel_id=1, source_target_pairs={{0,16},{16,0},{32,48},{48,32},{1,17},{17,1},{33,49},{49,33},{2,18}... | collective-permute-start | bytes 393224 | tf_op jit(solution)/shard_map/ppermute | solution.py:66
  83.2 11.2 %collective-permute-start.4 = (f32[128,512]{1,0:T(8,128)S(1)}, f32[128,512]{1,0:T(8,128)}, u32[]{:S(2)}, u32[]{:S(2)}) collective-permute-start(f32[128,512]{1,0:T(8,128)S(1)} %add.90), channel_id=1, source_target_pairs={{0,16},{16,0},{32,48},{48,32},{1,17},{17,1},{33,49},{49,33},{2,18}... | collective-permute-start | bytes 786440 | tf_op jit(solution)/shard_map/ppermute | solution.py:81
  86.3 24.2 %copy-start.7 = (bf16[1024]{0:T(1024)(128)(2,1)S(1)}, bf16[1024]{0:T(1024)(128)(2,1)}, u32[]{:S(2)}) copy-start(bf16[1024]{0:T(1024)(128)(2,1)} %param.8) | copy-start | bytes 6148
  88.4 11.2 %collective-permute-start.2 = (f32[64,1024]{1,0:T(8,128)}, f32[64,1024]{1,0:T(8,128)}, u32[]{:S(2)}, u32[]{:S(2)}) collective-permute-start(f32[64,1024]{1,0:T(8,128)} %maximum_select_fusion.1), channel_id=1, source_target_pairs={{0,32},{16,48},{32,0},{48,16},{1,33},{17,49},{33,1},{49,17},{2,34}... | collective-permute-start | bytes 786440 | tf_op jit(solution)/shard_map/ppermute | solution.py:66
  96.1 12.5 %collective-permute-start.5 = (f32[128,512]{1,0:T(8,128)}, f32[128,512]{1,0:T(8,128)}, u32[]{:S(2)}, u32[]{:S(2)}) collective-permute-start(f32[128,512]{1,0:T(8,128)} %add.91), channel_id=1, source_target_pairs={{0,8},{8,0},{1,9},{9,1},{2,10},{10,2},{3,11},{11,3},{4,12},{12,4},... | collective-permute-start | bytes 786440 | tf_op jit(solution)/shard_map/ppermute | solution.py:81
  100.9 23.4 %copy-start.8 = (s32[1,128]{1,0:T(1,128)S(1)}, s32[1,128]{1,0:T(1,128)}, u32[]{:S(2)}) copy-start(s32[1,128]{1,0:T(1,128)} %param.9) | copy-start | bytes 1540
  110.5 91.8 %reduce-scatter.5.cloned.1.call-start = ((), (), s32[]{:S(2)}) async-start(), calls=%async_computation.5 | async-start | bytes 2359296 | tf_op jit(solution)/shard_map/reduce_scatter | solution.py:160
  133.7 1.3 copy-start.2
  173.2 1.6 copy-start
  178.0 2.2 %copy-start.3 = (bf16[8,128,1024]{2,1,0:T(8,128)(2,1)S(1)}, bf16[8,128,1024]{2,1,0:T(8,128)(2,1)}, u32[]{:S(2)}) copy-start(bf16[8,128,1024]{2,1,0:T(8,128)(2,1)} %copy-done.2) | copy-start | bytes 6291460
  178.0 2.2 %copy-start.9 = (bf16[1024,512]{1,0:T(8,128)(2,1)S(1)}, bf16[1024,512]{1,0:T(8,128)(2,1)}, u32[]{:S(2)}) copy-start(bf16[1024,512]{1,0:T(8,128)(2,1)} %all-gather.5.cloned.1.call-done) | copy-start | bytes 3145732
Sparse Core Ops, SparseCore 0:
  10.8 50.5 reduce-scatter.2
  110.6 44.9 all-gather.4
  160.2 42.0 reduce-scatter.4

commit v8 on v7

--- a/solution.py
+++ b/solution.py
@@ -93,8 +93,11 @@
     summed = lax.psum_scatter(summed, island_axes[0], scatter_dimension=0, tiled=True)
     rest = island_axes[1:]
     state = jnp.concatenate([outer_weight, momentum], axis=1)
+    first_gathered = None
     for ax in reversed(rest):
         state = doubling_gather(state, ax)
+        if first_gathered is None:
+            first_gathered = state
     for ax in rest:
         summed = doubling_sum(summed, ax)
     cols = outer_weight.shape[1]
@@ -131,6 +134,8 @@
         ],
         axis=2,
     )
+    if first_gathered is not None:
+        _, outgoing = lax.optimization_barrier((first_gathered, outgoing))
     incoming = lax.all_to_all(outgoing, "fsdp", split_axis=0, concat_axis=0, tiled=True)
     columns = incoming[:, :, :width].reshape(seq, width)
     all_cot = incoming[:, :, width:].reshape(seq, cols_out)

time: 212 us -> 198 us (0.934)
  waiting for transfers between devices: 99 us -> 84.6 us
  starting transfers between devices: 27.6 us -> 30 us
    ppermute x3, waiting for transfers between devices: 14.9 us -> 0.01 us  [doubling_gather(): got = lax.ppermute(values, axis, [(j, j ^ step) for j in range(n)])]
    ppermute x3, waiting for transfers between devices: 10.4 us -> 14.6 us  [doubling_sum(): lax.ppermute(values, axis, [(j, j ^ step) for j in range(n)])]
    ppermute x3, starting transfers between devices: 9.93 us -> 13.5 us  [doubling_sum(): lax.ppermute(values, axis, [(j, j ^ step) for j in range(n)])]
    all_gather x1, waiting for transfers between devices: 18.7 us -> 15.2 us  [body(): lax.all_gather(weight_shard, island_axes[0], axis=0, tiled=True)]
  transfers between devices with their start and end apart: 10 -> 10, of which waited for: 7 -> 6; matrix products, arithmetic and copies ran while one was open for 18% -> 19% of each run, Pallas kernels for 0% -> 0%
where the time goes in v8:
time: 198 us; the launch traced here: 197 us
  waiting for transfers between devices  84.6 us (43%)
  starting transfers between devices  30 us (15%)
  other arithmetic  27.5 us (14%)
  blocking collectives  19 us (10%)
  between operations  14.2 us (7%)
  matrix products  11.7 us (6%)
  local copies, waits for them, and re-layouts  10.4 us (5%)
    reduce_scatter x1, waiting for transfers between devices, body(): lax.psum_scatter(summed, island_axes[0], scatter_dimension=0, tiled=True)  35 us
    reduce_scatter x1, waiting for transfers between devices, body(): lax.psum_scatter(partial_keys, 'fsdp', scatter_dimension=0, tiled=True)  19.7 us
    all_gather x1, waiting for transfers between devices, body(): lax.all_gather(weight_shard, island_axes[0], axis=0, tiled=True)  15.2 us
    ppermute x3, waiting for transfers between devices, doubling_sum(): lax.ppermute(values, axis, [(j, j ^ step) for j in range(n)])  14.6 us
    ppermute x3, starting transfers between devices, doubling_sum(): lax.ppermute(values, axis, [(j, j ^ step) for j in range(n)])  13.5 us
    ppermute x3, starting transfers between devices, doubling_gather(): got = lax.ppermute(values, axis, [(j, j ^ step) for j in range(n)])  12.7 us
    all_gather x1, blocking collectives, body(): all_scales = lax.all_gather(row_scale, 'fsdp', axis=0, tiled=True)  10 us
    all_gather x1, blocking collectives, body(): all_docs = lax.all_gather(doc_ids[0], 'fsdp', axis=0, tiled=True)  8.95 us
  transfers between devices with their start and end apart: 10, of which 6 were waited for; matrix products, arithmetic and copies ran while one was open for 19% of the time, Pallas kernels for 0%

profile of v8, /device:TPU:6, one launch (start us, length us, event | category | flops | bytes accessed | tf_op | source)
XLA Modules:
  0.0 197.3 jit_solution(10125187881662655797)
XLA Ops:
  7.2 3.0 %bitcast_convert_fusion = f32[1024,512]{1,0:T(8,128)} fusion(bf16[1,1024,512]{2,1,0:T(8,128)(2,1)} %param.11), kind=kLoop, calls=%fused_computation.23 | loop fusion | flops 524288 | bytes 3145728 | tf_op jit(solution)/shard_map/convert_element_type | solution.py:92
  10.3 7.7 %collective-permute-start = (f32[16,1024]{1,0:T(8,128)S(1)}, f32[16,1024]{1,0:T(8,128)S(1)}, u32[]{:S(2)}, u32[]{:S(2)}) collective-permute-start(f32[16,1024]{1,0:T(8,128)S(1)} %constant_dynamic-update-slice_fusion), channel_id=1, source_target_pairs={{0,8},{8,0},{1,9},{9,1},{2,10},{10,2},{3,11},{11,3},{4,12},{12,4},... | collective-permute-start | bytes 196616 | tf_op jit(solution)/shard_map/ppermute | solution.py:66
  20.8 1.9 pad_maximum_fusion
  22.7 3.7 %all-to-all-start = ((bf16[8,128,1536]{2,1,0:T(8,128)(2,1)}), bf16[8,128,1536]{2,1,0:T(8,128)(2,1)S(1)}, u32[]{:S(2)}, u32[]{:S(2)}) async-start(bf16[8,128,1536]{2,1,0:T(8,128)(2,1)} %pad_maximum_fusion), calls=%async_computation | async-start | bytes 6291456 | tf_op jit(solution)/shard_map/all_to_all | solution.py:139
  26.4 35.0 %reduce-scatter.3.cloned.1.call-done = f32[128,512]{1,0:T(8,128)} async-done(((f32[1024,512]{1,0:T(8,128)}), f32[128,512]{1,0:T(8,128)}) %reduce-scatter.3.cloned.1.call-update) | async-done | bytes 262160 | tf_op jit(solution)/shard_map/reduce_scatter | solution.py:93
  61.4 3.4 %collective-permute-start.3 = (f32[128,512]{1,0:T(8,128)}, f32[128,512]{1,0:T(8,128)S(1)}, u32[]{:S(2)}, u32[]{:S(2)}) collective-permute-start(f32[128,512]{1,0:T(8,128)} %reduce-scatter.3.cloned.1.call-done), channel_id=1, source_target_pairs={{0,32},{16,48},{32,0},{48,16},{1,33},{17,49},{33,1},{49,17},{2,34}... | collective-permute-start | bytes 786440 | tf_op jit(solution)/shard_map/ppermute | solution.py:81
  64.8 1.9 collective-permute-start.1
  66.7 4.7 %collective-permute-done.3 = f32[128,512]{1,0:T(8,128)S(1)} collective-permute-done((f32[128,512]{1,0:T(8,128)}, f32[128,512]{1,0:T(8,128)S(1)}, u32[]{:S(2)}, u32[]{:S(2)}) %collective-permute-start.3) | collective-permute-done | bytes 262176 | tf_op jit(solution)/shard_map/ppermute | solution.py:81
  72.4 2.8 %collective-permute-start.4 = (f32[128,512]{1,0:T(8,128)S(1)}, f32[128,512]{1,0:T(8,128)}, u32[]{:S(2)}, u32[]{:S(2)}) collective-permute-start(f32[128,512]{1,0:T(8,128)S(1)} %add.90), channel_id=1, source_target_pairs={{0,16},{16,0},{32,48},{48,32},{1,17},{17,1},{33,49},{49,33},{2,18}... | collective-permute-start | bytes 786440 | tf_op jit(solution)/shard_map/ppermute | solution.py:81
  76.9 3.0 %collective-permute-start.2 = (f32[64,1024]{1,0:T(8,128)}, f32[64,1024]{1,0:T(8,128)}, u32[]{:S(2)}, u32[]{:S(2)}) collective-permute-start(f32[64,1024]{1,0:T(8,128)} %maximum_select_fusion.1), channel_id=1, source_target_pairs={{0,32},{16,48},{32,0},{48,16},{1,33},{17,49},{33,1},{49,17},{2,34}... | collective-permute-start | bytes 786440 | tf_op jit(solution)/shard_map/ppermute | solution.py:66
  79.9 2.0 %collective-permute-done.4 = f32[128,512]{1,0:T(8,128)} collective-permute-done((f32[128,512]{1,0:T(8,128)S(1)}, f32[128,512]{1,0:T(8,128)}, u32[]{:S(2)}, u32[]{:S(2)}) %collective-permute-start.4) | collective-permute-done | bytes 262176 | tf_op jit(solution)/shard_map/ppermute | solution.py:81
  83.6 7.4 %collective-permute-start.5 = (f32[128,512]{1,0:T(8,128)}, f32[128,512]{1,0:T(8,128)}, u32[]{:S(2)}, u32[]{:S(2)}) collective-permute-start(f32[128,512]{1,0:T(8,128)} %add.91), channel_id=1, source_target_pairs={{0,8},{8,0},{1,9},{9,1},{2,10},{10,2},{3,11},{11,3},{4,12},{12,4},... | collective-permute-start | bytes 786440 | tf_op jit(solution)/shard_map/ppermute | solution.py:81
  92.3 7.9 %collective-permute-done.5 = f32[128,512]{1,0:T(8,128)} collective-permute-done((f32[128,512]{1,0:T(8,128)}, f32[128,512]{1,0:T(8,128)}, u32[]{:S(2)}, u32[]{:S(2)}) %collective-permute-start.5) | collective-permute-done | bytes 262176 | tf_op jit(solution)/shard_map/ppermute | solution.py:81
  102.2 2.1 %multiply_reduce_fusion = f32[128]{0:T(128)S(1)} fusion(bf16[1,128,8192]{2,1,0:T(8,128)(2,1)} %param.7), kind=kLoop, calls=%fused_computation.5 | loop fusion | flops 3145600 | bytes 2097664 | tf_op jit(solution)/shard_map/reduce_sum | solution.py:145
  104.3 10.0 %all-gather.2 = f32[8,1,128]{2,1,0:T(1,128)S(1)} all-gather(f32[1,1,128]{2,1,0:T(1,128)S(1)} %rsqrt_bitcast_fusion), channel_id=2, replica_groups=mesh['island0'=8,'island1'=4,'island2'=2,'fsdp'=8] {'fsdp'}, dimensions={0}, use_global_device_ids=true | all-gather | bytes 4608 | tf_op jit(solution)/shard_map/all_gather | solution.py:146
  114.3 8.9 %all-gather.1 = s32[1,1024]{1,0:T(1,128)S(1)} all-gather(s32[1,128]{1,0:T(1,128)S(1)} %copy-done.8), channel_id=3, replica_groups=mesh['island0'=8,'island1'=4,'island2'=2,'fsdp'=8] {'fsdp'}, dimensions={1}, use_global_device_ids=true | all-gather | bytes 4608 | tf_op jit(solution)/shard_map/all_gather | solution.py:120
  127.0 15.2 %all-gather.5.cloned.1.call-done = bf16[1024,512]{1,0:T(8,128)(2,1)} async-done(((bf16[128,512]{1,0:T(8,128)(2,1)}), bf16[1024,512]{1,0:T(8,128)(2,1)}) %all-gather.5.cloned.1.call-update) | async-done | bytes 1048592 | tf_op jit(solution)/shard_map/all_gather | solution.py:109
  142.2 4.4 %fusion.33 = f32[1024,512]{1,0:T(8,128)} fusion(bf16[1024,1024]{1,0:T(8,128)(2,1)} %fusion.2, bf16[1024,512]{1,0:T(8,128)(2,1)} %all-gather.5.cloned.1.call-done), kind=kOutput, calls=%fused_computation.83 | convolution fusion | flops 1073741824 | bytes 5242880 | tf_op jit(solution)/shard_map/dot_general | solution.py:164
  146.7 3.2 %broadcast_multiply_fusion = (f32[1024,64]{1,0:T(8,128)}, f32[1024,64]{1,0:T(8,128)}, f32[1024,64]{1,0:T(8,128)}) fusion(f32[64]{0:T(128)S(1)} %multiply_exponential_fusion, f32[1024]{0:T(1024)S(1)} %subtract_convert_fusion.2), kind=kLoop, calls=%fused_computation.39 | loop fusion | flops 131072 | bytes 790784 | tf_op jit(solution)/shard_map/mul | solution.py:39
  153.8 1.9 reshape.137
  155.7 2.6 %subtract_convert_fusion = (bf16[1024,4,64]{2,1,0:T(4,128)(2,1)S(1)}, bf16[1024,4,64]{2,1,0:T(4,128)(2,1)S(1)}) fusion(f32[1024,4,128]{2,1,0:T(4,128)S(1)} %reshape.137, f32[1024,64]{1,0:T(8,128)} %get-tuple-element.22, f32[1024,64]{1,0:T(8,128)} %get-tuple-element.24), kind=kLoop, calls=%fused_computation.10 | loop fusion | flops 2097152 | bytes 3670016 | tf_op jit(solution)/shard_map/convert.3
  164.7 2.2 %fusion.4 = bf16[1,1024,512]{2,1,0:T(8,128)(2,1)} fusion(bf16[1024,512]{1,0:T(8,128)(2,1)S(1)} %convolution_convert_fusion, bf16[1024,512]{1,0:T(8,128)(2,1)S(1)} %convolution_convert_fusion.1, bf16[1024,512]{1,0:T(8,128)(2,1)S(1)} %convolution_convert_fusion.2, bf16[1024,512]{1,0:T(8,128)(2,1)S(1)} %convolution_convert_fusion.3, ...), kind=kOutput, calls=%fused_computation.19 | convolution fusion | flops 143130624 | bytes 8781824 | tf_op jit(solution)/shard_map/dot_general | solution.py:154
  166.9 1.9 fusion.3
  168.8 19.7 %reduce-scatter.5.cloned.1.call-done = f32[128,512]{1,0:T(8,128)} async-done(((f32[1024,512]{1,0:T(8,128)}), f32[128,512]{1,0:T(8,128)}) %reduce-scatter.5.cloned.1.call-update) | async-done | bytes 262160 | tf_op jit(solution)/shard_map/reduce_scatter | solution.py:165
  (66 shorter events, 26.5 us)
Async XLA Ops:
  7.2 3.1 %copy-start.5 = (f32[16,512]{1,0:T(8,128)S(1)}, f32[16,512]{1,0:T(8,128)}, u32[]{:S(2)}) copy-start(f32[16,512]{1,0:T(8,128)} %param.12) | copy-start | bytes 98308
  7.2 3.1 %copy-start.6 = (f32[16,512]{1,0:T(8,128)S(1)}, f32[16,512]{1,0:T(8,128)}, u32[]{:S(2)}) copy-start(f32[16,512]{1,0:T(8,128)} %param.13) | copy-start | bytes 98308
  7.2 10.9 %copy-start.1 = (bf16[1,128,8192]{2,1,0:T(8,128)(2,1)S(1)}, bf16[1,128,8192]{2,1,0:T(8,128)(2,1)}, u32[]{:S(2)}) copy-start(bf16[1,128,8192]{2,1,0:T(8,128)(2,1)} %param.7) | copy-start | bytes 6291460
  7.2 54.2 %reduce-scatter.3.cloned.1.call-start = ((), (), s32[]{:S(2)}) async-start(), calls=%async_computation.3 | async-start | bytes 2359296 | tf_op jit(solution)/shard_map/reduce_scatter | solution.py:93
  10.3 12.4 %collective-permute-start = (f32[16,1024]{1,0:T(8,128)S(1)}, f32[16,1024]{1,0:T(8,128)S(1)}, u32[]{:S(2)}, u32[]{:S(2)}) collective-permute-start(f32[16,1024]{1,0:T(8,128)S(1)} %constant_dynamic-update-slice_fusion), channel_id=1, source_target_pairs={{0,8},{8,0},{1,9},{9,1},{2,10},{10,2},{3,11},{11,3},{4,12},{12,4},... | collective-permute-start | bytes 196616 | tf_op jit(solution)/shard_map/ppermute | solution.py:66
  19.5 1.2 copy-start.4
  22.7 100.8 %all-to-all-start = ((bf16[8,128,1536]{2,1,0:T(8,128)(2,1)}), bf16[8,128,1536]{2,1,0:T(8,128)(2,1)S(1)}, u32[]{:S(2)}, u32[]{:S(2)}) async-start(bf16[8,128,1536]{2,1,0:T(8,128)(2,1)} %pad_maximum_fusion), calls=%async_computation | async-start | bytes 6291456 | tf_op jit(solution)/shard_map/all_to_all | solution.py:139
  26.4 115.9 %all-gather.5.cloned.1.call-start = ((), (), s32[]{:S(2)}) async-start(), calls=%async_computation.4 | async-start | bytes 1179648 | tf_op jit(solution)/shard_map/all_gather | solution.py:109
  61.4 10.0 %collective-permute-start.3 = (f32[128,512]{1,0:T(8,128)}, f32[128,512]{1,0:T(8,128)S(1)}, u32[]{:S(2)}, u32[]{:S(2)}) collective-permute-start(f32[128,512]{1,0:T(8,128)} %reduce-scatter.3.cloned.1.call-done), channel_id=1, source_target_pairs={{0,32},{16,48},{32,0},{48,16},{1,33},{17,49},{33,1},{49,17},{2,34}... | collective-permute-start | bytes 786440 | tf_op jit(solution)/shard_map/ppermute | solution.py:81
  64.8 10.4 %collective-permute-start.1 = (f32[32,1024]{1,0:T(8,128)S(1)}, f32[32,1024]{1,0:T(8,128)}, u32[]{:S(2)}, u32[]{:S(2)}) collective-permute-start(f32[32,1024]{1,0:T(8,128)S(1)} %maximum_select_fusion.2), channel_id=1, source_target_pairs={{0,16},{16,0},{32,48},{48,32},{1,17},{17,1},{33,49},{49,33},{2,18}... | collective-permute-start | bytes 393224 | tf_op jit(solution)/shard_map/ppermute | solution.py:66
  72.4 9.5 %collective-permute-start.4 = (f32[128,512]{1,0:T(8,128)S(1)}, f32[128,512]{1,0:T(8,128)}, u32[]{:S(2)}, u32[]{:S(2)}) collective-permute-start(f32[128,512]{1,0:T(8,128)S(1)} %add.90), channel_id=1, source_target_pairs={{0,16},{16,0},{32,48},{48,32},{1,17},{17,1},{33,49},{49,33},{2,18}... | collective-permute-start | bytes 786440 | tf_op jit(solution)/shard_map/ppermute | solution.py:81
  75.2 27.0 %copy-start.7 = (bf16[1024]{0:T(1024)(128)(2,1)S(1)}, bf16[1024]{0:T(1024)(128)(2,1)}, u32[]{:S(2)}) copy-start(bf16[1024]{0:T(1024)(128)(2,1)} %param.8) | copy-start | bytes 6148
  76.9 14.1 %collective-permute-start.2 = (f32[64,1024]{1,0:T(8,128)}, f32[64,1024]{1,0:T(8,128)}, u32[]{:S(2)}, u32[]{:S(2)}) collective-permute-start(f32[64,1024]{1,0:T(8,128)} %maximum_select_fusion.1), channel_id=1, source_target_pairs={{0,32},{16,48},{32,0},{48,16},{1,33},{17,49},{33,1},{49,17},{2,34}... | collective-permute-start | bytes 786440 | tf_op jit(solution)/shard_map/ppermute | solution.py:66
  83.6 16.6 %collective-permute-start.5 = (f32[128,512]{1,0:T(8,128)}, f32[128,512]{1,0:T(8,128)}, u32[]{:S(2)}, u32[]{:S(2)}) collective-permute-start(f32[128,512]{1,0:T(8,128)} %add.91), channel_id=1, source_target_pairs={{0,8},{8,0},{1,9},{9,1},{2,10},{10,2},{3,11},{11,3},{4,12},{12,4},... | collective-permute-start | bytes 786440 | tf_op jit(solution)/shard_map/ppermute | solution.py:81
  92.3 22.0 %copy-start.8 = (s32[1,128]{1,0:T(1,128)S(1)}, s32[1,128]{1,0:T(1,128)}, u32[]{:S(2)}) copy-start(s32[1,128]{1,0:T(1,128)} %param.9) | copy-start | bytes 1540
  102.1 86.4 %reduce-scatter.5.cloned.1.call-start = ((), (), s32[]{:S(2)}) async-start(), calls=%async_computation.5 | async-start | bytes 2359296 | tf_op jit(solution)/shard_map/reduce_scatter | solution.py:165
  123.8 1.3 copy-start.2
  159.8 1.6 copy-start
  164.6 2.2 %copy-start.3 = (bf16[8,128,1024]{2,1,0:T(8,128)(2,1)S(1)}, bf16[8,128,1024]{2,1,0:T(8,128)(2,1)}, u32[]{:S(2)}) copy-start(bf16[8,128,1024]{2,1,0:T(8,128)(2,1)} %copy-done.2) | copy-start | bytes 6291460
  164.7 2.2 %copy-start.9 = (bf16[1024,512]{1,0:T(8,128)(2,1)S(1)}, bf16[1024,512]{1,0:T(8,128)(2,1)}, u32[]{:S(2)}) copy-start(bf16[1024,512]{1,0:T(8,128)(2,1)} %all-gather.5.cloned.1.call-done) | copy-start | bytes 3145732
Sparse Core Ops, SparseCore 0:
  10.8 50.5 reduce-scatter.2
  102.2 39.9 all-gather.4
  146.8 41.6 reduce-scatter.4

commit v9 on v8

--- a/solution.py
+++ b/solution.py
@@ -117,33 +117,42 @@
     tok_rows = hidden.shape[1]
     seq = tok_rows * fsdp_ways
     me = lax.axis_index("fsdp")
-    all_docs = lax.all_gather(doc_ids[0], "fsdp", axis=0, tiled=True)
     indices = jnp.arange(seq, dtype=jnp.int32)
     documents = jnp.arange(DOCS, dtype=jnp.int32)
+    hidden_f = hidden[0].astype(jnp.float32)
+    row_scale = lax.rsqrt(jnp.mean(hidden_f * hidden_f, axis=1, keepdims=True) + norm_eps)
+    width = hidden.shape[2] // fsdp_ways
+    cols_out = cotangent.shape[2]
+    scale_high = lax.reduce_precision(row_scale, exponent_bits=8, mantissa_bits=7)
+    scale_mid = lax.reduce_precision(row_scale - scale_high, exponent_bits=8, mantissa_bits=7)
+    scale_low = row_scale - scale_high - scale_mid
+    extras = jnp.concatenate(
+        [doc_ids[0][:, None].astype(jnp.float32), scale_high, scale_mid, scale_low], axis=1
+    ).astype(jnp.bfloat16)
+    extras = jnp.pad(extras, ((0, 0), (0, 128 - extras.shape[1])))
+    outgoing = jnp.concatenate(
+        [
+            hidden[0].reshape(tok_rows, fsdp_ways, width).transpose(1, 0, 2),
+            jnp.broadcast_to(cotangent[0][None], (fsdp_ways, tok_rows, cols_out)),
+            jnp.broadcast_to(extras[None], (fsdp_ways,) + extras.shape),
+        ],
+        axis=2,
+    )
+    if first_gathered is not None:
+        _, outgoing = lax.optimization_barrier((first_gathered, outgoing))
+    incoming = lax.all_to_all(outgoing, "fsdp", split_axis=0, concat_axis=0, tiled=True)
+    columns = incoming[:, :, :width].reshape(seq, width)
+    all_cot = incoming[:, :, width : width + cols_out].reshape(seq, cols_out)
+    all_extras = incoming[:, :, width + cols_out :].reshape(seq, -1).astype(jnp.float32)
+    all_docs = all_extras[:, 0].astype(jnp.int32)
+    all_scales = (all_extras[:, 1:2] + all_extras[:, 2:3]) + all_extras[:, 3:4]
     in_document = all_docs[:, None] == documents[None, :]
     starts = jnp.min(jnp.where(in_document, indices[:, None], far_index), axis=0)
     doc_start = jnp.sum(jnp.where(in_document, starts[None, :], 0), axis=1)
     positions = (indices - doc_start).astype(jnp.float32)
     cosine, sine_part = angles_for(positions, HEAD)
-    width = hidden.shape[2] // fsdp_ways
-    cols_out = cotangent.shape[2]
-    outgoing = jnp.concatenate(
-        [
-            hidden[0].reshape(tok_rows, fsdp_ways, width).transpose(1, 0, 2),
-            jnp.broadcast_to(cotangent[0][None], (fsdp_ways, tok_rows, cols_out)),
-        ],
-        axis=2,
-    )
-    if first_gathered is not None:
-        _, outgoing = lax.optimization_barrier((first_gathered, outgoing))
-    incoming = lax.all_to_all(outgoing, "fsdp", split_axis=0, concat_axis=0, tiled=True)
-    columns = incoming[:, :, :width].reshape(seq, width)
-    all_cot = incoming[:, :, width:].reshape(seq, cols_out)
     all_back = rotate(all_cot.astype(jnp.float32), cosine, sine_part, -1.0).astype(jnp.bfloat16)
 
-    hidden_f = hidden[0].astype(jnp.float32)
-    row_scale = lax.rsqrt(jnp.mean(hidden_f * hidden_f, axis=1, keepdims=True) + norm_eps)
-    all_scales = lax.all_gather(row_scale, "fsdp", axis=0, tiled=True)
     normed_cols = columns.astype(jnp.float32) * all_scales
     act_cols = (normed_cols * gain.astype(jnp.float32)[None, :]).astype(jnp.bfloat16)
 

time: 198 us -> 219 us (1.11)
  waiting for transfers between devices: 84.6 us -> 121 us
  blocking collectives: 19 us -> 0 us
  local copies, waits for them, and re-layouts: 10.4 us -> 15.2 us
    all_gather x2 -> x0, blocking collectives: 19 us -> none  [the longest x1 10 us: body(): all_scales = lax.all_gather(row_scale, 'fsdp', axis=0, tiled=True)]
    all_gather x1, waiting for transfers between devices: 15.2 us -> 31.7 us  [body(): lax.all_gather(weight_shard, island_axes[0], axis=0, tiled=True)]
    reduce_scatter x1, waiting for transfers between devices: 35 us -> 49.5 us  [body(): lax.psum_scatter(summed, island_axes[0], scatter_dimension=0, tiled=True)]
    reduce_scatter x1, waiting for transfers between devices: 19.7 us -> 25.9 us  [body(): lax.psum_scatter(partial_keys, 'fsdp', scatter_dimension=0, tiled=True)]
    unnamed x22 -> x23, local copies, waits for them, and re-layouts: 2.93 us -> 7.57 us
    convert_element_type x0 -> x3, other arithmetic: none -> 2.49 us  [the longest x1 1.78 us: body(): all_docs = all_extras[:, 0].astype(jnp.int32)]
  transfers between devices with their start and end apart: 10 -> 10, of which waited for: 6 -> 6; matrix products, arithmetic and copies ran while one was open for 19% -> 21% of each run, Pallas kernels for 0% -> 0%
where the time goes in v9:
time: 219 us; the launch traced here: 218 us
  waiting for transfers between devices  121 us (55%)
  starting transfers between devices  29.1 us (13%)
  other arithmetic  27.4 us (13%)
  local copies, waits for them, and re-layouts  15.2 us (7%)
  between operations  14.2 us (6%)
  matrix products  11 us (5%)
    reduce_scatter x1, waiting for transfers between devices, body(): lax.psum_scatter(summed, island_axes[0], scatter_dimension=0, tiled=True)  49.5 us
    all_gather x1, waiting for transfers between devices, body(): lax.all_gather(weight_shard, island_axes[0], axis=0, tiled=True)  31.7 us
    reduce_scatter x1, waiting for transfers between devices, body(): lax.psum_scatter(partial_keys, 'fsdp', scatter_dimension=0, tiled=True)  25.9 us
    ppermute x3, waiting for transfers between devices, doubling_sum(): lax.ppermute(values, axis, [(j, j ^ step) for j in range(n)])  14.3 us
    ppermute x3, starting transfers between devices, doubling_gather(): got = lax.ppermute(values, axis, [(j, j ^ step) for j in range(n)])  12.7 us
    ppermute x3, starting transfers between devices, doubling_sum(): lax.ppermute(values, axis, [(j, j ^ step) for j in range(n)])  12.6 us
    unnamed x23, local copies, waits for them, and re-layouts  7.57 us
    dot_general x8, matrix products, body(): lax.dot_general(act_block, back_block, (((0,), (0,)), ((), ())), preferre...  5.31 us
  transfers between devices with their start and end apart: 10, of which 6 were waited for; matrix products, arithmetic and copies ran while one was open for 21% of the time, Pallas kernels for 0%

profile of v9, /device:TPU:6, one launch (start us, length us, event | category | flops | bytes accessed | tf_op | source)
XLA Modules:
  0.0 218.4 jit_solution(11528407154966214646)
XLA Ops:
  8.8 7.7 %collective-permute-start = (f32[16,1024]{1,0:T(8,128)S(1)}, f32[16,1024]{1,0:T(8,128)S(1)}, u32[]{:S(2)}, u32[]{:S(2)}) collective-permute-start(f32[16,1024]{1,0:T(8,128)S(1)} %constant_dynamic-update-slice_fusion), channel_id=1, source_target_pairs={{0,8},{8,0},{1,9},{9,1},{2,10},{10,2},{3,11},{11,3},{4,12},{12,4},... | collective-permute-start | bytes 196616 | tf_op jit(solution)/shard_map/ppermute | solution.py:66
  17.2 2.1 multiply_reduce_fusion
  22.2 1.9 pad_maximum_fusion
  24.1 3.7 %all-to-all-start = ((bf16[8,128,1664]{2,1,0:T(8,128)(2,1)}), bf16[8,128,1664]{2,1,0:T(8,128)(2,1)S(1)}, u32[]{:S(2)}, u32[]{:S(2)}) async-start(bf16[8,128,1664]{2,1,0:T(8,128)(2,1)} %pad_maximum_fusion), calls=%async_computation | async-start | bytes 6815744 | tf_op jit(solution)/shard_map/all_to_all | solution.py:143
  27.9 2.9 %bitcast_convert_fusion = f32[1024,512]{1,0:T(8,128)} fusion(bf16[1,1024,512]{2,1,0:T(8,128)(2,1)} %param.11), kind=kLoop, calls=%fused_computation.23 | loop fusion | flops 524288 | bytes 3145728 | tf_op jit(solution)/shard_map/convert_element_type | solution.py:92
  30.8 49.5 %reduce-scatter.3.cloned.1.call-done = f32[128,512]{1,0:T(8,128)} async-done(((f32[1024,512]{1,0:T(8,128)}), f32[128,512]{1,0:T(8,128)}) %reduce-scatter.3.cloned.1.call-update) | async-done | bytes 262160 | tf_op jit(solution)/shard_map/reduce_scatter | solution.py:93
  80.3 3.0 %collective-permute-start.3 = (f32[128,512]{1,0:T(8,128)}, f32[128,512]{1,0:T(8,128)S(1)}, u32[]{:S(2)}, u32[]{:S(2)}) collective-permute-start(f32[128,512]{1,0:T(8,128)} %reduce-scatter.3.cloned.1.call-done), channel_id=1, source_target_pairs={{0,32},{16,48},{32,0},{48,16},{1,33},{17,49},{33,1},{49,17},{2,34}... | collective-permute-start | bytes 786440 | tf_op jit(solution)/shard_map/ppermute | solution.py:81
  83.3 1.9 collective-permute-start.1
  85.2 5.0 %collective-permute-done.3 = f32[128,512]{1,0:T(8,128)S(1)} collective-permute-done((f32[128,512]{1,0:T(8,128)}, f32[128,512]{1,0:T(8,128)S(1)}, u32[]{:S(2)}, u32[]{:S(2)}) %collective-permute-start.3) | collective-permute-done | bytes 262176 | tf_op jit(solution)/shard_map/ppermute | solution.py:81
  91.9 2.4 %collective-permute-start.4 = (f32[128,512]{1,0:T(8,128)}, f32[128,512]{1,0:T(8,128)}, u32[]{:S(2)}, u32[]{:S(2)}) collective-permute-start(f32[128,512]{1,0:T(8,128)} %add.108), channel_id=1, source_target_pairs={{0,16},{16,0},{32,48},{48,32},{1,17},{17,1},{33,49},{49,33},{2,18}... | collective-permute-start | bytes 786440 | tf_op jit(solution)/shard_map/ppermute | solution.py:81
  96.1 3.0 %collective-permute-start.2 = (f32[64,1024]{1,0:T(8,128)}, f32[64,1024]{1,0:T(8,128)}, u32[]{:S(2)}, u32[]{:S(2)}) collective-permute-start(f32[64,1024]{1,0:T(8,128)} %maximum_select_fusion.1), channel_id=1, source_target_pairs={{0,32},{16,48},{32,0},{48,16},{1,33},{17,49},{33,1},{49,17},{2,34}... | collective-permute-start | bytes 786440 | tf_op jit(solution)/shard_map/ppermute | solution.py:66
  102.5 7.2 %collective-permute-start.5 = (f32[128,512]{1,0:T(8,128)}, f32[128,512]{1,0:T(8,128)}, u32[]{:S(2)}, u32[]{:S(2)}) collective-permute-start(f32[128,512]{1,0:T(8,128)} %add.109), channel_id=1, source_target_pairs={{0,8},{8,0},{1,9},{9,1},{2,10},{10,2},{3,11},{11,3},{4,12},{12,4},... | collective-permute-start | bytes 786440 | tf_op jit(solution)/shard_map/ppermute | solution.py:81
  111.0 7.7 %collective-permute-done.5 = f32[128,512]{1,0:T(8,128)} collective-permute-done((f32[128,512]{1,0:T(8,128)}, f32[128,512]{1,0:T(8,128)}, u32[]{:S(2)}, u32[]{:S(2)}) %collective-permute-start.5) | collective-permute-done | bytes 262176 | tf_op jit(solution)/shard_map/ppermute | solution.py:81
  118.7 2.0 fusion.33
  122.3 1.8 slice_convert_fusion.1
  129.5 1.9 slice_convert_fusion
  131.9 31.7 %all-gather.2.cloned.1.call-done = bf16[1024,512]{1,0:T(8,128)(2,1)} async-done(((bf16[128,512]{1,0:T(8,128)(2,1)}), bf16[1024,512]{1,0:T(8,128)(2,1)}) %all-gather.2.cloned.1.call-update) | async-done | bytes 1048592 | tf_op jit(solution)/shard_map/all_gather | solution.py:109
  163.6 3.8 %fusion.34 = f32[1024,512]{1,0:T(8,128)} fusion(bf16[1024,1024]{1,0:T(8,128)(2,1)S(1)} %fusion.2, bf16[1024,512]{1,0:T(8,128)(2,1)} %all-gather.2.cloned.1.call-done), kind=kOutput, calls=%fused_computation.93 | convolution fusion | flops 1073741824 | bytes 5242880 | tf_op jit(solution)/shard_map/dot_general | solution.py:173
  167.5 2.1 reshape.179
  169.7 1.9 broadcast_multiply_fusion
  171.6 1.8 subtract_convert_fusion
  179.6 2.2 fusion.4
  181.8 1.9 fusion.3
  183.7 25.9 %reduce-scatter.5.cloned.1.call-done = f32[128,512]{1,0:T(8,128)} async-done(((f32[1024,512]{1,0:T(8,128)}), f32[128,512]{1,0:T(8,128)}) %reduce-scatter.5.cloned.1.call-update) | async-done | bytes 262160 | tf_op jit(solution)/shard_map/reduce_scatter | solution.py:174
  (73 shorter events, 29.3 us)
Async XLA Ops:
  7.2 12.3 %copy-start.2 = (bf16[1,128,8192]{2,1,0:T(8,128)(2,1)S(1)}, bf16[1,128,8192]{2,1,0:T(8,128)(2,1)}, u32[]{:S(2)}) copy-start(bf16[1,128,8192]{2,1,0:T(8,128)(2,1)} %param.7) | copy-start | bytes 6291460
  8.8 15.3 %collective-permute-start = (f32[16,1024]{1,0:T(8,128)S(1)}, f32[16,1024]{1,0:T(8,128)S(1)}, u32[]{:S(2)}, u32[]{:S(2)}) collective-permute-start(f32[16,1024]{1,0:T(8,128)S(1)} %constant_dynamic-update-slice_fusion), channel_id=1, source_target_pairs={{0,8},{8,0},{1,9},{9,1},{2,10},{10,2},{3,11},{11,3},{4,12},{12,4},... | collective-permute-start | bytes 196616 | tf_op jit(solution)/shard_map/ppermute | solution.py:66
  20.9 1.2 copy-start.5
  24.1 98.1 %all-to-all-start = ((bf16[8,128,1664]{2,1,0:T(8,128)(2,1)}), bf16[8,128,1664]{2,1,0:T(8,128)(2,1)S(1)}, u32[]{:S(2)}, u32[]{:S(2)}) async-start(bf16[8,128,1664]{2,1,0:T(8,128)(2,1)} %pad_maximum_fusion), calls=%async_computation | async-start | bytes 6815744 | tf_op jit(solution)/shard_map/all_to_all | solution.py:143
  27.8 52.5 %reduce-scatter.3.cloned.1.call-start = ((), (), s32[]{:S(2)}) async-start(), calls=%async_computation.3 | async-start | bytes 2359296 | tf_op jit(solution)/shard_map/reduce_scatter | solution.py:93
  30.7 132.9 %all-gather.2.cloned.1.call-start = ((), (), s32[]{:S(2)}) async-start(), calls=%async_computation.4 | async-start | bytes 1179648 | tf_op jit(solution)/shard_map/all_gather | solution.py:109
  80.3 10.0 %collective-permute-start.3 = (f32[128,512]{1,0:T(8,128)}, f32[128,512]{1,0:T(8,128)S(1)}, u32[]{:S(2)}, u32[]{:S(2)}) collective-permute-start(f32[128,512]{1,0:T(8,128)} %reduce-scatter.3.cloned.1.call-done), channel_id=1, source_target_pairs={{0,32},{16,48},{32,0},{48,16},{1,33},{17,49},{33,1},{49,17},{2,34}... | collective-permute-start | bytes 786440 | tf_op jit(solution)/shard_map/ppermute | solution.py:81
  83.3 11.1 %collective-permute-start.1 = (f32[32,1024]{1,0:T(8,128)S(1)}, f32[32,1024]{1,0:T(8,128)}, u32[]{:S(2)}, u32[]{:S(2)}) collective-permute-start(f32[32,1024]{1,0:T(8,128)S(1)} %maximum_select_fusion.2), channel_id=1, source_target_pairs={{0,16},{16,0},{32,48},{48,32},{1,17},{17,1},{33,49},{49,33},{2,18}... | collective-permute-start | bytes 393224 | tf_op jit(solution)/shard_map/ppermute | solution.py:66
  91.9 8.8 %collective-permute-start.4 = (f32[128,512]{1,0:T(8,128)}, f32[128,512]{1,0:T(8,128)}, u32[]{:S(2)}, u32[]{:S(2)}) collective-permute-start(f32[128,512]{1,0:T(8,128)} %add.108), channel_id=1, source_target_pairs={{0,16},{16,0},{32,48},{48,32},{1,17},{17,1},{33,49},{49,33},{2,18}... | collective-permute-start | bytes 786440 | tf_op jit(solution)/shard_map/ppermute | solution.py:81
  94.4 26.4 %copy-start.6 = (bf16[1024]{0:T(1024)(128)(2,1)S(1)}, bf16[1024]{0:T(1024)(128)(2,1)}, u32[]{:S(2)}) copy-start(bf16[1024]{0:T(1024)(128)(2,1)} %param.8) | copy-start | bytes 6148
  96.1 13.6 %collective-permute-start.2 = (f32[64,1024]{1,0:T(8,128)}, f32[64,1024]{1,0:T(8,128)}, u32[]{:S(2)}, u32[]{:S(2)}) collective-permute-start(f32[64,1024]{1,0:T(8,128)} %maximum_select_fusion.1), channel_id=1, source_target_pairs={{0,32},{16,48},{32,0},{48,16},{1,33},{17,49},{33,1},{49,17},{2,34}... | collective-permute-start | bytes 786440 | tf_op jit(solution)/shard_map/ppermute | solution.py:66
  102.5 16.3 %collective-permute-start.5 = (f32[128,512]{1,0:T(8,128)}, f32[128,512]{1,0:T(8,128)}, u32[]{:S(2)}, u32[]{:S(2)}) collective-permute-start(f32[128,512]{1,0:T(8,128)} %add.109), channel_id=1, source_target_pairs={{0,8},{8,0},{1,9},{9,1},{2,10},{10,2},{3,11},{11,3},{4,12},{12,4},... | collective-permute-start | bytes 786440 | tf_op jit(solution)/shard_map/ppermute | solution.py:81
  120.7 88.9 %reduce-scatter.5.cloned.1.call-start = ((), (), s32[]{:S(2)}) async-start(), calls=%async_computation.5 | async-start | bytes 2359296 | tf_op jit(solution)/shard_map/reduce_scatter | solution.py:174
  129.3 2.0 copy-start.3
  131.9 35.5 %copy-start = (bf16[1024,1024]{1,0:T(8,128)(2,1)}, bf16[1024,1024]{1,0:T(8,128)(2,1)S(1)}, u32[]{:S(2)}) copy-start(bf16[1024,1024]{1,0:T(8,128)(2,1)S(1)} %fusion.2) | copy-start | bytes 6291460
  174.8 1.6 copy-start.1
  179.6 2.2 %copy-start.4 = (bf16[8,128,1024]{2,1,0:T(8,128)(2,1)S(1)}, bf16[8,128,1024]{2,1,0:T(8,128)(2,1)}, u32[]{:S(2)}) copy-start(bf16[8,128,1024]{2,1,0:T(8,128)(2,1)} %copy-done.3) | copy-start | bytes 6291460
  179.6 2.2 copy-start.7
Sparse Core Ops, SparseCore 0:
  31.4 48.7 reduce-scatter.2
  120.8 42.7 all-gather.1
  167.6 41.9 reduce-scatter.4
